TPU v7x, 256 devices: a whole 4x4x8 slice. The times are simulated.
256 devices in a mesh: turb: 8 (over x, core), age: 8 (over z), span: 4 (over y).
Axes of the slice: x: 4, y: 4, z: 8, core: 2. Of those that a mesh axis runs over, the one named last changes fastest.
Arguments:
- positions: float32 [3, 16, 3, 64, 1024], P(None, 'turb', None, 'span', 'age'), may hold values from -6 to 6
- strengths: float32 [2, 16, 3, 64, 1024], P(None, 'turb', None, 'span', 'age'), may hold values from -12 to 12
- core_radius: float32 [16, 3, 64, 1024], P('turb', None, 'span', 'age'), may hold values from 0.3 to 1.5
- adjoint_seed: float32 [3, 16, 3, 64, 1024], P(None, 'turb', None, 'span', 'age'), may hold values from -6 to 6
- pair_target: int32 [8, 8, 4, 128], P('turb', 'age', 'span'), may hold values from 0 to 95
- pair_owner: int32 [8, 8, 4, 128], P('turb', 'age', 'span'), may hold values from 0 to 63, as said below
- pair_source: int32 [8, 8, 4, 128], P('turb', 'age', 'span'), may hold values from 0 to 95
Outputs:
- advected: float32 [3, 16, 3, 64, 1024], P(None, 'turb', None, 'span', 'age')
- grad_positions: float32 [3, 16, 3, 64, 1024], P(None, 'turb', None, 'span', 'age')
- grad_strengths: float32 [2, 16, 3, 64, 1024], P(None, 'turb', None, 'span', 'age')
Inputs may be any that keep to these rules, and one draw needn't show every extreme that they name: `pair_owner`: at most 4 of the pairs of one device name one owner. One owner, the same for all devices, is named by exactly 4 pairs of every device.
All inputs are finite; a program needn't handle non-finite values.
Results may differ from a plain program's by a relative error of at most 0.0003.
Values sent between devices are 32-bit elements; how exact they have to be, the bound alone decides.
No kernel may reach another device: no remote copies, remote signals or barrier semaphores. Data moves between devices by JAX's collectives and lax.ppermute only.
A program may use at most 64 MiB of HBM per device.

v0:
```python
import math

import jax
import jax.numpy as jnp
from jax import lax
from jax.sharding import PartitionSpec as P

REACH = 8


time_step = 0.5
four_pi = 4.0 * math.pi
batch_rows = 16


def shifted_2(value, axis, steps):
    count = lax.axis_size(axis)
    leading, last = (max(0, -steps), min(count, count - steps))
    return lax.ppermute(value, axis, [(source, source + steps) for source in range(leading, last)])


def windows(payload):
    age_count = payload.shape[-1]
    padded = jnp.pad(payload, ((0, 0), (0, 0), (REACH, REACH)))
    stacked = jnp.stack(
        [
            padded[:, :, REACH + offset : REACH + offset + age_count]
            for offset in range(-REACH, REACH)
        ]
    )
    shifted = (
        jnp.arange(-REACH, REACH, dtype=jnp.int32)[:, None]
        + jnp.arange(age_count, dtype=jnp.int32)[None, :]
    )
    inside = ((shifted >= 0) & (shifted < age_count)).astype(payload.dtype)
    return (stacked, inside)


def induced(targets, payload):
    stacked, inside = windows(payload)
    begins = stacked[:, :, 0:3]
    end_points = jnp.stack([stacked[:, :, 3:6], stacked[:, :, 6:9]])
    gammas = jnp.stack([stacked[:, :, 9], stacked[:, :, 10]]) * inside[None, :, None, :]
    core = jnp.where(inside[:, None, :] > 0, stacked[:, :, 11], 1.0)
    core_sq = core * core
    core_quad = core_sq * core_sq
    from_begin = targets[None] - begins
    from_end = targets[None, None] - end_points
    along = end_points - begins[None]
    near = from_begin[None]
    cross_x = near[..., 1, :] * from_end[..., 2, :] - near[..., 2, :] * from_end[..., 1, :]
    cross_y = near[..., 2, :] * from_end[..., 0, :] - near[..., 0, :] * from_end[..., 2, :]
    cross_z = near[..., 0, :] * from_end[..., 1, :] - near[..., 1, :] * from_end[..., 0, :]
    cross_sq = cross_x * cross_x + cross_y * cross_y + cross_z * cross_z
    length_sq = jnp.sum(along * along, axis=-2) + core_sq
    dist_begin = jnp.sqrt(jnp.sum(from_begin * from_begin, axis=-2) + core_sq)
    dist_end = jnp.sqrt(jnp.sum(from_end * from_end, axis=-2) + core_sq)
    projected = jnp.sum(
        along * (near / dist_begin[None, :, :, None, :] - from_end / dist_end[..., None, :]),
        axis=-2,
    )
    factor = (
        gammas
        * projected
        / (four_pi * jnp.sqrt(cross_sq * cross_sq + core_quad * length_sq * length_sq))
    )
    return jnp.stack(
        [
            jnp.sum(cross_x * factor, axis=(0, 1)),
            jnp.sum(cross_y * factor, axis=(0, 1)),
            jnp.sum(cross_z * factor, axis=(0, 1)),
        ],
        axis=1,
    )


def run_pairs(targets, payload, cotangent):
    number = targets.shape[0]
    age_count = targets.shape[-1]

    def one_batch(operands):
        velocity, pullback = jax.vjp(induced, operands[0], operands[1])
        grad_targets, grad_payload = pullback(operands[2])
        return (velocity, grad_targets, grad_payload)

    shaped = (
        targets.reshape(number // batch_rows, batch_rows, 3, age_count),
        payload.reshape(number // batch_rows, batch_rows, 12, age_count),
        cotangent.reshape(number // batch_rows, batch_rows, 3, age_count),
    )
    velocity, grad_targets, grad_payload = lax.map(one_batch, shaped)
    return (
        velocity.reshape(number, 3, age_count),
        grad_targets.reshape(number, 3, age_count),
        grad_payload.reshape(number, 12, age_count),
    )


def onehot_sum(indices, rows, values):
    selector = (jnp.arange(rows, dtype=jnp.int32)[:, None] == indices[None, :]).astype(jnp.float32)
    flat = values.reshape(values.shape[0], -1)
    summed = jnp.dot(
        selector, flat, precision=lax.Precision.HIGHEST, preferred_element_type=jnp.float32
    )
    return summed.reshape((rows,) + values.shape[1:])


def local(positions, strengths, core_radius, adjoint_seed, pair_target, pair_owner, pair_source):
    shape_here = positions.shape
    station_here = shape_here[3]
    age_here = shape_here[4]
    blocks_here = shape_here[1] * shape_here[2] * station_here
    group_size = lax.axis_size("turb") * lax.axis_size("age")
    pair_count = pair_target.shape[-1]
    capacity = 2 * pair_count // group_size
    target_ids = pair_target.reshape(pair_count)
    owner_ids = pair_owner.reshape(pair_count)
    source_ids = pair_source.reshape(pair_count)
    next_ages = shifted_2(positions[..., 0], "age", -1)
    next_stations = shifted_2(positions[:, :, :, 0, :], "span", -1)
    age_keep = (
        lax.axis_index("age") * age_here + jnp.arange(age_here, dtype=jnp.int32)
        < age_here * lax.axis_size("age") - 1
    ).astype(jnp.float32)
    station_keep = (
        lax.axis_index("span") * station_here + jnp.arange(station_here, dtype=jnp.int32)
        < station_here * lax.axis_size("span") - 1
    ).astype(jnp.float32)

    def build(nodes, after_age, after_station, circulation):
        trail_end = jnp.concatenate([nodes[..., 1:], after_age[..., None]], axis=-1)
        shed_end = jnp.concatenate([nodes[:, :, :, 1:, :], after_station[:, :, :, None, :]], axis=3)
        trail_gamma = circulation[0] * age_keep
        shed_gamma = circulation[1] * station_keep[:, None]
        stacked = jnp.concatenate(
            [nodes, trail_end, shed_end, trail_gamma[None], shed_gamma[None], core_radius[None]],
            axis=0,
        )
        return jnp.transpose(stacked.reshape(12, blocks_here, age_here), (1, 0, 2))

    payload, build_pullback = jax.vjp(build, positions, next_ages, next_stations, strengths)

    def to_rows(array):
        return jnp.transpose(array.reshape(array.shape[0], blocks_here, age_here), (1, 0, 2))

    def from_rows(array):
        return jnp.transpose(array, (1, 0, 2)).reshape(shape_here)

    target_blocks = to_rows(positions)
    seed_blocks = to_rows(adjoint_seed) * time_step
    owner_onehot = (owner_ids[:, None] == jnp.arange(group_size, dtype=jnp.int32)[None, :]).astype(
        jnp.int32
    )
    rank_within = jnp.sum((jnp.cumsum(owner_onehot, axis=0) - owner_onehot) * owner_onehot, axis=1)
    slot_index = owner_ids * capacity + rank_within
    request = (
        jnp.zeros((group_size * capacity,), jnp.int32)
        .at[slot_index]
        .set(source_ids)
        .reshape(group_size, capacity)
    )
    asked = lax.all_to_all(
        request, ("turb", "age"), split_axis=0, concat_axis=0, tiled=True
    ).reshape(group_size * capacity)
    pair_targets = target_blocks[target_ids]
    pair_seed = seed_blocks[target_ids]
    picked = payload[asked].reshape(group_size, capacity, 12, age_here)
    fetched = lax.all_to_all(
        picked, ("turb", "age"), split_axis=0, concat_axis=0, tiled=True
    ).reshape(group_size * capacity, 12, age_here)
    pair_velocity, pair_grad, payload_terms = run_pairs(
        pair_targets, fetched[slot_index], pair_seed
    )
    outgoing = (
        jnp.zeros((group_size * capacity, 12, age_here), jnp.float32)
        .at[slot_index]
        .set(payload_terms)
    )
    returned = lax.all_to_all(
        outgoing.reshape(group_size, capacity, 12, age_here),
        ("turb", "age"),
        split_axis=0,
        concat_axis=0,
        tiled=True,
    )
    payload_grad = onehot_sum(
        asked, blocks_here, returned.reshape(group_size * capacity, 12, age_here)
    )
    velocity = onehot_sum(target_ids, blocks_here, pair_velocity)
    target_grad = onehot_sum(target_ids, blocks_here, pair_grad)
    advected = positions + time_step * from_rows(velocity)
    advected = advected.at[0].add(time_step)
    grad_nodes, grad_after_age, grad_after_station, grad_strengths = build_pullback(payload_grad)
    from_prior_age = shifted_2(grad_after_age, "age", 1)
    from_prior_station = shifted_2(grad_after_station, "span", 1)
    grad_positions = adjoint_seed + grad_nodes + from_rows(target_grad)
    grad_positions = grad_positions.at[..., 0].add(from_prior_age)
    grad_positions = grad_positions.at[:, :, :, 0, :].add(from_prior_station)
    return (advected, grad_positions, grad_strengths)


def solution(mesh):
    placed = (
        P(None, "turb", None, "span", "age"),
        P(None, "turb", None, "span", "age"),
        P("turb", None, "span", "age"),
        P(None, "turb", None, "span", "age"),
        P("turb", "age", "span", None),
        P("turb", "age", "span", None),
        P("turb", "age", "span", None),
    )
    return jax.shard_map(
        local,
        mesh=mesh,
        in_specs=placed,
        out_specs=(
            P(None, "turb", None, "span", "age"),
            P(None, "turb", None, "span", "age"),
            P(None, "turb", None, "span", "age"),
        ),
        check_vma=False,
    )
```

profile of v0, /device:TPU:1, one launch (start us, length us, event | category | flops | bytes accessed | tf_op | source)
XLA Modules:
  0.0 261.0 jit_solution(16885877001061027463)
XLA Ops:
  0.6 0.9 slice.295
  1.5 1.3 collective-permute-start.1
  2.8 1.1 copy.348
  3.9 1.3 collective-permute-start
  6.1 0.8 select_reduce_fusion
  7.6 1.1 scatter_custom_fusion
  9.5 14.2 %all-to-all-start = ((s32[64,1,4]{2,1,0:T(1,128)}), s32[64,1,4]{2,1,0:T(1,128)S(1)}, u32[]{:S(2)}, u32[]{:S(2)}) async-start(s32[64,1,4]{2,1,0:T(1,128)} %bitcast.110), calls=%async_computation | async-start | bytes 65536 | tf_op jit(solution)/shard_map/all_to_all | solution.py:162
  23.7 0.9 slice_multiply_fusion
  24.6 0.9 slice.294
  25.5 1.0 slice.292
  26.5 1.0 copy.346
  28.1 4.7 %all-to-all-done = s32[64,1,4]{2,1,0:T(1,128)S(1)} async-done(((s32[64,1,4]{2,1,0:T(1,128)}), s32[64,1,4]{2,1,0:T(1,128)S(1)}, u32[]{:S(2)}, u32[]{:S(2)}) %all-to-all-start) | async-done | bytes 1056 | tf_op jit(solution)/shard_map/all_to_all | solution.py:162
  34.4 1.2 concatenate.57
  35.6 1.0 gather_fusion.1
  36.6 1.9 copy.355
  38.5 5.8 %all-to-all-start.1 = ((f32[64,4,12,128]{3,1,2,0:T(4,128)}), f32[64,4,12,128]{3,1,2,0:T(4,128)S(1)}, u32[]{:S(2)}, u32[]{:S(2)}) async-start(f32[64,4,12,128]{3,1,2,0:T(4,128)} %copy.355), calls=%async_computation.1 | async-start | bytes 3145728 | tf_op jit(solution)/shard_map/all_to_all | solution.py:168
  46.1 37.5 %all-to-all-done.1 = f32[64,4,12,128]{3,1,2,0:T(4,128)S(1)} async-done(((f32[64,4,12,128]{3,1,2,0:T(4,128)}), f32[64,4,12,128]{3,1,2,0:T(4,128)S(1)}, u32[]{:S(2)}, u32[]{:S(2)}) %all-to-all-start.1) | async-done | bytes 1572896 | tf_op jit(solution)/shard_map/all_to_all | solution.py:168
  83.6 1.6 copy.356
  85.2 2.2 gather_fusion.2
  87.7 106.1 %while.19 = (s32[]{:T(128)}, f32[8,16,3,128]{3,2,1,0:T(4,128)S(1)}, f32[8,16,3,128]{3,1,2,0:T(8,128)}, f32[8,16,12,128]{3,1,0,2:T(8,128)}, f32[8,16,3,128]{3,1,2...) while((s32[]{:T(128)}, f32[8,16,3,128]{3,2,1,0:T(4,128)S(1)}, ...), condition=%wide.region_26.27_spmd, body=%wide.region_3.26_spmd.sunk | while | flops 23116816 | bytes 77752920 | solution.py:91
  92.3 0.8 slice_bitcast_fusion.39
  93.2 1.2 fusion.171
  95.6 1.0 bitcast_multiply_fusion.20
  96.6 1.1 multiply_bitcast_fusion.7
  100.0 0.9 fusion.175
  105.6 0.8 slice_bitcast_fusion.39
  106.4 1.2 fusion.171
  108.9 1.0 bitcast_multiply_fusion.20
  109.8 1.1 multiply_bitcast_fusion.7
  113.3 0.9 fusion.175
  118.9 0.8 slice_bitcast_fusion.39
  119.7 1.2 fusion.171
  122.1 1.0 bitcast_multiply_fusion.20
  123.1 1.1 multiply_bitcast_fusion.7
  126.6 0.9 fusion.175
  132.1 0.8 slice_bitcast_fusion.39
  132.9 1.2 fusion.171
  135.4 1.0 bitcast_multiply_fusion.20
  136.4 1.1 multiply_bitcast_fusion.7
  139.8 0.9 fusion.175
  146.2 1.2 fusion.171
  148.6 1.0 bitcast_multiply_fusion.20
  149.6 1.1 multiply_bitcast_fusion.7
  153.0 0.9 fusion.175
  159.4 1.2 fusion.171
  161.9 1.0 bitcast_multiply_fusion.20
  162.8 1.1 multiply_bitcast_fusion.7
  166.3 0.9 fusion.175
  172.7 1.2 fusion.171
  175.2 1.0 bitcast_multiply_fusion.20
  176.1 1.1 multiply_bitcast_fusion.7
  179.6 0.9 fusion.175
  186.0 1.2 fusion.171
  188.4 1.0 bitcast_multiply_fusion.20
  189.4 1.1 multiply_bitcast_fusion.7
  192.9 0.9 fusion.175
  194.5 1.6 copy.365
  196.3 4.4 %scatter_fusion = f32[256,12,128]{2,1,0:T(8,128)S(1)} fusion(f32[256,12,128]{2,1,0:T(8,128)S(1)} %broadcast_in_dim.147, s32[128]{0:T(128)S(1)} %copy-done.30, f32[128,12,128]{2,1,0:T(8,128)S(1)} %copy.365), kind=kCustom, calls=%fused_computation.5 | custom fusion | bytes 2359808 | tf_op jit(solution)/shard_map/scatter | solution.py:177
  200.7 1.9 copy.367
  202.6 7.0 %all-to-all-start.2 = ((f32[64,4,12,128]{3,1,2,0:T(4,128)}), f32[64,4,12,128]{3,1,2,0:T(4,128)S(1)}, u32[]{:S(2)}, u32[]{:S(2)}) async-start(f32[64,4,12,128]{3,1,2,0:T(4,128)} %copy.367), calls=%async_computation.2 | async-start | bytes 3145728 | tf_op jit(solution)/shard_map/all_to_all | solution.py:179
  211.0 37.8 %all-to-all-done.2 = f32[64,4,12,128]{3,1,2,0:T(4,128)S(1)} async-done(((f32[64,4,12,128]{3,1,2,0:T(4,128)}), f32[64,4,12,128]{3,1,2,0:T(4,128)S(1)}, u32[]{:S(2)}, u32[]{:S(2)}) %all-to-all-start.2) | async-done | bytes 1572896 | tf_op jit(solution)/shard_map/all_to_all | solution.py:179
  250.3 0.9 convolution_bitcast_fusion
  251.3 4.3 %collective-permute-start.3 = (f32[3,2,3,128]{3,1,2,0:T(2,128)S(1)}, f32[3,2,3,128]{3,1,2,0:T(2,128)S(1)}, u32[]{:S(2)}, u32[]{:S(2)}) collective-permute-start(f32[3,2,3,128]{3,1,2,0:T(2,128)S(1)} %bitcast.599), channel_id=1, source_target_pairs={{0,1},{1,2},{2,3},{4,5},{5,6},{6,7},{8,9},{9,10},{10,11},{12,13},{... | collective-permute-start | bytes 27656 | tf_op jit(solution)/shard_map/ppermute | solution.py:19
  255.9 3.2 %collective-permute-start.2 = (f32[3,2,3,16]{3,1,2,0:T(2,128)S(1)}, f32[3,2,3,16]{3,1,2,0:T(2,128)S(1)}, u32[]{:S(2)}, u32[]{:S(2)}) collective-permute-start(f32[3,2,3,16]{3,1,2,0:T(2,128)S(1)} %bitcast.594), channel_id=1, source_target_pairs={{0,4},{4,8},{8,12},{12,16},{16,20},{20,24},{24,28},{1,5},{5,9},{9,... | collective-permute-start | bytes 3464 | tf_op jit(solution)/shard_map/ppermute | solution.py:19
  (699 shorter events, 77.7 us)
Async XLA Ops:
  1.5 32.6 %collective-permute-start.1 = (f32[3,2,3,128]{3,1,2,0:T(2,128)S(1)}, f32[3,2,3,128]{3,1,2,0:T(2,128)S(1)}, u32[]{:S(2)}, u32[]{:S(2)}) collective-permute-start(f32[3,2,3,128]{3,1,2,0:T(2,128)S(1)} %bitcast.597), channel_id=1, source_target_pairs={{1,0},{2,1},{3,2},{5,4},{6,5},{7,6},{9,8},{10,9},{11,10},{13,12},{... | collective-permute-start | bytes 27656 | tf_op jit(solution)/shard_map/ppermute | solution.py:19
  3.9 23.8 %collective-permute-start = (f32[3,2,3,16]{3,1,2,0:T(2,128)S(1)}, f32[3,2,3,16]{3,1,2,0:T(2,128)S(1)}, u32[]{:S(2)}, u32[]{:S(2)}) collective-permute-start(f32[3,2,3,16]{3,1,2,0:T(2,128)S(1)} %bitcast.593), channel_id=1, source_target_pairs={{4,0},{8,4},{12,8},{16,12},{20,16},{24,20},{28,24},{5,1},{9,5},{13... | collective-permute-start | bytes 3464 | tf_op jit(solution)/shard_map/ppermute | solution.py:19
  7.6 38.4 %copy-start.29 = (s32[128]{0:T(128)}, s32[128]{0:T(128)S(1)}, u32[]{:S(2)}) copy-start(s32[128]{0:T(128)S(1)} %fusion.99) | copy-start | bytes 1540
  9.5 23.3 %all-to-all-start = ((s32[64,1,4]{2,1,0:T(1,128)}), s32[64,1,4]{2,1,0:T(1,128)S(1)}, u32[]{:S(2)}, u32[]{:S(2)}) async-start(s32[64,1,4]{2,1,0:T(1,128)} %bitcast.110), calls=%async_computation | async-start | bytes 65536 | tf_op jit(solution)/shard_map/all_to_all | solution.py:162
  23.6 10.7 %copy-start.22 = (f32[2,3,16,128]{3,2,1,0:T(8,128)S(1)}, f32[2,3,16,128]{3,2,1,0:T(8,128)}, u32[]{:S(2)}) copy-start(f32[2,3,16,128]{3,2,1,0:T(8,128)} %param.17) | copy-start | bytes 147460
  23.7 4.3 %copy-start.25 = (f32[128]{0:T(128)}, f32[128]{0:T(128)S(1)}, u32[]{:S(2)}) copy-start(f32[128]{0:T(128)S(1)} %compare_convert_fusion.1) | copy-start | bytes 1540
  23.7 4.3 %copy-start.27 = (f32[16]{0:T(128)}, f32[16]{0:T(128)S(1)}, u32[]{:S(2)}) copy-start(f32[16]{0:T(128)S(1)} %compare_convert_fusion) | copy-start | bytes 196
  32.8 2.8 %copy-start.14 = (s32[64,1,4]{2,1,0:T(1,128)}, s32[64,1,4]{2,1,0:T(1,128)S(1)}, u32[]{:S(2)}) copy-start(s32[64,1,4]{2,1,0:T(1,128)S(1)} %all-to-all-done) | copy-start | bytes 3076
  38.5 5.8 %copy-start.8 = (f32[3,2,3,16,128]{4,3,2,1,0:T(8,128)S(1)}, f32[3,2,3,16,128]{4,3,2,1,0:T(8,128)}, u32[]{:S(2)}) copy-start(f32[3,2,3,16,128]{4,3,2,1,0:T(8,128)} %param.18) | copy-start | bytes 442372
  38.5 6.0 %copy-start.23 = (s32[1,1,1,128]{3,2,1,0:T(1,128)S(1)}, s32[1,1,1,128]{3,2,1,0:T(1,128)}, u32[]{:S(2)}) copy-start(s32[1,1,1,128]{3,2,1,0:T(1,128)} %param.19) | copy-start | bytes 1540
  38.5 45.1 %all-to-all-start.1 = ((f32[64,4,12,128]{3,1,2,0:T(4,128)}), f32[64,4,12,128]{3,1,2,0:T(4,128)S(1)}, u32[]{:S(2)}, u32[]{:S(2)}) async-start(f32[64,4,12,128]{3,1,2,0:T(4,128)} %copy.355), calls=%async_computation.1 | async-start | bytes 3145728 | tf_op jit(solution)/shard_map/all_to_all | solution.py:168
  87.7 1.5 copy-start.3
  87.7 1.5 copy-start.10
  87.7 1.5 copy-start.12
  99.4 1.5 copy-start.4
  99.4 1.5 copy-start.11
  99.4 1.5 copy-start.13
  101.0 1.5 copy-start.3
  101.0 1.5 copy-start.10
  101.0 1.5 copy-start.12
  112.7 1.5 copy-start.4
  112.7 1.5 copy-start.11
  112.7 1.5 copy-start.13
  114.2 1.5 copy-start.3
  114.2 1.5 copy-start.10
  114.3 1.5 copy-start.12
  125.9 1.5 copy-start.4
  127.5 1.5 copy-start.3
  127.5 1.5 copy-start.10
  127.5 1.5 copy-start.12
  139.2 1.5 copy-start.4
  140.7 1.5 copy-start.3
  140.7 1.5 copy-start.10
  140.7 1.5 copy-start.12
  152.4 1.5 copy-start.4
  152.4 1.5 copy-start.11
  152.4 1.5 copy-start.13
  154.0 1.5 copy-start.3
  154.0 1.5 copy-start.10
  154.0 1.5 copy-start.12
  165.7 1.6 copy-start.4
  165.7 1.6 copy-start.11
  165.7 1.6 copy-start.13
  165.7 1.5 copy-start.18
  167.3 1.5 copy-start.3
  179.0 1.5 copy-start.4
  179.0 1.5 copy-start.11
  179.0 1.5 copy-start.13
  179.0 1.5 copy-start.18
  192.3 1.5 copy-start.4
  192.3 1.5 copy-start.11
  192.3 1.5 copy-start.13
  194.5 1.8 copy-start.30
  202.6 7.0 %copy-start.15 = (s32[64,1,4]{2,1,0:T(1,128)S(1)}, s32[64,1,4]{2,1,0:T(1,128)}, u32[]{:S(2)}) copy-start(s32[64,1,4]{2,1,0:T(1,128)} %copy-done.14) | copy-start | bytes 3076
  202.6 7.1 %copy-start.20 = (f32[8,16,3,128]{3,2,1,0:T(4,128)S(1)}, f32[8,16,3,128]{3,2,1,0:T(4,128)}, u32[]{:S(2)}) copy-start(f32[8,16,3,128]{3,2,1,0:T(4,128)} %copy-done.19) | copy-start | bytes 589828
  202.6 7.3 %copy-start.24 = (s32[1,1,1,128]{3,2,1,0:T(1,128)S(1)}, s32[1,1,1,128]{3,2,1,0:T(1,128)}, u32[]{:S(2)}) copy-start(s32[1,1,1,128]{3,2,1,0:T(1,128)} %param.19) | copy-start | bytes 1540
  202.6 7.6 %copy-start.5 = (f32[3,2,3,16,128]{4,3,2,1,0:T(8,128)S(1)}, f32[3,2,3,16,128]{4,3,2,1,0:T(8,128)}, u32[]{:S(2)}) copy-start(f32[3,2,3,16,128]{4,3,2,1,0:T(8,128)} %param.15) | copy-start | bytes 442372
  202.6 46.3 %all-to-all-start.2 = ((f32[64,4,12,128]{3,1,2,0:T(4,128)}), f32[64,4,12,128]{3,1,2,0:T(4,128)S(1)}, u32[]{:S(2)}, u32[]{:S(2)}) async-start(f32[64,4,12,128]{3,1,2,0:T(4,128)} %copy.367), calls=%async_computation.2 | async-start | bytes 3145728 | tf_op jit(solution)/shard_map/all_to_all | solution.py:179
  210.8 38.4 %copy-start.16 = (f32[3,2,3,16,128]{4,3,2,1,0:T(8,128)}, f32[3,2,3,16,128]{4,3,2,1,0:T(8,128)S(1)}, u32[]{:S(2)}) copy-start(f32[3,2,3,16,128]{4,3,2,1,0:T(8,128)S(1)} %fusion.90) | copy-start | bytes 442372
  250.3 8.8 %copy-start.26 = (f32[128]{0:T(128)S(1)}, f32[128]{0:T(128)}, u32[]{:S(2)}) copy-start(f32[128]{0:T(128)} %copy-done.25) | copy-start | bytes 1540
  250.3 8.8 %copy-start.28 = (f32[16]{0:T(128)S(1)}, f32[16]{0:T(128)}, u32[]{:S(2)}) copy-start(f32[16]{0:T(128)} %copy-done.27) | copy-start | bytes 196
  250.3 8.9 %copy-start.9 = (f32[3,2,3,16,128]{4,3,2,1,0:T(8,128)S(1)}, f32[3,2,3,16,128]{4,3,2,1,0:T(8,128)}, u32[]{:S(2)}) copy-start(f32[3,2,3,16,128]{4,3,2,1,0:T(8,128)} %param.18) | copy-start | bytes 442372
  251.3 8.9 %collective-permute-start.3 = (f32[3,2,3,128]{3,1,2,0:T(2,128)S(1)}, f32[3,2,3,128]{3,1,2,0:T(2,128)S(1)}, u32[]{:S(2)}, u32[]{:S(2)}) collective-permute-start(f32[3,2,3,128]{3,1,2,0:T(2,128)S(1)} %bitcast.599), channel_id=1, source_target_pairs={{0,1},{1,2},{2,3},{4,5},{5,6},{6,7},{8,9},{9,10},{10,11},{12,13},{... | collective-permute-start | bytes 27656 | tf_op jit(solution)/shard_map/ppermute | solution.py:19
  255.9 4.0 %collective-permute-start.2 = (f32[3,2,3,16]{3,1,2,0:T(2,128)S(1)}, f32[3,2,3,16]{3,1,2,0:T(2,128)S(1)}, u32[]{:S(2)}, u32[]{:S(2)}) collective-permute-start(f32[3,2,3,16]{3,1,2,0:T(2,128)S(1)} %bitcast.594), channel_id=1, source_target_pairs={{0,4},{4,8},{8,12},{12,16},{16,20},{20,24},{24,28},{1,5},{5,9},{9,... | collective-permute-start | bytes 3464 | tf_op jit(solution)/shard_map/ppermute | solution.py:19
  (58 other events, 66.2 us)
where the time goes:
time: 264 us; the launch traced here: 261 us
  other arithmetic  83.6 us (32%)
  waiting for transfers between devices  80 us (30%)
  local copies, waits for them, and re-layouts  53.8 us (20%)
  starting transfers between devices  37 us (14%)
  loops' own time  3.86 us (1%)
    all_to_all x1, waiting for transfers between devices, local(): lax.all_to_all(outgoing.reshape(group_size, capacity, 12, age_here), ('tu...  37.8 us
    all_to_all x1, waiting for transfers between devices, local(): lax.all_to_all(picked, ('turb', 'age'), split_axis=0, concat_axis=0, tile...  37.5 us
    while x328, local copies, waits for them, and re-layouts  14.9 us
    all_to_all x1, starting transfers between devices, local(): lax.all_to_all(request, ('turb', 'age'), split_axis=0, concat_axis=0, til...  14.2 us
    dynamic_update_slice x24, other arithmetic, run_pairs(): velocity, grad_targets, grad_payload = lax.map(one_batch, shaped)  12.5 us
    ppermute x4, starting transfers between devices, shifted_2(): lax.ppermute(value, axis, [(source, source + steps) for source in range(l...  10 us
    mul x8, other arithmetic, induced(): near[..., 1, :] * from_end[..., 0, :]  9.9 us
    while x24, other arithmetic  8.93 us
  transfers between devices with their start and end apart: 7, of which 3 were waited for; matrix products, arithmetic and copies ran while one was open for 6% of the time, Pallas kernels for 0%

commit v1 on v0

--- a/solution.py
+++ b/solution.py
@@ -4,6 +4,8 @@
 import jax.numpy as jnp
 from jax import lax
 from jax.sharding import PartitionSpec as P
+from jax.experimental import pallas as pl
+from jax.experimental.pallas import tpu as pltpu
 
 REACH = 8
 
@@ -74,25 +76,111 @@
     )
 
 
+GROUP_PAIRS = 8
+
+
+def segment_pair(target, begin, trail_end, shed_end, trail_gamma, shed_gamma, core, inside):
+    core_sq = core * core
+    core_quad = core_sq * core_sq
+    near = [target[i] - begin[i] for i in range(3)]
+    begin_sq = near[0] * near[0] + near[1] * near[1] + near[2] * near[2]
+    dist_begin = jnp.sqrt(begin_sq + core_sq)
+    total = [0.0, 0.0, 0.0]
+    for end_point, gamma in ((trail_end, trail_gamma), (shed_end, shed_gamma)):
+        far = [target[i] - end_point[i] for i in range(3)]
+        along = [end_point[i] - begin[i] for i in range(3)]
+        cross_x = near[1] * far[2] - near[2] * far[1]
+        cross_y = near[2] * far[0] - near[0] * far[2]
+        cross_z = near[0] * far[1] - near[1] * far[0]
+        cross_sq = cross_x * cross_x + cross_y * cross_y + cross_z * cross_z
+        length_sq = along[0] * along[0] + along[1] * along[1] + along[2] * along[2] + core_sq
+        dist_end = jnp.sqrt(far[0] * far[0] + far[1] * far[1] + far[2] * far[2] + core_sq)
+        projected = (
+            along[0] * (near[0] / dist_begin - far[0] / dist_end)
+            + along[1] * (near[1] / dist_begin - far[1] / dist_end)
+            + along[2] * (near[2] / dist_begin - far[2] / dist_end)
+        )
+        masked = jnp.where(inside, gamma, 0.0)
+        factor = (
+            masked
+            * projected
+            / (four_pi * jnp.sqrt(cross_sq * cross_sq + core_quad * length_sq * length_sq))
+        )
+        total = [total[0] + cross_x * factor, total[1] + cross_y * factor, total[2] + cross_z * factor]
+    return tuple(total)
+
+
+def pair_kernel(t_ref, s_ref, c_ref, v_ref, gt_ref, gs_ref):
+    shape = t_ref.shape[1:]
+    age_count = shape[-1]
+    lane = lax.broadcasted_iota(jnp.int32, shape, 1)
+    target = tuple(t_ref[i] for i in range(3))
+    cotangent = tuple(c_ref[i] for i in range(3))
+    rows = [s_ref[i] for i in range(12)]
+    zero = jnp.zeros(shape, jnp.float32)
+    velocity = [zero] * 3
+    grad_target = [zero] * 3
+    grad_rows = [zero] * 11
+    for offset in range(-REACH, REACH):
+        amount = (-offset) % age_count
+        moved = [pltpu.roll(r, amount, 1) if amount else r for r in rows]
+        inside = (lane + offset >= 0) & (lane + offset < age_count)
+        core = moved[11]
+
+        def field(t, b, te, se, tg, sg):
+            return segment_pair(t, b, te, se, tg, sg, core, inside)
+
+        u, pullback = jax.vjp(
+            field,
+            target,
+            tuple(moved[0:3]),
+            tuple(moved[3:6]),
+            tuple(moved[6:9]),
+            moved[9],
+            moved[10],
+        )
+        d_t, d_b, d_te, d_se, d_tg, d_sg = pullback(cotangent)
+        grads = list(d_b) + list(d_te) + list(d_se) + [d_tg, d_sg]
+        back = (offset) % age_count
+        for i in range(3):
+            velocity[i] = velocity[i] + u[i]
+            grad_target[i] = grad_target[i] + d_t[i]
+        for i in range(11):
+            g = pltpu.roll(grads[i], back, 1) if back else grads[i]
+            grad_rows[i] = grad_rows[i] + g
+    for i in range(3):
+        v_ref[i] = velocity[i]
+        gt_ref[i] = grad_target[i]
+    for i in range(11):
+        gs_ref[i] = grad_rows[i]
+
+
 def run_pairs(targets, payload, cotangent):
     number = targets.shape[0]
     age_count = targets.shape[-1]
-
-    def one_batch(operands):
-        velocity, pullback = jax.vjp(induced, operands[0], operands[1])
-        grad_targets, grad_payload = pullback(operands[2])
-        return (velocity, grad_targets, grad_payload)
-
-    shaped = (
-        targets.reshape(number // batch_rows, batch_rows, 3, age_count),
-        payload.reshape(number // batch_rows, batch_rows, 12, age_count),
-        cotangent.reshape(number // batch_rows, batch_rows, 3, age_count),
-    )
-    velocity, grad_targets, grad_payload = lax.map(one_batch, shaped)
+    step = GROUP_PAIRS
+
+    def spec(rows):
+        return pl.BlockSpec((rows, step, age_count), lambda i: (0, i, 0))
+
+    t_rows = jnp.transpose(targets, (1, 0, 2))
+    s_rows = jnp.transpose(payload, (1, 0, 2))
+    c_rows = jnp.transpose(cotangent, (1, 0, 2))
+    velocity, grad_targets, grad_payload = pl.pallas_call(
+        pair_kernel,
+        grid=(number // step,),
+        in_specs=[spec(3), spec(12), spec(3)],
+        out_specs=[spec(3), spec(3), spec(11)],
+        out_shape=[
+            jax.ShapeDtypeStruct((3, number, age_count), jnp.float32),
+            jax.ShapeDtypeStruct((3, number, age_count), jnp.float32),
+            jax.ShapeDtypeStruct((11, number, age_count), jnp.float32),
+        ],
+    )(t_rows, s_rows, c_rows)
     return (
-        velocity.reshape(number, 3, age_count),
-        grad_targets.reshape(number, 3, age_count),
-        grad_payload.reshape(number, 12, age_count),
+        jnp.transpose(velocity, (1, 0, 2)),
+        jnp.transpose(grad_targets, (1, 0, 2)),
+        jnp.transpose(grad_payload, (1, 0, 2)),
     )
 
 
@@ -171,6 +259,9 @@
     pair_velocity, pair_grad, payload_terms = run_pairs(
         pair_targets, fetched[slot_index], pair_seed
     )
+    payload_terms = jnp.concatenate(
+        [payload_terms, jnp.zeros_like(payload_terms[:, :1])], axis=1
+    )
     outgoing = (
         jnp.zeros((group_size * capacity, 12, age_here), jnp.float32)
         .at[slot_index]

time: 264 us -> 184 us (0.70)
  other arithmetic: 83.6 us -> 5.18 us
  Pallas kernels: 0 us -> 27.2 us
  local copies, waits for them, and re-layouts: 53.8 us -> 30.4 us
  loops' own time: 3.86 us -> 0 us
    pallas_call x0 -> x1, Pallas kernels: none -> 27.2 us  [run_pairs(): pl.pallas_call(pair_kernel, grid=(number // step,), in_specs=[spec(3), sp...]
    reduce_sum x72 -> x0, other arithmetic: 18.7 us -> none  [the longest x8 5.01 us: induced(): from_begin = targets[None] - begins]
    mul x32 -> x1, other arithmetic: 18.1 us -> 0.01 us  [build(): trail_gamma = circulation[0] * age_keep]
    while x332 -> x0, local copies, waits for them, and re-layouts: 15.3 us -> none
    dynamic_update_slice x24 -> x0, other arithmetic: 12.5 us -> none  [run_pairs(): velocity, grad_targets, grad_payload = lax.map(one_batch, shaped)]
    while x24 -> x0, other arithmetic: 8.93 us -> none
    add_any x32 -> x0, other arithmetic: 8.67 us -> none  [the longest x8 4.59 us: windows(): padded[:, :, REACH + offset:REACH + offset + age_count]]
    another operation x41 -> x1, local copies, waits for them, and re-layouts: 8.49 us -> 0.18 us  [the longest x8 6.35 us: induced(): stacked[:, :, 9]]
  transfers between devices with their start and end apart: 7 -> 7, of which waited for: 3 -> 3; matrix products, arithmetic and copies ran while one was open for 6% -> 8% of each run, Pallas kernels for 0% -> 0%
where the time goes in v1:
time: 184 us; the launch traced here: 182 us
  waiting for transfers between devices  79.9 us (43%)
  starting transfers between devices  36.9 us (20%)
  local copies, waits for them, and re-layouts  30.4 us (17%)
  Pallas kernels  27.2 us (15%)
  other arithmetic  5.18 us (3%)
    all_to_all x1, waiting for transfers between devices, local(): lax.all_to_all(outgoing.reshape(group_size, capacity, 12, age_here), ('tu...  38.3 us
    all_to_all x1, waiting for transfers between devices, local(): lax.all_to_all(picked, ('turb', 'age'), split_axis=0, concat_axis=0, tile...  36.8 us
    pallas_call x1, Pallas kernels, run_pairs(): pl.pallas_call(pair_kernel, grid=(number // step,), in_specs=[spec(3), sp...  27.2 us
    all_to_all x1, starting transfers between devices, local(): lax.all_to_all(request, ('turb', 'age'), split_axis=0, concat_axis=0, til...  14.2 us
    ppermute x4, starting transfers between devices, shifted_2(): lax.ppermute(value, axis, [(source, source + steps) for source in range(l...  10 us
    all_to_all x1, starting transfers between devices, local(): lax.all_to_all(outgoing.reshape(group_size, capacity, 12, age_here), ('tu...  6.97 us
    all_to_all x1, starting transfers between devices, local(): lax.all_to_all(picked, ('turb', 'age'), split_axis=0, concat_axis=0, tile...  5.73 us
    all_to_all x1, waiting for transfers between devices, local(): lax.all_to_all(request, ('turb', 'age'), split_axis=0, concat_axis=0, til...  4.7 us
  transfers between devices with their start and end apart: 7, of which 3 were waited for; matrix products, arithmetic and copies ran while one was open for 8% of the time, Pallas kernels for 0%

profile of v1, /device:TPU:1, one launch (start us, length us, event | category | flops | bytes accessed | tf_op | source)
XLA Modules:
  0.0 182.2 jit_solution(1447280751862078546)
XLA Ops:
  0.6 0.9 slice.122
  1.6 1.3 collective-permute-start.1
  2.9 1.1 copy.128
  3.9 1.3 collective-permute-start
  5.2 0.7 fusion.5
  6.0 0.2 reduce_window_sum.11
  6.2 0.8 select_reduce_fusion
  7.0 0.7 fusion.14
  7.7 1.1 scatter_custom_fusion
  8.8 0.7 all_to_all.12
  9.5 14.2 %all-to-all-start = ((s32[64,1,4]{2,1,0:T(1,128)}), s32[64,1,4]{2,1,0:T(1,128)S(1)}, u32[]{:S(2)}, u32[]{:S(2)}) async-start(s32[64,1,4]{2,1,0:T(1,128)} %bitcast.21), calls=%async_computation | async-start | bytes 65536 | tf_op jit(solution)/shard_map/all_to_all | solution.py:250
  23.7 0.9 slice_multiply_fusion
  24.6 0.9 slice.121
  25.5 1.0 slice.119
  26.5 1.0 copy.125
  27.5 0.1 copy.127
  27.7 0.1 concatenate.33
  27.8 0.2 copy.130
  27.9 0.2 pad_maximum_fusion
  28.1 4.7 %all-to-all-done = s32[64,1,4]{2,1,0:T(1,128)S(1)} async-done(((s32[64,1,4]{2,1,0:T(1,128)}), s32[64,1,4]{2,1,0:T(1,128)S(1)}, u32[]{:S(2)}, u32[]{:S(2)}) %all-to-all-start) | async-done | bytes 1056 | tf_op jit(solution)/shard_map/all_to_all | solution.py:250
  32.8 0.5 broadcast.247
  33.3 0.7 reduce.11
  34.1 0.1 reshape.314
  34.2 0.1 copy.133
  34.4 1.2 concatenate.40
  35.6 1.0 gather_fusion.1
  36.6 1.9 %copy.135 = f32[64,4,12,128]{3,1,2,0:T(4,128)} copy(f32[64,4,12,128]{3,2,1,0:T(8,128)S(1)} %bitcast.105) | data formatting | bytes 3145728 | tf_op jit(solution)/shard_map/reshape | solution.py:255
  38.5 5.7 %all-to-all-start.1 = ((f32[64,4,12,128]{3,1,2,0:T(4,128)}), f32[64,4,12,128]{3,1,2,0:T(4,128)S(1)}, u32[]{:S(2)}, u32[]{:S(2)}) async-start(f32[64,4,12,128]{3,1,2,0:T(4,128)} %copy.135), calls=%async_computation.1 | async-start | bytes 3145728 | tf_op jit(solution)/shard_map/all_to_all | solution.py:256
  44.3 0.1 copy.138
  44.4 0.8 gather_fusion.3
  45.2 0.8 gather_fusion
  45.9 0.8 copy_bitcast_fusion.1
  46.7 36.8 %all-to-all-done.1 = f32[64,4,12,128]{3,1,2,0:T(4,128)S(1)} async-done(((f32[64,4,12,128]{3,1,2,0:T(4,128)}), f32[64,4,12,128]{3,1,2,0:T(4,128)S(1)}, u32[]{:S(2)}, u32[]{:S(2)}) %all-to-all-start.1) | async-done | bytes 1572896 | tf_op jit(solution)/shard_map/all_to_all | solution.py:256
  83.6 1.6 copy.136
  85.1 2.2 %gather_fusion.2 = f32[128,12,128]{2,1,0:T(8,128)S(1)} fusion(f32[256,12,128]{2,1,0:T(8,128)} %bitcast.109, s32[1024]{0:T(1024)S(1)} %pad_clamp_fusion), kind=kCustom, calls=%fused_computation.2 | custom fusion | bytes 1573376 | tf_op jit(solution)/shard_map/gather | solution.py:260
  87.4 1.1 copy.163
  88.5 27.2 %shard_map.94 = (f32[3,128,128]{2,1,0:T(8,128)}, f32[3,128,128]{2,1,0:T(8,128)}, f32[11,128,128]{2,1,0:T(8,128)}) custom-call(f32[3,128,128]{2,1,0:T(8,128)} %get-tuple-element.62.t_ref, f32[12,128,128]{2,1,0:T(8,128)} %bitcast.111, f32[3,128,128]{2,1,0:T(8,128)} %get-tuple-element.61.c_ref), custom_call_target="tpu_custom_call" | custom-call | tf_op jit(solution)/shard_map/pallas_call | solution.py:169
  115.7 1.5 copy.153
  117.3 0.1 concatenate.41.clone
  117.4 0.1 broadcast_in_dim.5
  117.5 4.4 %scatter_fusion = f32[256,12,128]{2,1,0:T(8,128)S(1)} fusion(f32[256,12,128]{2,1,0:T(8,128)S(1)} %broadcast_in_dim.5, s32[128]{0:T(128)S(1)} %fusion.14, f32[128,12,128]{2,1,0:T(8,128)S(1)} %concatenate.41.clone), kind=kCustom, calls=%fused_computation.5 | custom fusion | bytes 2359808 | tf_op jit(solution)/shard_map/scatter | solution.py:268
  121.9 1.9 %copy.143 = f32[64,4,12,128]{3,1,2,0:T(4,128)} copy(f32[64,4,12,128]{3,2,1,0:T(8,128)S(1)} %bitcast.103) | data formatting | bytes 3145728 | tf_op jit(solution)/shard_map/reshape | solution.py:271
  123.8 7.0 %all-to-all-start.2 = ((f32[64,4,12,128]{3,1,2,0:T(4,128)}), f32[64,4,12,128]{3,1,2,0:T(4,128)S(1)}, u32[]{:S(2)}, u32[]{:S(2)}) async-start(f32[64,4,12,128]{3,1,2,0:T(4,128)} %copy.143), calls=%async_computation.2 | async-start | bytes 3145728 | tf_op jit(solution)/shard_map/all_to_all | solution.py:270
  130.8 0.1 eq.61
  130.9 0.1 copy.140
  131.0 0.3 convolution_multiply_fusion
  131.3 0.1 copy.146
  131.5 0.3 fusion
  131.8 38.3 %all-to-all-done.2 = f32[64,4,12,128]{3,1,2,0:T(4,128)S(1)} async-done(((f32[64,4,12,128]{3,1,2,0:T(4,128)}), f32[64,4,12,128]{3,1,2,0:T(4,128)S(1)}, u32[]{:S(2)}, u32[]{:S(2)}) %all-to-all-start.2) | async-done | bytes 1572896 | tf_op jit(solution)/shard_map/all_to_all | solution.py:270
  170.1 0.2 copy.144
  170.3 0.7 copy.162
  171.0 0.5 copy.145
  171.5 0.9 convolution_bitcast_fusion
  172.5 0.1 broadcast_multiply_fusion.1
  172.6 4.3 %collective-permute-start.3 = (f32[3,2,3,128]{3,1,2,0:T(2,128)S(1)}, f32[3,2,3,128]{3,1,2,0:T(2,128)S(1)}, u32[]{:S(2)}, u32[]{:S(2)}) collective-permute-start(f32[3,2,3,128]{3,1,2,0:T(2,128)S(1)} %bitcast.139), channel_id=1, source_target_pairs={{0,1},{1,2},{2,3},{4,5},{5,6},{6,7},{8,9},{9,10},{10,11},{12,13},{... | collective-permute-start | bytes 27656 | tf_op jit(solution)/shard_map/ppermute | solution.py:21
  176.9 0.1 split.56
  177.0 0.2 copy.147
  177.1 3.2 %collective-permute-start.2 = (f32[3,2,3,16]{3,1,2,0:T(2,128)S(1)}, f32[3,2,3,16]{3,1,2,0:T(2,128)S(1)}, u32[]{:S(2)}, u32[]{:S(2)}) collective-permute-start(f32[3,2,3,16]{3,1,2,0:T(2,128)S(1)} %bitcast.134), channel_id=1, source_target_pairs={{0,4},{4,8},{8,12},{12,16},{16,20},{20,24},{24,28},{1,5},{5,9},{9,... | collective-permute-start | bytes 3464 | tf_op jit(solution)/shard_map/ppermute | solution.py:21
  180.3 0.1 add_add_fusion
  180.4 0.6 pad_add_fusion
  181.1 0.2 copy.148
  181.3 0.2 scatter-add.11
  181.5 0.1 scatter-add.14
  181.6 0.7 copy-done.1
  (40 shorter events, 0.3 us)
Async XLA Ops:
  0.6 33.7 %copy-start.6 = (f32[2,3,16,128]{3,2,1,0:T(8,128)S(1)}, f32[2,3,16,128]{3,2,1,0:T(8,128)}, u32[]{:S(2)}) copy-start(f32[2,3,16,128]{3,2,1,0:T(8,128)} %param.15) | copy-start | bytes 147460
  1.6 32.6 %collective-permute-start.1 = (f32[3,2,3,128]{3,1,2,0:T(2,128)S(1)}, f32[3,2,3,128]{3,1,2,0:T(2,128)S(1)}, u32[]{:S(2)}, u32[]{:S(2)}) collective-permute-start(f32[3,2,3,128]{3,1,2,0:T(2,128)S(1)} %bitcast.137), channel_id=1, source_target_pairs={{1,0},{2,1},{3,2},{5,4},{6,5},{7,6},{9,8},{10,9},{11,10},{13,12},{... | collective-permute-start | bytes 27656 | tf_op jit(solution)/shard_map/ppermute | solution.py:21
  3.9 23.7 %collective-permute-start = (f32[3,2,3,16]{3,1,2,0:T(2,128)S(1)}, f32[3,2,3,16]{3,1,2,0:T(2,128)S(1)}, u32[]{:S(2)}, u32[]{:S(2)}) collective-permute-start(f32[3,2,3,16]{3,1,2,0:T(2,128)S(1)} %bitcast.133), channel_id=1, source_target_pairs={{4,0},{8,4},{12,8},{16,12},{20,16},{24,20},{28,24},{5,1},{9,5},{13... | collective-permute-start | bytes 3464 | tf_op jit(solution)/shard_map/ppermute | solution.py:21
  9.5 23.3 %all-to-all-start = ((s32[64,1,4]{2,1,0:T(1,128)}), s32[64,1,4]{2,1,0:T(1,128)S(1)}, u32[]{:S(2)}, u32[]{:S(2)}) async-start(s32[64,1,4]{2,1,0:T(1,128)} %bitcast.21), calls=%async_computation | async-start | bytes 65536 | tf_op jit(solution)/shard_map/all_to_all | solution.py:250
  38.5 5.7 %copy-start.2 = (f32[3,2,3,16,128]{4,3,2,1,0:T(8,128)S(1)}, f32[3,2,3,16,128]{4,3,2,1,0:T(8,128)}, u32[]{:S(2)}) copy-start(f32[3,2,3,16,128]{4,3,2,1,0:T(8,128)} %param.16) | copy-start | bytes 442372
  38.5 5.9 %copy-start.7 = (s32[1,1,1,128]{3,2,1,0:T(1,128)S(1)}, s32[1,1,1,128]{3,2,1,0:T(1,128)}, u32[]{:S(2)}) copy-start(s32[1,1,1,128]{3,2,1,0:T(1,128)} %param.17) | copy-start | bytes 1540
  38.5 45.1 %all-to-all-start.1 = ((f32[64,4,12,128]{3,1,2,0:T(4,128)}), f32[64,4,12,128]{3,1,2,0:T(4,128)S(1)}, u32[]{:S(2)}, u32[]{:S(2)}) async-start(f32[64,4,12,128]{3,1,2,0:T(4,128)} %copy.135), calls=%async_computation.1 | async-start | bytes 3145728 | tf_op jit(solution)/shard_map/all_to_all | solution.py:256
  123.8 7.1 %copy-start.5 = (f32[3,128,128]{2,1,0:T(8,128)S(1)}, f32[3,128,128]{2,1,0:T(8,128)}, u32[]{:S(2)}) copy-start(f32[3,128,128]{2,1,0:T(8,128)} %get-tuple-element.42) | copy-start | bytes 589828
  123.8 7.5 %copy-start = (f32[3,2,3,16,128]{4,3,2,1,0:T(8,128)S(1)}, f32[3,2,3,16,128]{4,3,2,1,0:T(8,128)}, u32[]{:S(2)}) copy-start(f32[3,2,3,16,128]{4,3,2,1,0:T(8,128)} %param.13) | copy-start | bytes 442372
  123.8 7.5 %copy-start.4 = (f32[3,128,128]{2,1,0:T(8,128)S(1)}, f32[3,128,128]{2,1,0:T(8,128)}, u32[]{:S(2)}) copy-start(f32[3,128,128]{2,1,0:T(8,128)} %get-tuple-element.44) | copy-start | bytes 589828
  123.8 46.3 %all-to-all-start.2 = ((f32[64,4,12,128]{3,1,2,0:T(4,128)}), f32[64,4,12,128]{3,1,2,0:T(4,128)S(1)}, u32[]{:S(2)}, u32[]{:S(2)}) async-start(f32[64,4,12,128]{3,1,2,0:T(4,128)} %copy.143), calls=%async_computation.2 | async-start | bytes 3145728 | tf_op jit(solution)/shard_map/all_to_all | solution.py:270
  131.5 39.5 %copy-start.3 = (f32[3,2,3,16,128]{4,3,2,1,0:T(8,128)}, f32[3,2,3,16,128]{4,3,2,1,0:T(8,128)S(1)}, u32[]{:S(2)}) copy-start(f32[3,2,3,16,128]{4,3,2,1,0:T(8,128)S(1)} %fusion.6) | copy-start | bytes 442372
  172.6 8.9 %collective-permute-start.3 = (f32[3,2,3,128]{3,1,2,0:T(2,128)S(1)}, f32[3,2,3,128]{3,1,2,0:T(2,128)S(1)}, u32[]{:S(2)}, u32[]{:S(2)}) collective-permute-start(f32[3,2,3,128]{3,1,2,0:T(2,128)S(1)} %bitcast.139), channel_id=1, source_target_pairs={{0,1},{1,2},{2,3},{4,5},{5,6},{6,7},{8,9},{9,10},{10,11},{12,13},{... | collective-permute-start | bytes 27656 | tf_op jit(solution)/shard_map/ppermute | solution.py:21
  177.1 3.9 %collective-permute-start.2 = (f32[3,2,3,16]{3,1,2,0:T(2,128)S(1)}, f32[3,2,3,16]{3,1,2,0:T(2,128)S(1)}, u32[]{:S(2)}, u32[]{:S(2)}) collective-permute-start(f32[3,2,3,16]{3,1,2,0:T(2,128)S(1)} %bitcast.134), channel_id=1, source_target_pairs={{0,4},{4,8},{8,12},{12,16},{16,20},{20,24},{24,28},{1,5},{5,9},{9,... | collective-permute-start | bytes 3464 | tf_op jit(solution)/shard_map/ppermute | solution.py:21
  181.6 0.7 copy-start.1

commit v2 on v1

--- a/solution.py
+++ b/solution.py
@@ -241,44 +241,47 @@
     )
     rank_within = jnp.sum((jnp.cumsum(owner_onehot, axis=0) - owner_onehot) * owner_onehot, axis=1)
     slot_index = owner_ids * capacity + rank_within
-    request = (
-        jnp.zeros((group_size * capacity,), jnp.int32)
-        .at[slot_index]
-        .set(source_ids)
-        .reshape(group_size, capacity)
-    )
-    asked = lax.all_to_all(
-        request, ("turb", "age"), split_axis=0, concat_axis=0, tiled=True
-    ).reshape(group_size * capacity)
+    slot_count = group_size * capacity
     pair_targets = target_blocks[target_ids]
     pair_seed = seed_blocks[target_ids]
-    picked = payload[asked].reshape(group_size, capacity, 12, age_here)
-    fetched = lax.all_to_all(
-        picked, ("turb", "age"), split_axis=0, concat_axis=0, tiled=True
-    ).reshape(group_size * capacity, 12, age_here)
-    pair_velocity, pair_grad, payload_terms = run_pairs(
-        pair_targets, fetched[slot_index], pair_seed
-    )
-    payload_terms = jnp.concatenate(
-        [payload_terms, jnp.zeros_like(payload_terms[:, :1])], axis=1
-    )
+    ident = jnp.broadcast_to(
+        source_ids.astype(jnp.float32)[:, None, None], (pair_count, 1, age_here)
+    )
+    sent = jnp.concatenate([pair_targets, pair_seed, ident], axis=1)
     outgoing = (
-        jnp.zeros((group_size * capacity, 12, age_here), jnp.float32)
+        jnp.zeros((slot_count, 7, age_here), jnp.float32)
+        .at[:, 6]
+        .set(-1.0)
         .at[slot_index]
-        .set(payload_terms)
-    )
-    returned = lax.all_to_all(
-        outgoing.reshape(group_size, capacity, 12, age_here),
+        .set(sent)
+    )
+    received = lax.all_to_all(
+        outgoing.reshape(group_size, capacity, 7, age_here),
         ("turb", "age"),
         split_axis=0,
         concat_axis=0,
         tiled=True,
-    )
-    payload_grad = onehot_sum(
-        asked, blocks_here, returned.reshape(group_size * capacity, 12, age_here)
-    )
-    velocity = onehot_sum(target_ids, blocks_here, pair_velocity)
-    target_grad = onehot_sum(target_ids, blocks_here, pair_grad)
+    ).reshape(slot_count, 7, age_here)
+    asked = received[:, 6, 0].astype(jnp.int32)
+    slot_payload = payload[jnp.clip(asked, 0, blocks_here - 1)]
+    slot_velocity, slot_grad, payload_terms = run_pairs(
+        received[:, 0:3], slot_payload, received[:, 3:6]
+    )
+    payload_terms = jnp.concatenate(
+        [payload_terms, jnp.zeros_like(payload_terms[:, :1])], axis=1
+    )
+    payload_grad = onehot_sum(asked, blocks_here, payload_terms)
+    answered = lax.all_to_all(
+        jnp.concatenate([slot_velocity, slot_grad], axis=1).reshape(
+            group_size, capacity, 6, age_here
+        ),
+        ("turb", "age"),
+        split_axis=0,
+        concat_axis=0,
+        tiled=True,
+    ).reshape(slot_count, 6, age_here)[slot_index]
+    velocity = onehot_sum(target_ids, blocks_here, answered[:, 0:3])
+    target_grad = onehot_sum(target_ids, blocks_here, answered[:, 3:6])
     advected = positions + time_step * from_rows(velocity)
     advected = advected.at[0].add(time_step)
     grad_nodes, grad_after_age, grad_after_station, grad_strengths = build_pullback(payload_grad)

time: 184 us -> 145 us (0.79)
  waiting for transfers between devices: 79.9 us -> 32.9 us
  Pallas kernels: 27.2 us -> 53.1 us
  local copies, waits for them, and re-layouts: 30.4 us -> 20.5 us
  starting transfers between devices: 36.9 us -> 30.2 us
    all_to_all x3 -> x2, waiting for transfers between devices: 79.8 us -> 10.3 us  [the longest x1 8.08 us: local(): lax.all_to_all(jnp.concatenate([slot_velocity, slot_grad], axis=1).reshap...]
    pallas_call x1, Pallas kernels: 27.2 us -> 53.1 us  [run_pairs(): pl.pallas_call(pair_kernel, grid=(number // step,), in_specs=[spec(3), sp...]
    ppermute x4, waiting for transfers between devices: 0.03 us -> 22.6 us  [shifted_2(): lax.ppermute(value, axis, [(source, source + steps) for source in range(l...]
    all_to_all x3 -> x2, starting transfers between devices: 26.9 us -> 21.1 us  [the longest x1 13 us: local(): lax.all_to_all(outgoing.reshape(group_size, capacity, 7, age_here), ('tur...]
    all_to_all x4 -> x2, local copies, waits for them, and re-layouts: 3.06 us -> 0.31 us  [the longest x1 0.16 us: local(): lax.all_to_all(outgoing.reshape(group_size, capacity, 7, age_here), ('tur...]
    reshape x3 -> x2, local copies, waits for them, and re-layouts: 3.84 us -> 2.18 us  [the longest x1 1.16 us: local(): outgoing.reshape(group_size, capacity, 7, age_here)]
    scatter x2 -> x1, local copies, waits for them, and re-layouts: 5.5 us -> 4.3 us  [local(): outgoing = jnp.zeros((slot_count, 7, age_here), jnp.float32).at[:, 6].set...]
    unnamed x19 -> x22, local copies, waits for them, and re-layouts: 3.91 us -> 4.56 us
  transfers between devices with their start and end apart: 7 -> 6, of which waited for: 3 -> 4; matrix products, arithmetic and copies ran while one was open for 8% -> 5% of each run, Pallas kernels for 0% -> 0%
where the time goes in v2:
time: 145 us; the launch traced here: 144 us
  Pallas kernels  53.1 us (37%)
  waiting for transfers between devices  32.9 us (23%)
  starting transfers between devices  30.2 us (21%)
  local copies, waits for them, and re-layouts  20.5 us (14%)
  other arithmetic  4.71 us (3%)
    pallas_call x1, Pallas kernels, run_pairs(): pl.pallas_call(pair_kernel, grid=(number // step,), in_specs=[spec(3), sp...  53.1 us
    ppermute x4, waiting for transfers between devices, shifted_2(): lax.ppermute(value, axis, [(source, source + steps) for source in range(l...  22.6 us
    all_to_all x1, starting transfers between devices, local(): lax.all_to_all(outgoing.reshape(group_size, capacity, 7, age_here), ('tur...  13 us
    ppermute x4, starting transfers between devices, shifted_2(): lax.ppermute(value, axis, [(source, source + steps) for source in range(l...  9.07 us
    all_to_all x1, starting transfers between devices, local(): lax.all_to_all(jnp.concatenate([slot_velocity, slot_grad], axis=1).reshap...  8.13 us
    all_to_all x1, waiting for transfers between devices, local(): lax.all_to_all(jnp.concatenate([slot_velocity, slot_grad], axis=1).reshap...  8.08 us
    unnamed x22, local copies, waits for them, and re-layouts  4.56 us
    scatter x1, local copies, waits for them, and re-layouts, local(): outgoing = jnp.zeros((slot_count, 7, age_here), jnp.float32).at[:, 6].set...  4.3 us
  transfers between devices with their start and end apart: 6, of which 4 were waited for; matrix products, arithmetic and copies ran while one was open for 5% of the time, Pallas kernels for 0%

profile of v2, /device:TPU:1, one launch (start us, length us, event | category | flops | bytes accessed | tf_op | source)
XLA Modules:
  0.0 144.0 jit_solution(1916917423751129527)
XLA Ops:
  0.7 1.0 copy.111
  1.7 0.7 fusion.17
  2.3 0.9 broadcast_multiply_fusion
  3.3 0.1 copy.112
  3.4 0.8 gather_fusion
  4.1 0.8 gather_fusion.1
  4.9 0.1 fusion.8
  5.0 0.2 reduce_window_sum.11
  5.2 0.2 select_reduce_fusion
  5.4 0.0 copy-start
  5.4 0.2 broadcast_in_dim.4
  5.6 0.2 pad_maximum_fusion.1
  5.8 0.8 copy-done
  6.6 4.3 %scatter_fusion = f32[256,7,128]{2,1,0:T(8,128)S(1)} fusion(f32[256,7,128]{2,1,0:T(8,128)S(1)} %copy-done, s32[128]{0:T(128)S(1)} %fusion.16, f32[128,7,128]{2,1,0:T(8,128)S(1)} %pad_maximum_fusion.1), kind=kCustom, calls=%fused_computation.4 | custom fusion | bytes 1376768 | tf_op jit(solution)/shard_map/scatter | solution.py:256
  10.9 0.0 copy-start.5
  10.9 1.2 copy.113
  12.1 13.0 %all-to-all-start = ((f32[64,4,7,128]{3,1,2,0:T(4,128)}), f32[64,4,7,128]{3,1,2,0:T(4,128)S(1)}, u32[]{:S(2)}, u32[]{:S(2)}) async-start(f32[64,4,7,128]{3,1,2,0:T(4,128)} %copy.113), calls=%async_computation | async-start | bytes 1835008 | tf_op jit(solution)/shard_map/all_to_all | solution.py:258
  25.1 0.2 copy.116
  25.3 1.3 collective-permute-start
  26.6 1.3 collective-permute-start.1
  28.0 0.1 slice_multiply_fusion
  28.0 0.1 slice.154
  28.2 0.1 copy.115
  28.3 18.1 %collective-permute-done = f32[3,2,3,16]{3,1,2,0:T(2,128)S(1)} collective-permute-done((f32[3,2,3,16]{3,1,2,0:T(2,128)S(1)}, f32[3,2,3,16]{3,1,2,0:T(2,128)S(1)}, u32[]{:S(2)}, u32[]{:S(2)}) %collective-permute-start) | collective-permute-done | bytes 1184 | tf_op jit(solution)/shard_map/ppermute | solution.py:21
  46.3 0.1 concatenate.42
  46.4 0.2 copy.118
  46.6 0.2 pad_maximum_fusion.2
  46.8 0.1 copy.121
  46.9 1.2 concatenate.49
  48.2 2.2 %all-to-all-done = f32[64,4,7,128]{3,1,2,0:T(4,128)S(1)} async-done(((f32[64,4,7,128]{3,1,2,0:T(4,128)}), f32[64,4,7,128]{3,1,2,0:T(4,128)S(1)}, u32[]{:S(2)}, u32[]{:S(2)}) %all-to-all-start) | async-done | bytes 917536 | tf_op jit(solution)/shard_map/all_to_all | solution.py:258
  50.4 0.2 copy.114
  50.6 0.1 fusion.5
  50.7 0.9 slice_bitcast_fusion
  51.6 1.0 gather_fusion.2
  52.7 1.7 %copy.137 = f32[256,12,128]{2,0,1:T(8,128)} copy(f32[256,12,128]{2,1,0:T(8,128)S(1)} %gather_fusion.2) | data formatting | bytes 3145728 | tf_op jit(solution)/shard_map/gather | solution.py:266
  54.3 53.1 %shard_map.94 = (f32[3,256,128]{2,1,0:T(8,128)}, f32[3,256,128]{2,1,0:T(8,128)}, f32[11,256,128]{2,1,0:T(8,128)}) custom-call(f32[3,256,128]{2,1,0:T(8,128)} %get-tuple-element.69.t_ref, f32[12,256,128]{2,1,0:T(8,128)} %bitcast.103, f32[3,256,128]{2,1,0:T(8,128)} %get-tuple-element.68.c_ref), custom_call_target="tpu_custom_call" | custom-call | tf_op jit(solution)/shard_map/pallas_call | solution.py:169
  107.4 1.2 pad_maximum_fusion
  108.6 1.0 copy.123
  109.6 8.1 %all-to-all-start.1 = ((f32[64,4,6,128]{3,1,2,0:T(4,128)}), f32[64,4,6,128]{3,1,2,0:T(4,128)S(1)}, u32[]{:S(2)}, u32[]{:S(2)}) async-start(f32[64,4,6,128]{3,1,2,0:T(4,128)} %copy.123), calls=%async_computation.1 | async-start | bytes 1572864 | tf_op jit(solution)/shard_map/all_to_all | solution.py:274
  117.7 1.8 %copy.132 = f32[256,11,128]{0,2,1:T(8,128)S(1)} copy(f32[256,11,128]{2,0,1:T(8,128)} %bitcast.111) | data formatting | bytes 2883584
  119.5 0.8 fusion.1
  120.4 0.1 split.56
  120.5 0.2 copy.128
  120.7 3.3 %collective-permute-start.2 = (f32[3,2,3,16]{3,1,2,0:T(2,128)S(1)}, f32[3,2,3,16]{3,1,2,0:T(2,128)S(1)}, u32[]{:S(2)}, u32[]{:S(2)}) collective-permute-start(f32[3,2,3,16]{3,1,2,0:T(2,128)S(1)} %bitcast.130), channel_id=1, source_target_pairs={{0,4},{4,8},{8,12},{12,16},{16,20},{20,24},{24,28},{1,5},{5,9},{9,... | collective-permute-start | bytes 3464 | tf_op jit(solution)/shard_map/ppermute | solution.py:21
  124.0 3.2 %collective-permute-start.3 = (f32[3,2,3,128]{3,1,2,0:T(2,128)S(1)}, f32[3,2,3,128]{3,1,2,0:T(2,128)S(1)}, u32[]{:S(2)}, u32[]{:S(2)}) collective-permute-start(f32[3,2,3,128]{3,1,2,0:T(2,128)S(1)} %bitcast.133), channel_id=1, source_target_pairs={{0,1},{1,2},{2,3},{4,5},{5,6},{6,7},{8,9},{9,10},{10,11},{12,13},{... | collective-permute-start | bytes 27656 | tf_op jit(solution)/shard_map/ppermute | solution.py:21
  127.2 0.1 broadcast_multiply_fusion.1
  127.3 0.6 pad_add_fusion
  128.0 4.5 %collective-permute-done.2 = f32[3,2,3,16]{3,1,2,0:T(2,128)S(1)} collective-permute-done((f32[3,2,3,16]{3,1,2,0:T(2,128)S(1)}, f32[3,2,3,16]{3,1,2,0:T(2,128)S(1)}, u32[]{:S(2)}, u32[]{:S(2)}) %collective-permute-start.2) | collective-permute-done | bytes 1184 | tf_op jit(solution)/shard_map/ppermute | solution.py:21
  132.5 0.2 copy.129
  132.7 8.1 %all-to-all-done.1 = f32[64,4,6,128]{3,1,2,0:T(4,128)S(1)} async-done(((f32[64,4,6,128]{3,1,2,0:T(4,128)}), f32[64,4,6,128]{3,1,2,0:T(4,128)S(1)}, u32[]{:S(2)}, u32[]{:S(2)}) %all-to-all-start.1) | async-done | bytes 786464 | tf_op jit(solution)/shard_map/all_to_all | solution.py:274
  140.8 0.1 copy.124
  140.9 0.0 copy-start.8
  141.0 0.8 gather_fusion.3
  141.7 0.1 fusion.21
  141.8 0.1 copy.127
  142.0 0.3 fusion.2
  142.3 0.1 add_add_fusion
  142.4 0.2 scatter-add.11
  142.6 0.1 scatter-add.14
  142.7 0.0 copy-start.2
  142.7 0.1 copy.125
  142.8 0.3 convolution_multiply_fusion
  143.2 0.2 copy-done.2
  143.3 0.7 copy-done.4
  (37 shorter events, 0.3 us)
Async XLA Ops:
  0.6 4.3 %copy-start.9 = (s32[1,1,1,128]{3,2,1,0:T(1,128)S(1)}, s32[1,1,1,128]{3,2,1,0:T(1,128)}, u32[]{:S(2)}) copy-start(s32[1,1,1,128]{3,2,1,0:T(1,128)} %param.21) | copy-start | bytes 1540
  0.6 4.3 %copy-start.7 = (s32[1,1,1,128]{3,2,1,0:T(1,128)S(1)}, s32[1,1,1,128]{3,2,1,0:T(1,128)}, u32[]{:S(2)}) copy-start(s32[1,1,1,128]{3,2,1,0:T(1,128)} %param.20) | copy-start | bytes 1540
  5.4 1.2 copy-start
  10.9 14.2 %copy-start.1 = (f32[3,2,3,16,128]{4,3,2,1,0:T(8,128)S(1)}, f32[3,2,3,16,128]{4,3,2,1,0:T(8,128)}, u32[]{:S(2)}) copy-start(f32[3,2,3,16,128]{4,3,2,1,0:T(8,128)} %param.15) | copy-start | bytes 442372
  10.9 17.0 %copy-start.5 = (f32[2,2,3,16,128]{4,3,2,1,0:T(8,128)S(1)}, f32[2,2,3,16,128]{4,3,2,1,0:T(8,128)}, u32[]{:S(2)}) copy-start(f32[2,2,3,16,128]{4,3,2,1,0:T(8,128)} %param.16) | copy-start | bytes 294916
  12.1 38.3 %all-to-all-start = ((f32[64,4,7,128]{3,1,2,0:T(4,128)}), f32[64,4,7,128]{3,1,2,0:T(4,128)S(1)}, u32[]{:S(2)}, u32[]{:S(2)}) async-start(f32[64,4,7,128]{3,1,2,0:T(4,128)} %copy.113), calls=%async_computation | async-start | bytes 1835008 | tf_op jit(solution)/shard_map/all_to_all | solution.py:258
  25.1 21.9 %copy-start.6 = (f32[2,3,16,128]{3,2,1,0:T(8,128)S(1)}, f32[2,3,16,128]{3,2,1,0:T(8,128)}, u32[]{:S(2)}) copy-start(f32[2,3,16,128]{3,2,1,0:T(8,128)} %param.17) | copy-start | bytes 147460
  25.3 21.1 %collective-permute-start = (f32[3,2,3,16]{3,1,2,0:T(2,128)S(1)}, f32[3,2,3,16]{3,1,2,0:T(2,128)S(1)}, u32[]{:S(2)}, u32[]{:S(2)}) collective-permute-start(f32[3,2,3,16]{3,1,2,0:T(2,128)S(1)} %bitcast.129), channel_id=1, source_target_pairs={{4,0},{8,4},{12,8},{16,12},{20,16},{24,20},{28,24},{5,1},{9,5},{13... | collective-permute-start | bytes 3464 | tf_op jit(solution)/shard_map/ppermute | solution.py:21
  26.6 20.2 %collective-permute-start.1 = (f32[3,2,3,128]{3,1,2,0:T(2,128)S(1)}, f32[3,2,3,128]{3,1,2,0:T(2,128)S(1)}, u32[]{:S(2)}, u32[]{:S(2)}) collective-permute-start(f32[3,2,3,128]{3,1,2,0:T(2,128)S(1)} %bitcast.134), channel_id=1, source_target_pairs={{1,0},{2,1},{3,2},{5,4},{6,5},{7,6},{9,8},{10,9},{11,10},{13,12},{... | collective-permute-start | bytes 27656 | tf_op jit(solution)/shard_map/ppermute | solution.py:21
  109.6 31.2 %all-to-all-start.1 = ((f32[64,4,6,128]{3,1,2,0:T(4,128)}), f32[64,4,6,128]{3,1,2,0:T(4,128)S(1)}, u32[]{:S(2)}, u32[]{:S(2)}) async-start(f32[64,4,6,128]{3,1,2,0:T(4,128)} %copy.123), calls=%async_computation.1 | async-start | bytes 1572864 | tf_op jit(solution)/shard_map/all_to_all | solution.py:274
  120.7 11.8 %collective-permute-start.2 = (f32[3,2,3,16]{3,1,2,0:T(2,128)S(1)}, f32[3,2,3,16]{3,1,2,0:T(2,128)S(1)}, u32[]{:S(2)}, u32[]{:S(2)}) collective-permute-start(f32[3,2,3,16]{3,1,2,0:T(2,128)S(1)} %bitcast.130), channel_id=1, source_target_pairs={{0,4},{4,8},{8,12},{12,16},{16,20},{20,24},{24,28},{1,5},{5,9},{9,... | collective-permute-start | bytes 3464 | tf_op jit(solution)/shard_map/ppermute | solution.py:21
  124.0 18.6 %collective-permute-start.3 = (f32[3,2,3,128]{3,1,2,0:T(2,128)S(1)}, f32[3,2,3,128]{3,1,2,0:T(2,128)S(1)}, u32[]{:S(2)}, u32[]{:S(2)}) collective-permute-start(f32[3,2,3,128]{3,1,2,0:T(2,128)S(1)} %bitcast.133), channel_id=1, source_target_pairs={{0,1},{1,2},{2,3},{4,5},{5,6},{6,7},{8,9},{9,10},{10,11},{12,13},{... | collective-permute-start | bytes 27656 | tf_op jit(solution)/shard_map/ppermute | solution.py:21
  140.9 1.0 copy-start.8
  140.9 1.3 copy-start.3
  142.7 0.7 copy-start.2
  143.3 0.7 copy-start.4

commit v3 on v2

--- a/solution.py
+++ b/solution.py
@@ -79,43 +79,75 @@
 GROUP_PAIRS = 8
 
 
-def segment_pair(target, begin, trail_end, shed_end, trail_gamma, shed_gamma, core, inside):
+def dot3(a, b):
+    return a[0] * b[0] + a[1] * b[1] + a[2] * b[2]
+
+
+def cross3(a, b):
+    return (
+        a[1] * b[2] - a[2] * b[1],
+        a[2] * b[0] - a[0] * b[2],
+        a[0] * b[1] - a[1] * b[0],
+    )
+
+
+def segment_pair(target, begin, ends, gammas, core, inside, weight):
     core_sq = core * core
     core_quad = core_sq * core_sq
     near = [target[i] - begin[i] for i in range(3)]
-    begin_sq = near[0] * near[0] + near[1] * near[1] + near[2] * near[2]
-    dist_begin = jnp.sqrt(begin_sq + core_sq)
-    total = [0.0, 0.0, 0.0]
-    for end_point, gamma in ((trail_end, trail_gamma), (shed_end, shed_gamma)):
+    inv_begin = lax.rsqrt(dot3(near, near) + core_sq)
+    velocity = [0.0, 0.0, 0.0]
+    grad_target = [0.0, 0.0, 0.0]
+    grad_begin = [0.0, 0.0, 0.0]
+    grad_ends = []
+    grad_gammas = []
+    for end_point, raw_gamma in zip(ends, gammas):
+        gamma = jnp.where(inside, raw_gamma, 0.0)
         far = [target[i] - end_point[i] for i in range(3)]
         along = [end_point[i] - begin[i] for i in range(3)]
-        cross_x = near[1] * far[2] - near[2] * far[1]
-        cross_y = near[2] * far[0] - near[0] * far[2]
-        cross_z = near[0] * far[1] - near[1] * far[0]
-        cross_sq = cross_x * cross_x + cross_y * cross_y + cross_z * cross_z
-        length_sq = along[0] * along[0] + along[1] * along[1] + along[2] * along[2] + core_sq
-        dist_end = jnp.sqrt(far[0] * far[0] + far[1] * far[1] + far[2] * far[2] + core_sq)
-        projected = (
-            along[0] * (near[0] / dist_begin - far[0] / dist_end)
-            + along[1] * (near[1] / dist_begin - far[1] / dist_end)
-            + along[2] * (near[2] / dist_begin - far[2] / dist_end)
-        )
-        masked = jnp.where(inside, gamma, 0.0)
-        factor = (
-            masked
-            * projected
-            / (four_pi * jnp.sqrt(cross_sq * cross_sq + core_quad * length_sq * length_sq))
-        )
-        total = [total[0] + cross_x * factor, total[1] + cross_y * factor, total[2] + cross_z * factor]
-    return tuple(total)
+        cross = cross3(near, far)
+        cross_sq = dot3(cross, cross)
+        length_sq = dot3(along, along) + core_sq
+        inv_end = lax.rsqrt(dot3(far, far) + core_sq)
+        along_near = dot3(along, near)
+        along_far = dot3(along, far)
+        projected = along_near * inv_begin - along_far * inv_end
+        inv_den = lax.rsqrt(cross_sq * cross_sq + core_quad * length_sq * length_sq)
+        base = projected * inv_den * (1.0 / four_pi)
+        factor = gamma * base
+        for i in range(3):
+            velocity[i] = velocity[i] + cross[i] * factor
+        ct_factor = dot3(cross, weight)
+        grad_gammas.append(jnp.where(inside, ct_factor * base, 0.0))
+        ct_proj = ct_factor * gamma * inv_den * (1.0 / four_pi)
+        ct_q = -0.5 * ct_factor * factor * inv_den * inv_den
+        cross_scale = 4.0 * cross_sq * ct_q
+        along_scale = 4.0 * core_quad * length_sq * ct_q
+        ct_cross = [factor * weight[i] + cross_scale * cross[i] for i in range(3)]
+        near_scale = ct_proj * inv_begin
+        far_scale = ct_proj * inv_end
+        near_radial = near_scale * along_near * inv_begin * inv_begin
+        far_radial = far_scale * along_far * inv_end * inv_end
+        from_far = cross3(far, ct_cross)
+        from_near = cross3(ct_cross, near)
+        ct_along = [
+            along_scale * along[i] + near_scale * near[i] - far_scale * far[i] for i in range(3)
+        ]
+        ct_near = [near_scale * along[i] - near_radial * near[i] + from_far[i] for i in range(3)]
+        ct_far = [-far_scale * along[i] + far_radial * far[i] + from_near[i] for i in range(3)]
+        for i in range(3):
+            grad_target[i] = grad_target[i] + ct_near[i] + ct_far[i]
+            grad_begin[i] = grad_begin[i] - ct_near[i] - ct_along[i]
+        grad_ends.append([ct_along[i] - ct_far[i] for i in range(3)])
+    return velocity, grad_target, grad_begin, grad_ends, grad_gammas
 
 
 def pair_kernel(t_ref, s_ref, c_ref, v_ref, gt_ref, gs_ref):
     shape = t_ref.shape[1:]
     age_count = shape[-1]
     lane = lax.broadcasted_iota(jnp.int32, shape, 1)
-    target = tuple(t_ref[i] for i in range(3))
-    cotangent = tuple(c_ref[i] for i in range(3))
+    target = [t_ref[i] for i in range(3)]
+    cotangent = [c_ref[i] for i in range(3)]
     rows = [s_ref[i] for i in range(12)]
     zero = jnp.zeros(shape, jnp.float32)
     velocity = [zero] * 3
@@ -125,23 +157,17 @@
         amount = (-offset) % age_count
         moved = [pltpu.roll(r, amount, 1) if amount else r for r in rows]
         inside = (lane + offset >= 0) & (lane + offset < age_count)
-        core = moved[11]
-
-        def field(t, b, te, se, tg, sg):
-            return segment_pair(t, b, te, se, tg, sg, core, inside)
-
-        u, pullback = jax.vjp(
-            field,
+        u, d_t, d_b, d_ends, d_gammas = segment_pair(
             target,
-            tuple(moved[0:3]),
-            tuple(moved[3:6]),
-            tuple(moved[6:9]),
-            moved[9],
-            moved[10],
+            moved[0:3],
+            (moved[3:6], moved[6:9]),
+            (moved[9], moved[10]),
+            moved[11],
+            inside,
+            cotangent,
         )
-        d_t, d_b, d_te, d_se, d_tg, d_sg = pullback(cotangent)
-        grads = list(d_b) + list(d_te) + list(d_se) + [d_tg, d_sg]
-        back = (offset) % age_count
+        grads = list(d_b) + list(d_ends[0]) + list(d_ends[1]) + list(d_gammas)
+        back = offset % age_count
         for i in range(3):
             velocity[i] = velocity[i] + u[i]
             grad_target[i] = grad_target[i] + d_t[i]

time: 145 us -> 141 us (0.972)
  Pallas kernels: 53.1 us -> 49.4 us
    pallas_call x1, Pallas kernels: 53.1 us -> 49.4 us  [run_pairs(): pl.pallas_call(pair_kernel, grid=(number // step,), in_specs=[spec(3), sp...]
  transfers between devices with their start and end apart: 6 -> 6, of which waited for: 4 -> 4; matrix products, arithmetic and copies ran while one was open for 5% -> 6% of each run, Pallas kernels for 0% -> 0%
where the time goes in v3:
time: 141 us; the launch traced here: 140 us
  Pallas kernels  49.4 us (35%)
  waiting for transfers between devices  32.9 us (23%)
  starting transfers between devices  30.2 us (21%)
  local copies, waits for them, and re-layouts  20.5 us (15%)
  other arithmetic  4.71 us (3%)
    pallas_call x1, Pallas kernels, run_pairs(): pl.pallas_call(pair_kernel, grid=(number // step,), in_specs=[spec(3), sp...  49.4 us
    ppermute x4, waiting for transfers between devices, shifted_2(): lax.ppermute(value, axis, [(source, source + steps) for source in range(l...  22.6 us
    all_to_all x1, starting transfers between devices, local(): lax.all_to_all(outgoing.reshape(group_size, capacity, 7, age_here), ('tur...  13 us
    ppermute x4, starting transfers between devices, shifted_2(): lax.ppermute(value, axis, [(source, source + steps) for source in range(l...  9.06 us
    all_to_all x1, starting transfers between devices, local(): lax.all_to_all(jnp.concatenate([slot_velocity, slot_grad], axis=1).reshap...  8.13 us
    all_to_all x1, waiting for transfers between devices, local(): lax.all_to_all(jnp.concatenate([slot_velocity, slot_grad], axis=1).reshap...  8.08 us
    unnamed x22, local copies, waits for them, and re-layouts  4.56 us
    scatter x1, local copies, waits for them, and re-layouts, local(): outgoing = jnp.zeros((slot_count, 7, age_here), jnp.float32).at[:, 6].set...  4.3 us
  transfers between devices with their start and end apart: 6, of which 4 were waited for; matrix products, arithmetic and copies ran while one was open for 6% of the time, Pallas kernels for 0%

profile of v3, /device:TPU:1, one launch (start us, length us, event | category | flops | bytes accessed | tf_op | source)
XLA Modules:
  0.0 140.4 jit_solution(16791916578815429953)
XLA Ops:
  0.7 1.0 copy.111
  1.7 0.7 fusion.17
  2.3 0.9 broadcast_multiply_fusion
  3.3 0.1 copy.112
  3.4 0.7 gather_fusion
  4.1 0.7 gather_fusion.1
  4.9 0.1 fusion.8
  5.0 0.2 reduce_window_sum.11
  5.2 0.2 select_reduce_fusion
  5.4 0.0 copy-start
  5.4 0.2 broadcast_in_dim.4
  5.6 0.2 pad_maximum_fusion.1
  5.8 0.8 copy-done
  6.6 4.3 %scatter_fusion = f32[256,7,128]{2,1,0:T(8,128)S(1)} fusion(f32[256,7,128]{2,1,0:T(8,128)S(1)} %copy-done, s32[128]{0:T(128)S(1)} %fusion.16, f32[128,7,128]{2,1,0:T(8,128)S(1)} %pad_maximum_fusion.1), kind=kCustom, calls=%fused_computation.4 | custom fusion | bytes 1376768 | tf_op jit(solution)/shard_map/scatter | solution.py:282
  10.9 0.0 copy-start.1
  10.9 0.0 copy-start.5
  10.9 1.2 copy.113
  12.1 13.0 %all-to-all-start = ((f32[64,4,7,128]{3,1,2,0:T(4,128)}), f32[64,4,7,128]{3,1,2,0:T(4,128)S(1)}, u32[]{:S(2)}, u32[]{:S(2)}) async-start(f32[64,4,7,128]{3,1,2,0:T(4,128)} %copy.113), calls=%async_computation | async-start | bytes 1835008 | tf_op jit(solution)/shard_map/all_to_all | solution.py:284
  25.1 0.2 copy.116
  25.3 1.3 collective-permute-start
  26.6 1.3 collective-permute-start.1
  28.0 0.1 slice_multiply_fusion
  28.0 0.1 slice.154
  28.2 0.1 copy.115
  28.3 18.1 %collective-permute-done = f32[3,2,3,16]{3,1,2,0:T(2,128)S(1)} collective-permute-done((f32[3,2,3,16]{3,1,2,0:T(2,128)S(1)}, f32[3,2,3,16]{3,1,2,0:T(2,128)S(1)}, u32[]{:S(2)}, u32[]{:S(2)}) %collective-permute-start) | collective-permute-done | bytes 1184 | tf_op jit(solution)/shard_map/ppermute | solution.py:21
  46.3 0.1 concatenate.42
  46.4 0.2 copy.118
  46.6 0.2 pad_maximum_fusion.2
  46.8 0.1 copy.121
  46.9 1.2 concatenate.49
  48.2 2.2 %all-to-all-done = f32[64,4,7,128]{3,1,2,0:T(4,128)S(1)} async-done(((f32[64,4,7,128]{3,1,2,0:T(4,128)}), f32[64,4,7,128]{3,1,2,0:T(4,128)S(1)}, u32[]{:S(2)}, u32[]{:S(2)}) %all-to-all-start) | async-done | bytes 917536 | tf_op jit(solution)/shard_map/all_to_all | solution.py:284
  50.4 0.2 copy.114
  50.6 0.1 fusion.5
  50.7 0.9 slice_bitcast_fusion
  51.6 1.0 gather_fusion.2
  52.7 1.7 %copy.137 = f32[256,12,128]{2,0,1:T(8,128)} copy(f32[256,12,128]{2,1,0:T(8,128)S(1)} %gather_fusion.2) | data formatting | bytes 3145728 | tf_op jit(solution)/shard_map/gather | solution.py:292
  54.3 49.4 %shard_map.94 = (f32[3,256,128]{2,1,0:T(8,128)}, f32[3,256,128]{2,1,0:T(8,128)}, f32[11,256,128]{2,1,0:T(8,128)}) custom-call(f32[3,256,128]{2,1,0:T(8,128)} %get-tuple-element.69.t_ref, f32[12,256,128]{2,1,0:T(8,128)} %bitcast.103, f32[3,256,128]{2,1,0:T(8,128)} %get-tuple-element.68.c_ref), custom_call_target="tpu_custom_call" | custom-call | tf_op jit(solution)/shard_map/pallas_call | solution.py:195
  103.8 1.2 pad_maximum_fusion
  104.9 1.0 copy.123
  106.0 8.1 %all-to-all-start.1 = ((f32[64,4,6,128]{3,1,2,0:T(4,128)}), f32[64,4,6,128]{3,1,2,0:T(4,128)S(1)}, u32[]{:S(2)}, u32[]{:S(2)}) async-start(f32[64,4,6,128]{3,1,2,0:T(4,128)} %copy.123), calls=%async_computation.1 | async-start | bytes 1572864 | tf_op jit(solution)/shard_map/all_to_all | solution.py:300
  114.1 1.8 %copy.132 = f32[256,11,128]{0,2,1:T(8,128)S(1)} copy(f32[256,11,128]{2,0,1:T(8,128)} %bitcast.111) | data formatting | bytes 2883584
  115.9 0.8 fusion.1
  116.8 0.1 split.56
  116.9 0.2 copy.128
  117.1 3.3 %collective-permute-start.2 = (f32[3,2,3,16]{3,1,2,0:T(2,128)S(1)}, f32[3,2,3,16]{3,1,2,0:T(2,128)S(1)}, u32[]{:S(2)}, u32[]{:S(2)}) collective-permute-start(f32[3,2,3,16]{3,1,2,0:T(2,128)S(1)} %bitcast.130), channel_id=1, source_target_pairs={{0,4},{4,8},{8,12},{12,16},{16,20},{20,24},{24,28},{1,5},{5,9},{9,... | collective-permute-start | bytes 3464 | tf_op jit(solution)/shard_map/ppermute | solution.py:21
  120.4 3.2 %collective-permute-start.3 = (f32[3,2,3,128]{3,1,2,0:T(2,128)S(1)}, f32[3,2,3,128]{3,1,2,0:T(2,128)S(1)}, u32[]{:S(2)}, u32[]{:S(2)}) collective-permute-start(f32[3,2,3,128]{3,1,2,0:T(2,128)S(1)} %bitcast.133), channel_id=1, source_target_pairs={{0,1},{1,2},{2,3},{4,5},{5,6},{6,7},{8,9},{9,10},{10,11},{12,13},{... | collective-permute-start | bytes 27656 | tf_op jit(solution)/shard_map/ppermute | solution.py:21
  123.6 0.1 broadcast_multiply_fusion.1
  123.7 0.6 pad_add_fusion
  124.3 4.5 %collective-permute-done.2 = f32[3,2,3,16]{3,1,2,0:T(2,128)S(1)} collective-permute-done((f32[3,2,3,16]{3,1,2,0:T(2,128)S(1)}, f32[3,2,3,16]{3,1,2,0:T(2,128)S(1)}, u32[]{:S(2)}, u32[]{:S(2)}) %collective-permute-start.2) | collective-permute-done | bytes 1184 | tf_op jit(solution)/shard_map/ppermute | solution.py:21
  128.9 0.2 copy.129
  129.1 8.1 %all-to-all-done.1 = f32[64,4,6,128]{3,1,2,0:T(4,128)S(1)} async-done(((f32[64,4,6,128]{3,1,2,0:T(4,128)}), f32[64,4,6,128]{3,1,2,0:T(4,128)S(1)}, u32[]{:S(2)}, u32[]{:S(2)}) %all-to-all-start.1) | async-done | bytes 786464 | tf_op jit(solution)/shard_map/all_to_all | solution.py:300
  137.1 0.1 copy.124
  137.3 0.8 gather_fusion.3
  138.1 0.1 fusion.21
  138.2 0.1 copy.127
  138.4 0.3 fusion.2
  138.6 0.1 add_add_fusion
  138.8 0.2 scatter-add.11
  139.0 0.1 scatter-add.14
  139.1 0.0 copy-start.2
  139.1 0.1 copy.125
  139.2 0.3 convolution_multiply_fusion
  139.5 0.2 copy-done.2
  139.7 0.7 copy-done.4
  (37 shorter events, 0.3 us)
Async XLA Ops:
  0.6 4.3 %copy-start.9 = (s32[1,1,1,128]{3,2,1,0:T(1,128)S(1)}, s32[1,1,1,128]{3,2,1,0:T(1,128)}, u32[]{:S(2)}) copy-start(s32[1,1,1,128]{3,2,1,0:T(1,128)} %param.21) | copy-start | bytes 1540
  0.6 4.3 %copy-start.7 = (s32[1,1,1,128]{3,2,1,0:T(1,128)S(1)}, s32[1,1,1,128]{3,2,1,0:T(1,128)}, u32[]{:S(2)}) copy-start(s32[1,1,1,128]{3,2,1,0:T(1,128)} %param.20) | copy-start | bytes 1540
  5.4 1.2 copy-start
  10.9 14.2 %copy-start.1 = (f32[3,2,3,16,128]{4,3,2,1,0:T(8,128)S(1)}, f32[3,2,3,16,128]{4,3,2,1,0:T(8,128)}, u32[]{:S(2)}) copy-start(f32[3,2,3,16,128]{4,3,2,1,0:T(8,128)} %param.15) | copy-start | bytes 442372
  10.9 17.0 %copy-start.5 = (f32[2,2,3,16,128]{4,3,2,1,0:T(8,128)S(1)}, f32[2,2,3,16,128]{4,3,2,1,0:T(8,128)}, u32[]{:S(2)}) copy-start(f32[2,2,3,16,128]{4,3,2,1,0:T(8,128)} %param.16) | copy-start | bytes 294916
  12.1 38.3 %all-to-all-start = ((f32[64,4,7,128]{3,1,2,0:T(4,128)}), f32[64,4,7,128]{3,1,2,0:T(4,128)S(1)}, u32[]{:S(2)}, u32[]{:S(2)}) async-start(f32[64,4,7,128]{3,1,2,0:T(4,128)} %copy.113), calls=%async_computation | async-start | bytes 1835008 | tf_op jit(solution)/shard_map/all_to_all | solution.py:284
  25.1 21.9 %copy-start.6 = (f32[2,3,16,128]{3,2,1,0:T(8,128)S(1)}, f32[2,3,16,128]{3,2,1,0:T(8,128)}, u32[]{:S(2)}) copy-start(f32[2,3,16,128]{3,2,1,0:T(8,128)} %param.17) | copy-start | bytes 147460
  25.3 21.1 %collective-permute-start = (f32[3,2,3,16]{3,1,2,0:T(2,128)S(1)}, f32[3,2,3,16]{3,1,2,0:T(2,128)S(1)}, u32[]{:S(2)}, u32[]{:S(2)}) collective-permute-start(f32[3,2,3,16]{3,1,2,0:T(2,128)S(1)} %bitcast.129), channel_id=1, source_target_pairs={{4,0},{8,4},{12,8},{16,12},{20,16},{24,20},{28,24},{5,1},{9,5},{13... | collective-permute-start | bytes 3464 | tf_op jit(solution)/shard_map/ppermute | solution.py:21
  26.6 20.2 %collective-permute-start.1 = (f32[3,2,3,128]{3,1,2,0:T(2,128)S(1)}, f32[3,2,3,128]{3,1,2,0:T(2,128)S(1)}, u32[]{:S(2)}, u32[]{:S(2)}) collective-permute-start(f32[3,2,3,128]{3,1,2,0:T(2,128)S(1)} %bitcast.134), channel_id=1, source_target_pairs={{1,0},{2,1},{3,2},{5,4},{6,5},{7,6},{9,8},{10,9},{11,10},{13,12},{... | collective-permute-start | bytes 27656 | tf_op jit(solution)/shard_map/ppermute | solution.py:21
  106.0 31.2 %all-to-all-start.1 = ((f32[64,4,6,128]{3,1,2,0:T(4,128)}), f32[64,4,6,128]{3,1,2,0:T(4,128)S(1)}, u32[]{:S(2)}, u32[]{:S(2)}) async-start(f32[64,4,6,128]{3,1,2,0:T(4,128)} %copy.123), calls=%async_computation.1 | async-start | bytes 1572864 | tf_op jit(solution)/shard_map/all_to_all | solution.py:300
  117.1 11.8 %collective-permute-start.2 = (f32[3,2,3,16]{3,1,2,0:T(2,128)S(1)}, f32[3,2,3,16]{3,1,2,0:T(2,128)S(1)}, u32[]{:S(2)}, u32[]{:S(2)}) collective-permute-start(f32[3,2,3,16]{3,1,2,0:T(2,128)S(1)} %bitcast.130), channel_id=1, source_target_pairs={{0,4},{4,8},{8,12},{12,16},{16,20},{20,24},{24,28},{1,5},{5,9},{9,... | collective-permute-start | bytes 3464 | tf_op jit(solution)/shard_map/ppermute | solution.py:21
  120.4 18.6 %collective-permute-start.3 = (f32[3,2,3,128]{3,1,2,0:T(2,128)S(1)}, f32[3,2,3,128]{3,1,2,0:T(2,128)S(1)}, u32[]{:S(2)}, u32[]{:S(2)}) collective-permute-start(f32[3,2,3,128]{3,1,2,0:T(2,128)S(1)} %bitcast.133), channel_id=1, source_target_pairs={{0,1},{1,2},{2,3},{4,5},{5,6},{6,7},{8,9},{9,10},{10,11},{12,13},{... | collective-permute-start | bytes 27656 | tf_op jit(solution)/shard_map/ppermute | solution.py:21
  137.3 1.0 copy-start.8
  137.3 1.3 copy-start.3
  139.1 0.7 copy-start.2
  139.7 0.7 copy-start.4

commit v4 on v3

--- a/solution.py
+++ b/solution.py
@@ -77,6 +77,7 @@
 
 
 GROUP_PAIRS = 8
+BLOCK_PAIRS = 64
 
 
 def dot3(a, b):
@@ -142,49 +143,59 @@
     return velocity, grad_target, grad_begin, grad_ends, grad_gammas
 
 
-def pair_kernel(t_ref, s_ref, c_ref, v_ref, gt_ref, gs_ref):
-    shape = t_ref.shape[1:]
-    age_count = shape[-1]
-    lane = lax.broadcasted_iota(jnp.int32, shape, 1)
-    target = [t_ref[i] for i in range(3)]
-    cotangent = [c_ref[i] for i in range(3)]
-    rows = [s_ref[i] for i in range(12)]
-    zero = jnp.zeros(shape, jnp.float32)
-    velocity = [zero] * 3
-    grad_target = [zero] * 3
-    grad_rows = [zero] * 11
+def pair_group(target, cotangent, rows, lane):
+    age_count = lane.shape[-1]
+    velocity = [0.0] * 3
+    grad_target = [0.0] * 3
+    grad_rows = [0.0] * 11
     for offset in range(-REACH, REACH):
-        amount = (-offset) % age_count
-        moved = [pltpu.roll(r, amount, 1) if amount else r for r in rows]
-        inside = (lane + offset >= 0) & (lane + offset < age_count)
+        amount = offset % age_count
+        moved = [pltpu.roll(r, amount, 1) if amount else r for r in target]
+        weight = [pltpu.roll(r, amount, 1) if amount else r for r in cotangent]
+        inside = (lane - offset >= 0) & (lane - offset < age_count)
         u, d_t, d_b, d_ends, d_gammas = segment_pair(
-            target,
-            moved[0:3],
-            (moved[3:6], moved[6:9]),
-            (moved[9], moved[10]),
-            moved[11],
+            moved,
+            rows[0:3],
+            (rows[3:6], rows[6:9]),
+            (rows[9], rows[10]),
+            rows[11],
             inside,
-            cotangent,
+            weight,
         )
         grads = list(d_b) + list(d_ends[0]) + list(d_ends[1]) + list(d_gammas)
-        back = offset % age_count
+        back = (-offset) % age_count
         for i in range(3):
-            velocity[i] = velocity[i] + u[i]
-            grad_target[i] = grad_target[i] + d_t[i]
+            velocity[i] = velocity[i] + (pltpu.roll(u[i], back, 1) if back else u[i])
+            grad_target[i] = grad_target[i] + (pltpu.roll(d_t[i], back, 1) if back else d_t[i])
         for i in range(11):
-            g = pltpu.roll(grads[i], back, 1) if back else grads[i]
-            grad_rows[i] = grad_rows[i] + g
-    for i in range(3):
-        v_ref[i] = velocity[i]
-        gt_ref[i] = grad_target[i]
-    for i in range(11):
-        gs_ref[i] = grad_rows[i]
+            grad_rows[i] = grad_rows[i] + grads[i]
+    return velocity, grad_target, grad_rows
+
+
+def pair_kernel(t_ref, s_ref, c_ref, v_ref, gt_ref, gs_ref):
+    age_count = t_ref.shape[-1]
+    lane = lax.broadcasted_iota(jnp.int32, (GROUP_PAIRS, age_count), 1)
+
+    def body(group, carry):
+        at = pl.ds(pl.multiple_of(group * GROUP_PAIRS, GROUP_PAIRS), GROUP_PAIRS)
+        target = [t_ref[i, at, :] for i in range(3)]
+        cotangent = [c_ref[i, at, :] for i in range(3)]
+        rows = [s_ref[i, at, :] for i in range(12)]
+        velocity, grad_target, grad_rows = pair_group(target, cotangent, rows, lane)
+        for i in range(3):
+            v_ref[i, at, :] = velocity[i]
+            gt_ref[i, at, :] = grad_target[i]
+        for i in range(11):
+            gs_ref[i, at, :] = grad_rows[i]
+        return carry
+
+    lax.fori_loop(0, t_ref.shape[1] // GROUP_PAIRS, body, 0)
 
 
 def run_pairs(targets, payload, cotangent):
     number = targets.shape[0]
     age_count = targets.shape[-1]
-    step = GROUP_PAIRS
+    step = min(number, BLOCK_PAIRS)
 
     def spec(rows):
         return pl.BlockSpec((rows, step, age_count), lambda i: (0, i, 0))

time: 141 us -> 120 us (0.85)
  Pallas kernels: 49.4 us -> 28.6 us
    pallas_call x1, Pallas kernels: 49.4 us -> 28.6 us  [run_pairs(): pl.pallas_call(pair_kernel, grid=(number // step,), in_specs=[spec(3), sp...]
  transfers between devices with their start and end apart: 6 -> 6, of which waited for: 4 -> 4; matrix products, arithmetic and copies ran while one was open for 6% -> 7% of each run, Pallas kernels for 0% -> 0%
where the time goes in v4:
time: 120 us
  waiting for transfers between devices  32.9 us (27%)
  starting transfers between devices  30.2 us (25%)
  Pallas kernels  28.6 us (24%)
  local copies, waits for them, and re-layouts  20.5 us (17%)
  other arithmetic  4.71 us (4%)
  matrix products  1.4 us (1%)
    pallas_call x1, Pallas kernels, run_pairs(): pl.pallas_call(pair_kernel, grid=(number // step,), in_specs=[spec(3), sp...  28.6 us
    ppermute x4, waiting for transfers between devices, shifted_2(): lax.ppermute(value, axis, [(source, source + steps) for source in range(l...  22.6 us
    all_to_all x1, starting transfers between devices, local(): lax.all_to_all(outgoing.reshape(group_size, capacity, 7, age_here), ('tur...  13 us
    ppermute x4, starting transfers between devices, shifted_2(): lax.ppermute(value, axis, [(source, source + steps) for source in range(l...  9.07 us
    all_to_all x1, starting transfers between devices, local(): lax.all_to_all(jnp.concatenate([slot_velocity, slot_grad], axis=1).reshap...  8.13 us
    all_to_all x1, waiting for transfers between devices, local(): lax.all_to_all(jnp.concatenate([slot_velocity, slot_grad], axis=1).reshap...  8.08 us
    unnamed x22, local copies, waits for them, and re-layouts  4.56 us
    scatter x1, local copies, waits for them, and re-layouts, local(): outgoing = jnp.zeros((slot_count, 7, age_here), jnp.float32).at[:, 6].set...  4.3 us
  transfers between devices with their start and end apart: 6, of which 4 were waited for; matrix products, arithmetic and copies ran while one was open for 7% of the time, Pallas kernels for 0%

profile of v4, /device:TPU:1, one launch (start us, length us, event | category | flops | bytes accessed | tf_op | source)
XLA Modules:
  0.0 119.6 jit_solution(18408277082403551736)
XLA Ops:
  0.7 1.0 copy.111
  1.7 0.7 fusion.17
  2.3 0.9 broadcast_multiply_fusion
  3.3 0.1 copy.112
  3.4 0.8 gather_fusion
  4.1 0.8 gather_fusion.1
  4.9 0.1 fusion.8
  5.0 0.2 reduce_window_sum.11
  5.2 0.2 select_reduce_fusion
  5.4 0.0 copy-start
  5.4 0.2 broadcast_in_dim.4
  5.6 0.2 pad_maximum_fusion.1
  5.8 0.8 copy-done
  6.6 4.3 %scatter_fusion = f32[256,7,128]{2,1,0:T(8,128)S(1)} fusion(f32[256,7,128]{2,1,0:T(8,128)S(1)} %copy-done, s32[128]{0:T(128)S(1)} %fusion.16, f32[128,7,128]{2,1,0:T(8,128)S(1)} %pad_maximum_fusion.1), kind=kCustom, calls=%fused_computation.4 | custom fusion | bytes 1376768 | tf_op jit(solution)/shard_map/scatter | solution.py:293
  10.9 0.0 copy-start.1
  10.9 0.0 copy-start.5
  10.9 1.2 copy.113
  12.1 13.0 %all-to-all-start = ((f32[64,4,7,128]{3,1,2,0:T(4,128)}), f32[64,4,7,128]{3,1,2,0:T(4,128)S(1)}, u32[]{:S(2)}, u32[]{:S(2)}) async-start(f32[64,4,7,128]{3,1,2,0:T(4,128)} %copy.113), calls=%async_computation | async-start | bytes 1835008 | tf_op jit(solution)/shard_map/all_to_all | solution.py:295
  25.1 0.2 copy.116
  25.3 1.3 %collective-permute-start = (f32[3,2,3,16]{3,1,2,0:T(2,128)S(1)}, f32[3,2,3,16]{3,1,2,0:T(2,128)S(1)}, u32[]{:S(2)}, u32[]{:S(2)}) collective-permute-start(f32[3,2,3,16]{3,1,2,0:T(2,128)S(1)} %bitcast.129), channel_id=1, source_target_pairs={{4,0},{8,4},{12,8},{16,12},{20,16},{24,20},{28,24},{5,1},{9,5},{13... | collective-permute-start | bytes 3464 | tf_op jit(solution)/shard_map/ppermute | solution.py:21
  26.6 1.3 %collective-permute-start.1 = (f32[3,2,3,128]{3,1,2,0:T(2,128)S(1)}, f32[3,2,3,128]{3,1,2,0:T(2,128)S(1)}, u32[]{:S(2)}, u32[]{:S(2)}) collective-permute-start(f32[3,2,3,128]{3,1,2,0:T(2,128)S(1)} %bitcast.134), channel_id=1, source_target_pairs={{1,0},{2,1},{3,2},{5,4},{6,5},{7,6},{9,8},{10,9},{11,10},{13,12},{... | collective-permute-start | bytes 27656 | tf_op jit(solution)/shard_map/ppermute | solution.py:21
  27.9 0.1 slice_multiply_fusion
  28.0 0.1 slice.154
  28.1 0.1 copy.115
  28.3 18.1 %collective-permute-done = f32[3,2,3,16]{3,1,2,0:T(2,128)S(1)} collective-permute-done((f32[3,2,3,16]{3,1,2,0:T(2,128)S(1)}, f32[3,2,3,16]{3,1,2,0:T(2,128)S(1)}, u32[]{:S(2)}, u32[]{:S(2)}) %collective-permute-start) | collective-permute-done | bytes 1184 | tf_op jit(solution)/shard_map/ppermute | solution.py:21
  46.3 0.1 concatenate.42
  46.4 0.2 copy.118
  46.6 0.2 pad_maximum_fusion.2
  46.8 0.1 copy.121
  46.9 1.2 %concatenate.49 = f32[12,96,128]{2,0,1:T(8,128)S(1)} concatenate(f32[3,96,128]{2,0,1:T(4,128)S(1)} %bitcast.110, f32[3,96,128]{2,0,1:T(4,128)S(1)} %pad_maximum_fusion.2, f32[3,96,128]{2,0,1:T(4,128)S(1)} %bitcast.115, f32[1,96,128]{2,0,1:T(1,128)S(1)} %bitcast.125, f32[1,96,128]{2,0,1:T(1,128)S(1)} %bitcast.124, f32[1,96,128]{2,0,1:T(1,128)S(1)} %bitcast.128), dimensions={0} | concatenate | bytes 1179648 | tf_op jit(solution)/shard_map/jvp()/concatenate | solution.py:260
  48.2 2.2 %all-to-all-done = f32[64,4,7,128]{3,1,2,0:T(4,128)S(1)} async-done(((f32[64,4,7,128]{3,1,2,0:T(4,128)}), f32[64,4,7,128]{3,1,2,0:T(4,128)S(1)}, u32[]{:S(2)}, u32[]{:S(2)}) %all-to-all-start) | async-done | bytes 917536 | tf_op jit(solution)/shard_map/all_to_all | solution.py:295
  50.4 0.2 copy.114
  50.6 0.1 fusion.5
  50.7 0.9 slice_bitcast_fusion
  51.6 1.0 gather_fusion.2
  52.7 1.7 %copy.137 = f32[256,12,128]{2,0,1:T(8,128)} copy(f32[256,12,128]{2,1,0:T(8,128)S(1)} %gather_fusion.2) | data formatting | bytes 3145728 | tf_op jit(solution)/shard_map/gather | solution.py:303
  54.3 28.6 %shard_map.94 = (f32[3,256,128]{2,1,0:T(8,128)}, f32[3,256,128]{2,1,0:T(8,128)}, f32[11,256,128]{2,1,0:T(8,128)}) custom-call(f32[3,256,128]{2,1,0:T(8,128)} %get-tuple-element.69.t_ref, f32[12,256,128]{2,1,0:T(8,128)} %bitcast.103, f32[3,256,128]{2,1,0:T(8,128)} %get-tuple-element.68.c_ref), custom_call_target="tpu_custom_call" | custom-call | tf_op jit(solution)/shard_map/pallas_call | solution.py:206
  83.0 1.2 pad_maximum_fusion
  84.1 1.0 copy.123
  85.2 8.1 %all-to-all-start.1 = ((f32[64,4,6,128]{3,1,2,0:T(4,128)}), f32[64,4,6,128]{3,1,2,0:T(4,128)S(1)}, u32[]{:S(2)}, u32[]{:S(2)}) async-start(f32[64,4,6,128]{3,1,2,0:T(4,128)} %copy.123), calls=%async_computation.1 | async-start | bytes 1572864 | tf_op jit(solution)/shard_map/all_to_all | solution.py:311
  93.3 1.8 %copy.132 = f32[256,11,128]{0,2,1:T(8,128)S(1)} copy(f32[256,11,128]{2,0,1:T(8,128)} %bitcast.111) | data formatting | bytes 2883584
  95.1 0.8 fusion.1
  96.0 0.1 split.56
  96.1 0.2 copy.128
  96.3 3.3 %collective-permute-start.2 = (f32[3,2,3,16]{3,1,2,0:T(2,128)S(1)}, f32[3,2,3,16]{3,1,2,0:T(2,128)S(1)}, u32[]{:S(2)}, u32[]{:S(2)}) collective-permute-start(f32[3,2,3,16]{3,1,2,0:T(2,128)S(1)} %bitcast.130), channel_id=1, source_target_pairs={{0,4},{4,8},{8,12},{12,16},{16,20},{20,24},{24,28},{1,5},{5,9},{9,... | collective-permute-start | bytes 3464 | tf_op jit(solution)/shard_map/ppermute | solution.py:21
  99.6 3.2 %collective-permute-start.3 = (f32[3,2,3,128]{3,1,2,0:T(2,128)S(1)}, f32[3,2,3,128]{3,1,2,0:T(2,128)S(1)}, u32[]{:S(2)}, u32[]{:S(2)}) collective-permute-start(f32[3,2,3,128]{3,1,2,0:T(2,128)S(1)} %bitcast.133), channel_id=1, source_target_pairs={{0,1},{1,2},{2,3},{4,5},{5,6},{6,7},{8,9},{9,10},{10,11},{12,13},{... | collective-permute-start | bytes 27656 | tf_op jit(solution)/shard_map/ppermute | solution.py:21
  102.8 0.1 broadcast_multiply_fusion.1
  102.9 0.6 pad_add_fusion
  103.5 4.5 %collective-permute-done.2 = f32[3,2,3,16]{3,1,2,0:T(2,128)S(1)} collective-permute-done((f32[3,2,3,16]{3,1,2,0:T(2,128)S(1)}, f32[3,2,3,16]{3,1,2,0:T(2,128)S(1)}, u32[]{:S(2)}, u32[]{:S(2)}) %collective-permute-start.2) | collective-permute-done | bytes 1184 | tf_op jit(solution)/shard_map/ppermute | solution.py:21
  108.1 0.2 copy.129
  108.3 8.1 %all-to-all-done.1 = f32[64,4,6,128]{3,1,2,0:T(4,128)S(1)} async-done(((f32[64,4,6,128]{3,1,2,0:T(4,128)}), f32[64,4,6,128]{3,1,2,0:T(4,128)S(1)}, u32[]{:S(2)}, u32[]{:S(2)}) %all-to-all-start.1) | async-done | bytes 786464 | tf_op jit(solution)/shard_map/all_to_all | solution.py:311
  116.3 0.1 copy.124
  116.5 0.8 gather_fusion.3
  117.3 0.1 fusion.21
  117.4 0.1 copy.127
  117.5 0.3 fusion.2
  117.8 0.1 add_add_fusion
  118.0 0.2 scatter-add.11
  118.2 0.1 scatter-add.14
  118.2 0.0 copy-start.2
  118.3 0.1 copy.125
  118.4 0.3 convolution_multiply_fusion
  118.7 0.2 copy-done.2
  118.9 0.7 copy-done.4
  (37 shorter events, 0.3 us)
Async XLA Ops:
  0.6 4.3 %copy-start.9 = (s32[1,1,1,128]{3,2,1,0:T(1,128)S(1)}, s32[1,1,1,128]{3,2,1,0:T(1,128)}, u32[]{:S(2)}) copy-start(s32[1,1,1,128]{3,2,1,0:T(1,128)} %param.21) | copy-start | bytes 1540
  0.6 4.3 %copy-start.7 = (s32[1,1,1,128]{3,2,1,0:T(1,128)S(1)}, s32[1,1,1,128]{3,2,1,0:T(1,128)}, u32[]{:S(2)}) copy-start(s32[1,1,1,128]{3,2,1,0:T(1,128)} %param.20) | copy-start | bytes 1540
  5.4 1.2 %copy-start = (f32[256,7,128]{2,1,0:T(8,128)S(1)}, f32[256,7,128]{2,1,0:T(8,128)}, u32[]{:S(2)}) copy-start(f32[256,7,128]{2,1,0:T(8,128)} %constant.133.clone.1) | copy-start | bytes 2752516
  10.9 14.2 %copy-start.1 = (f32[3,2,3,16,128]{4,3,2,1,0:T(8,128)S(1)}, f32[3,2,3,16,128]{4,3,2,1,0:T(8,128)}, u32[]{:S(2)}) copy-start(f32[3,2,3,16,128]{4,3,2,1,0:T(8,128)} %param.15) | copy-start | bytes 442372
  10.9 17.0 %copy-start.5 = (f32[2,2,3,16,128]{4,3,2,1,0:T(8,128)S(1)}, f32[2,2,3,16,128]{4,3,2,1,0:T(8,128)}, u32[]{:S(2)}) copy-start(f32[2,2,3,16,128]{4,3,2,1,0:T(8,128)} %param.16) | copy-start | bytes 294916
  12.1 38.3 %all-to-all-start = ((f32[64,4,7,128]{3,1,2,0:T(4,128)}), f32[64,4,7,128]{3,1,2,0:T(4,128)S(1)}, u32[]{:S(2)}, u32[]{:S(2)}) async-start(f32[64,4,7,128]{3,1,2,0:T(4,128)} %copy.113), calls=%async_computation | async-start | bytes 1835008 | tf_op jit(solution)/shard_map/all_to_all | solution.py:295
  25.1 21.9 %copy-start.6 = (f32[2,3,16,128]{3,2,1,0:T(8,128)S(1)}, f32[2,3,16,128]{3,2,1,0:T(8,128)}, u32[]{:S(2)}) copy-start(f32[2,3,16,128]{3,2,1,0:T(8,128)} %param.17) | copy-start | bytes 147460
  25.3 21.1 %collective-permute-start = (f32[3,2,3,16]{3,1,2,0:T(2,128)S(1)}, f32[3,2,3,16]{3,1,2,0:T(2,128)S(1)}, u32[]{:S(2)}, u32[]{:S(2)}) collective-permute-start(f32[3,2,3,16]{3,1,2,0:T(2,128)S(1)} %bitcast.129), channel_id=1, source_target_pairs={{4,0},{8,4},{12,8},{16,12},{20,16},{24,20},{28,24},{5,1},{9,5},{13... | collective-permute-start | bytes 3464 | tf_op jit(solution)/shard_map/ppermute | solution.py:21
  26.6 20.2 %collective-permute-start.1 = (f32[3,2,3,128]{3,1,2,0:T(2,128)S(1)}, f32[3,2,3,128]{3,1,2,0:T(2,128)S(1)}, u32[]{:S(2)}, u32[]{:S(2)}) collective-permute-start(f32[3,2,3,128]{3,1,2,0:T(2,128)S(1)} %bitcast.134), channel_id=1, source_target_pairs={{1,0},{2,1},{3,2},{5,4},{6,5},{7,6},{9,8},{10,9},{11,10},{13,12},{... | collective-permute-start | bytes 27656 | tf_op jit(solution)/shard_map/ppermute | solution.py:21
  85.2 31.2 %all-to-all-start.1 = ((f32[64,4,6,128]{3,1,2,0:T(4,128)}), f32[64,4,6,128]{3,1,2,0:T(4,128)S(1)}, u32[]{:S(2)}, u32[]{:S(2)}) async-start(f32[64,4,6,128]{3,1,2,0:T(4,128)} %copy.123), calls=%async_computation.1 | async-start | bytes 1572864 | tf_op jit(solution)/shard_map/all_to_all | solution.py:311
  96.3 11.8 %collective-permute-start.2 = (f32[3,2,3,16]{3,1,2,0:T(2,128)S(1)}, f32[3,2,3,16]{3,1,2,0:T(2,128)S(1)}, u32[]{:S(2)}, u32[]{:S(2)}) collective-permute-start(f32[3,2,3,16]{3,1,2,0:T(2,128)S(1)} %bitcast.130), channel_id=1, source_target_pairs={{0,4},{4,8},{8,12},{12,16},{16,20},{20,24},{24,28},{1,5},{5,9},{9,... | collective-permute-start | bytes 3464 | tf_op jit(solution)/shard_map/ppermute | solution.py:21
  99.6 18.6 %collective-permute-start.3 = (f32[3,2,3,128]{3,1,2,0:T(2,128)S(1)}, f32[3,2,3,128]{3,1,2,0:T(2,128)S(1)}, u32[]{:S(2)}, u32[]{:S(2)}) collective-permute-start(f32[3,2,3,128]{3,1,2,0:T(2,128)S(1)} %bitcast.133), channel_id=1, source_target_pairs={{0,1},{1,2},{2,3},{4,5},{5,6},{6,7},{8,9},{9,10},{10,11},{12,13},{... | collective-permute-start | bytes 27656 | tf_op jit(solution)/shard_map/ppermute | solution.py:21
  116.5 1.0 copy-start.8
  116.5 1.3 %copy-start.3 = (f32[3,2,3,16,128]{4,3,2,1,0:T(8,128)S(1)}, f32[3,2,3,16,128]{4,3,2,1,0:T(8,128)}, u32[]{:S(2)}) copy-start(f32[3,2,3,16,128]{4,3,2,1,0:T(8,128)} %param.18) | copy-start | bytes 442372
  118.2 0.7 copy-start.2
  118.9 0.7 copy-start.4

commit v5 on v4

--- a/solution.py
+++ b/solution.py
@@ -279,18 +279,22 @@
     rank_within = jnp.sum((jnp.cumsum(owner_onehot, axis=0) - owner_onehot) * owner_onehot, axis=1)
     slot_index = owner_ids * capacity + rank_within
     slot_count = group_size * capacity
-    pair_targets = target_blocks[target_ids]
-    pair_seed = seed_blocks[target_ids]
-    ident = jnp.broadcast_to(
-        source_ids.astype(jnp.float32)[:, None, None], (pair_count, 1, age_here)
-    )
-    sent = jnp.concatenate([pair_targets, pair_seed, ident], axis=1)
-    outgoing = (
-        jnp.zeros((slot_count, 7, age_here), jnp.float32)
-        .at[:, 6]
-        .set(-1.0)
+    pair_of_slot = (
+        jnp.full((slot_count,), pair_count, jnp.int32)
         .at[slot_index]
-        .set(sent)
+        .set(jnp.arange(pair_count, dtype=jnp.int32))
+    )
+    block_of_slot = jnp.concatenate([target_ids, jnp.zeros((1,), jnp.int32)])[pair_of_slot]
+    id_of_slot = jnp.concatenate(
+        [source_ids.astype(jnp.float32), jnp.full((1,), -1.0, jnp.float32)]
+    )[pair_of_slot]
+    outgoing = jnp.concatenate(
+        [
+            target_blocks[block_of_slot],
+            seed_blocks[block_of_slot],
+            jnp.broadcast_to(id_of_slot[:, None, None], (slot_count, 1, age_here)),
+        ],
+        axis=1,
     )
     received = lax.all_to_all(
         outgoing.reshape(group_size, capacity, 7, age_here),

time: 120 us -> 122 us (1.017)
  other arithmetic: 4.71 us -> 6 us
    gather x2 -> x4, local copies, waits for them, and re-layouts: 1.5 us -> 5.87 us  [the longest x1 1.94 us: local(): jnp.concatenate([source_ids.astype(jnp.float32), jnp.full((1,), -1.0, jnp...]
    scatter x1, local copies, waits for them, and re-layouts: 4.3 us -> 0.97 us  [local(): pair_of_slot = jnp.full((slot_count,), pair_count, jnp.int32).at[slot_ind...]
    unnamed x22 -> x20, local copies, waits for them, and re-layouts: 4.56 us -> 3.71 us
  transfers between devices with their start and end apart: 6 -> 6, of which waited for: 4 -> 4; matrix products, arithmetic and copies ran while one was open for 7% -> 6% of each run, Pallas kernels for 0% -> 0%
where the time goes in v5:
time: 122 us; the launch traced here: 121 us
  waiting for transfers between devices  32.9 us (27%)
  starting transfers between devices  30.2 us (25%)
  Pallas kernels  28.7 us (24%)
  local copies, waits for them, and re-layouts  20.9 us (17%)
  other arithmetic  6 us (5%)
  matrix products  1.4 us (1%)
  between operations  1.23 us (1%)
    pallas_call x1, Pallas kernels, run_pairs(): pl.pallas_call(pair_kernel, grid=(number // step,), in_specs=[spec(3), sp...  28.7 us
    ppermute x4, waiting for transfers between devices, shifted_2(): lax.ppermute(value, axis, [(source, source + steps) for source in range(l...  22.6 us
    all_to_all x1, starting transfers between devices, local(): lax.all_to_all(outgoing.reshape(group_size, capacity, 7, age_here), ('tur...  13 us
    ppermute x4, starting transfers between devices, shifted_2(): lax.ppermute(value, axis, [(source, source + steps) for source in range(l...  9.07 us
    all_to_all x1, starting transfers between devices, local(): lax.all_to_all(jnp.concatenate([slot_velocity, slot_grad], axis=1).reshap...  8.13 us
    all_to_all x1, waiting for transfers between devices, local(): lax.all_to_all(jnp.concatenate([slot_velocity, slot_grad], axis=1).reshap...  8.08 us
    unnamed x20, local copies, waits for them, and re-layouts  3.71 us
    gather x2, local copies, waits for them, and re-layouts, local(): slot_payload = payload[jnp.clip(asked, 0, blocks_here - 1)]  2.65 us
  transfers between devices with their start and end apart: 6, of which 4 were waited for; matrix products, arithmetic and copies ran while one was open for 6% of the time, Pallas kernels for 0%

profile of v5, /device:TPU:1, one launch (start us, length us, event | category | flops | bytes accessed | tf_op | source)
XLA Modules:
  0.0 121.2 jit_solution(14029997457510935248)
XLA Ops:
  0.6 0.0 copy-start.2
  0.6 0.8 fusion.8
  1.4 0.2 reduce_window_sum.11
  1.6 0.8 select_reduce_fusion
  2.4 0.7 fusion.16
  3.1 1.0 scatter_custom_fusion
  4.1 0.7 pad_add_fusion.1
  4.8 1.9 %gather_fusion = s32[256]{0:T(256)S(1)} fusion(s32[129]{0:T(256)S(1)} %pad_add_fusion.1, s32[1024]{0:T(1024)S(1)} %pad_clamp_fusion.3), kind=kCustom, calls=%fused_computation | custom fusion | bytes 3072 | tf_op jit(solution)/shard_map/gather | solution.py:287
  6.8 1.0 copy.111
  7.8 0.1 copy.112
  7.9 1.0 gather_fusion.1
  8.9 1.0 gather_fusion.2
  10.0 1.9 %gather_fusion.3 = f32[256]{0:T(256)S(1)} fusion(f32[129]{0:T(256)S(1)} %pad_maximum_fusion.4, s32[1024]{0:T(1024)S(1)} %pad_clamp_fusion.3), kind=kCustom, calls=%fused_computation.3 | custom fusion | bytes 3072 | tf_op jit(solution)/shard_map/gather | solution.py:288
  11.9 0.3 broadcast_in_dim.10
  12.2 0.3 pad_maximum_fusion
  12.6 0.0 copy-start
  12.6 1.2 copy.113
  13.8 13.0 %all-to-all-start = ((f32[64,4,7,128]{3,1,2,0:T(4,128)}), f32[64,4,7,128]{3,1,2,0:T(4,128)S(1)}, u32[]{:S(2)}, u32[]{:S(2)}) async-start(f32[64,4,7,128]{3,1,2,0:T(4,128)} %copy.113), calls=%async_computation | async-start | bytes 1835008 | tf_op jit(solution)/shard_map/all_to_all | solution.py:299
  26.8 0.2 copy.116
  26.9 1.3 %collective-permute-start = (f32[3,2,3,16]{3,1,2,0:T(2,128)S(1)}, f32[3,2,3,16]{3,1,2,0:T(2,128)S(1)}, u32[]{:S(2)}, u32[]{:S(2)}) collective-permute-start(f32[3,2,3,16]{3,1,2,0:T(2,128)S(1)} %bitcast.127), channel_id=1, source_target_pairs={{4,0},{8,4},{12,8},{16,12},{20,16},{24,20},{28,24},{5,1},{9,5},{13... | collective-permute-start | bytes 3464 | tf_op jit(solution)/shard_map/ppermute | solution.py:21
  28.3 1.3 %collective-permute-start.1 = (f32[3,2,3,128]{3,1,2,0:T(2,128)S(1)}, f32[3,2,3,128]{3,1,2,0:T(2,128)S(1)}, u32[]{:S(2)}, u32[]{:S(2)}) collective-permute-start(f32[3,2,3,128]{3,1,2,0:T(2,128)S(1)} %bitcast.132), channel_id=1, source_target_pairs={{1,0},{2,1},{3,2},{5,4},{6,5},{7,6},{9,8},{10,9},{11,10},{13,12},{... | collective-permute-start | bytes 27656 | tf_op jit(solution)/shard_map/ppermute | solution.py:21
  29.6 0.1 slice_multiply_fusion
  29.7 0.1 slice.135
  29.8 0.1 copy.115
  29.9 18.1 %collective-permute-done = f32[3,2,3,16]{3,1,2,0:T(2,128)S(1)} collective-permute-done((f32[3,2,3,16]{3,1,2,0:T(2,128)S(1)}, f32[3,2,3,16]{3,1,2,0:T(2,128)S(1)}, u32[]{:S(2)}, u32[]{:S(2)}) %collective-permute-start) | collective-permute-done | bytes 1184 | tf_op jit(solution)/shard_map/ppermute | solution.py:21
  48.0 0.1 concatenate.48
  48.1 0.2 copy.118
  48.3 0.2 pad_maximum_fusion.2
  48.5 0.1 copy.121
  48.6 1.2 %concatenate.55 = f32[12,96,128]{2,0,1:T(8,128)S(1)} concatenate(f32[3,96,128]{2,0,1:T(4,128)S(1)} %bitcast.102, f32[3,96,128]{2,0,1:T(4,128)S(1)} %pad_maximum_fusion.2, f32[3,96,128]{2,0,1:T(4,128)S(1)} %bitcast.113, f32[1,96,128]{2,0,1:T(1,128)S(1)} %bitcast.123, f32[1,96,128]{2,0,1:T(1,128)S(1)} %bitcast.122, f32[1,96,128]{2,0,1:T(1,128)S(1)} %bitcast.126), dimensions={0} | concatenate | bytes 1179648 | tf_op jit(solution)/shard_map/jvp()/concatenate | solution.py:260
  49.9 2.2 %all-to-all-done = f32[64,4,7,128]{3,1,2,0:T(4,128)S(1)} async-done(((f32[64,4,7,128]{3,1,2,0:T(4,128)}), f32[64,4,7,128]{3,1,2,0:T(4,128)S(1)}, u32[]{:S(2)}, u32[]{:S(2)}) %all-to-all-start) | async-done | bytes 917536 | tf_op jit(solution)/shard_map/all_to_all | solution.py:299
  52.1 0.2 copy.114
  52.2 0.1 fusion.5
  52.4 0.9 slice_bitcast_fusion
  53.3 1.0 gather_fusion.4
  54.4 1.6 %copy.137 = f32[256,12,128]{2,0,1:T(8,128)} copy(f32[256,12,128]{2,1,0:T(8,128)S(1)} %gather_fusion.4) | data formatting | bytes 3145728 | tf_op jit(solution)/shard_map/gather | solution.py:307
  56.0 28.7 %shard_map.94 = (f32[3,256,128]{2,1,0:T(8,128)}, f32[3,256,128]{2,1,0:T(8,128)}, f32[11,256,128]{2,1,0:T(8,128)}) custom-call(f32[3,256,128]{2,1,0:T(8,128)} %get-tuple-element.57.t_ref, f32[12,256,128]{2,1,0:T(8,128)} %bitcast.100, f32[3,256,128]{2,1,0:T(8,128)} %get-tuple-element.56.c_ref), custom_call_target="tpu_custom_call" | custom-call | tf_op jit(solution)/shard_map/pallas_call | solution.py:206
  84.6 1.2 pad_maximum_fusion.1
  85.8 1.0 copy.123
  86.8 8.1 %all-to-all-start.1 = ((f32[64,4,6,128]{3,1,2,0:T(4,128)}), f32[64,4,6,128]{3,1,2,0:T(4,128)S(1)}, u32[]{:S(2)}, u32[]{:S(2)}) async-start(f32[64,4,6,128]{3,1,2,0:T(4,128)} %copy.123), calls=%async_computation.1 | async-start | bytes 1572864 | tf_op jit(solution)/shard_map/all_to_all | solution.py:315
  95.0 1.8 %copy.132 = f32[256,11,128]{0,2,1:T(8,128)S(1)} copy(f32[256,11,128]{2,0,1:T(8,128)} %bitcast.110) | data formatting | bytes 2883584
  96.8 0.8 fusion.1
  97.7 0.1 split.56
  97.8 0.2 copy.128
  98.0 3.3 %collective-permute-start.2 = (f32[3,2,3,16]{3,1,2,0:T(2,128)S(1)}, f32[3,2,3,16]{3,1,2,0:T(2,128)S(1)}, u32[]{:S(2)}, u32[]{:S(2)}) collective-permute-start(f32[3,2,3,16]{3,1,2,0:T(2,128)S(1)} %bitcast.128), channel_id=1, source_target_pairs={{0,4},{4,8},{8,12},{12,16},{16,20},{20,24},{24,28},{1,5},{5,9},{9,... | collective-permute-start | bytes 3464 | tf_op jit(solution)/shard_map/ppermute | solution.py:21
  101.3 3.2 %collective-permute-start.3 = (f32[3,2,3,128]{3,1,2,0:T(2,128)S(1)}, f32[3,2,3,128]{3,1,2,0:T(2,128)S(1)}, u32[]{:S(2)}, u32[]{:S(2)}) collective-permute-start(f32[3,2,3,128]{3,1,2,0:T(2,128)S(1)} %bitcast.131), channel_id=1, source_target_pairs={{0,1},{1,2},{2,3},{4,5},{5,6},{6,7},{8,9},{9,10},{10,11},{12,13},{... | collective-permute-start | bytes 27656 | tf_op jit(solution)/shard_map/ppermute | solution.py:21
  104.5 0.1 broadcast_multiply_fusion.1
  104.6 0.6 pad_add_fusion
  105.2 4.5 %collective-permute-done.2 = f32[3,2,3,16]{3,1,2,0:T(2,128)S(1)} collective-permute-done((f32[3,2,3,16]{3,1,2,0:T(2,128)S(1)}, f32[3,2,3,16]{3,1,2,0:T(2,128)S(1)}, u32[]{:S(2)}, u32[]{:S(2)}) %collective-permute-start.2) | collective-permute-done | bytes 1184 | tf_op jit(solution)/shard_map/ppermute | solution.py:21
  109.8 0.2 copy.129
  109.9 8.1 %all-to-all-done.1 = f32[64,4,6,128]{3,1,2,0:T(4,128)S(1)} async-done(((f32[64,4,6,128]{3,1,2,0:T(4,128)}), f32[64,4,6,128]{3,1,2,0:T(4,128)S(1)}, u32[]{:S(2)}, u32[]{:S(2)}) %all-to-all-start.1) | async-done | bytes 786464 | tf_op jit(solution)/shard_map/all_to_all | solution.py:315
  118.0 0.1 copy.124
  118.2 0.8 gather_fusion.5
  119.0 0.1 fusion.22
  119.1 0.1 copy.127
  119.2 0.3 fusion.2
  119.5 0.1 add_add_fusion
  119.7 0.2 scatter-add.11
  119.9 0.1 scatter-add.14
  119.9 0.0 copy-start.1
  119.9 0.1 copy.125
  120.1 0.3 convolution_multiply_fusion
  120.4 0.2 copy-done.1
  120.6 0.7 copy-done.4
  (42 shorter events, 0.3 us)
Async XLA Ops:
  0.6 7.1 %copy-start.2 = (f32[3,2,3,16,128]{4,3,2,1,0:T(8,128)S(1)}, f32[3,2,3,16,128]{4,3,2,1,0:T(8,128)}, u32[]{:S(2)}) copy-start(f32[3,2,3,16,128]{4,3,2,1,0:T(8,128)} %param.16) | copy-start | bytes 442372
  6.7 3.2 %copy-start.8 = (s32[1,1,1,128]{3,2,1,0:T(1,128)S(1)}, s32[1,1,1,128]{3,2,1,0:T(1,128)}, u32[]{:S(2)}) copy-start(s32[1,1,1,128]{3,2,1,0:T(1,128)} %param.19) | copy-start | bytes 1540
  12.6 14.2 %copy-start = (f32[3,2,3,16,128]{4,3,2,1,0:T(8,128)S(1)}, f32[3,2,3,16,128]{4,3,2,1,0:T(8,128)}, u32[]{:S(2)}) copy-start(f32[3,2,3,16,128]{4,3,2,1,0:T(8,128)} %param.13) | copy-start | bytes 442372
  12.6 17.0 %copy-start.5 = (f32[2,2,3,16,128]{4,3,2,1,0:T(8,128)S(1)}, f32[2,2,3,16,128]{4,3,2,1,0:T(8,128)}, u32[]{:S(2)}) copy-start(f32[2,2,3,16,128]{4,3,2,1,0:T(8,128)} %param.14) | copy-start | bytes 294916
  13.8 38.3 %all-to-all-start = ((f32[64,4,7,128]{3,1,2,0:T(4,128)}), f32[64,4,7,128]{3,1,2,0:T(4,128)S(1)}, u32[]{:S(2)}, u32[]{:S(2)}) async-start(f32[64,4,7,128]{3,1,2,0:T(4,128)} %copy.113), calls=%async_computation | async-start | bytes 1835008 | tf_op jit(solution)/shard_map/all_to_all | solution.py:299
  26.8 21.9 %copy-start.6 = (f32[2,3,16,128]{3,2,1,0:T(8,128)S(1)}, f32[2,3,16,128]{3,2,1,0:T(8,128)}, u32[]{:S(2)}) copy-start(f32[2,3,16,128]{3,2,1,0:T(8,128)} %param.15) | copy-start | bytes 147460
  26.9 21.1 %collective-permute-start = (f32[3,2,3,16]{3,1,2,0:T(2,128)S(1)}, f32[3,2,3,16]{3,1,2,0:T(2,128)S(1)}, u32[]{:S(2)}, u32[]{:S(2)}) collective-permute-start(f32[3,2,3,16]{3,1,2,0:T(2,128)S(1)} %bitcast.127), channel_id=1, source_target_pairs={{4,0},{8,4},{12,8},{16,12},{20,16},{24,20},{28,24},{5,1},{9,5},{13... | collective-permute-start | bytes 3464 | tf_op jit(solution)/shard_map/ppermute | solution.py:21
  28.3 20.2 %collective-permute-start.1 = (f32[3,2,3,128]{3,1,2,0:T(2,128)S(1)}, f32[3,2,3,128]{3,1,2,0:T(2,128)S(1)}, u32[]{:S(2)}, u32[]{:S(2)}) collective-permute-start(f32[3,2,3,128]{3,1,2,0:T(2,128)S(1)} %bitcast.132), channel_id=1, source_target_pairs={{1,0},{2,1},{3,2},{5,4},{6,5},{7,6},{9,8},{10,9},{11,10},{13,12},{... | collective-permute-start | bytes 27656 | tf_op jit(solution)/shard_map/ppermute | solution.py:21
  86.8 31.2 %all-to-all-start.1 = ((f32[64,4,6,128]{3,1,2,0:T(4,128)}), f32[64,4,6,128]{3,1,2,0:T(4,128)S(1)}, u32[]{:S(2)}, u32[]{:S(2)}) async-start(f32[64,4,6,128]{3,1,2,0:T(4,128)} %copy.123), calls=%async_computation.1 | async-start | bytes 1572864 | tf_op jit(solution)/shard_map/all_to_all | solution.py:315
  98.0 11.8 %collective-permute-start.2 = (f32[3,2,3,16]{3,1,2,0:T(2,128)S(1)}, f32[3,2,3,16]{3,1,2,0:T(2,128)S(1)}, u32[]{:S(2)}, u32[]{:S(2)}) collective-permute-start(f32[3,2,3,16]{3,1,2,0:T(2,128)S(1)} %bitcast.128), channel_id=1, source_target_pairs={{0,4},{4,8},{8,12},{12,16},{16,20},{20,24},{24,28},{1,5},{5,9},{9,... | collective-permute-start | bytes 3464 | tf_op jit(solution)/shard_map/ppermute | solution.py:21
  101.3 18.6 %collective-permute-start.3 = (f32[3,2,3,128]{3,1,2,0:T(2,128)S(1)}, f32[3,2,3,128]{3,1,2,0:T(2,128)S(1)}, u32[]{:S(2)}, u32[]{:S(2)}) collective-permute-start(f32[3,2,3,128]{3,1,2,0:T(2,128)S(1)} %bitcast.131), channel_id=1, source_target_pairs={{0,1},{1,2},{2,3},{4,5},{5,6},{6,7},{8,9},{9,10},{10,11},{12,13},{... | collective-permute-start | bytes 27656 | tf_op jit(solution)/shard_map/ppermute | solution.py:21
  118.2 1.0 copy-start.7
  118.2 1.3 %copy-start.3 = (f32[3,2,3,16,128]{4,3,2,1,0:T(8,128)S(1)}, f32[3,2,3,16,128]{4,3,2,1,0:T(8,128)}, u32[]{:S(2)}) copy-start(f32[3,2,3,16,128]{4,3,2,1,0:T(8,128)} %param.16) | copy-start | bytes 442372
  119.9 0.7 copy-start.1
  120.6 0.7 copy-start.4

commit v6 on v4

--- a/solution.py
+++ b/solution.py
@@ -230,6 +230,14 @@
     return summed.reshape((rows,) + values.shape[1:])
 
 
+def staged_all_to_all(slots):
+    turb_count = lax.axis_size("turb")
+    age_count = lax.axis_size("age")
+    split = slots.reshape((turb_count, age_count, -1) + slots.shape[1:])
+    split = lax.all_to_all(split, "age", split_axis=1, concat_axis=1, tiled=True)
+    return lax.all_to_all(split, "turb", split_axis=0, concat_axis=0, tiled=True)
+
+
 def local(positions, strengths, core_radius, adjoint_seed, pair_target, pair_owner, pair_source):
     shape_here = positions.shape
     station_here = shape_here[3]
@@ -292,13 +300,7 @@
         .at[slot_index]
         .set(sent)
     )
-    received = lax.all_to_all(
-        outgoing.reshape(group_size, capacity, 7, age_here),
-        ("turb", "age"),
-        split_axis=0,
-        concat_axis=0,
-        tiled=True,
-    ).reshape(slot_count, 7, age_here)
+    received = staged_all_to_all(outgoing).reshape(slot_count, 7, age_here)
     asked = received[:, 6, 0].astype(jnp.int32)
     slot_payload = payload[jnp.clip(asked, 0, blocks_here - 1)]
     slot_velocity, slot_grad, payload_terms = run_pairs(
@@ -308,14 +310,8 @@
         [payload_terms, jnp.zeros_like(payload_terms[:, :1])], axis=1
     )
     payload_grad = onehot_sum(asked, blocks_here, payload_terms)
-    answered = lax.all_to_all(
-        jnp.concatenate([slot_velocity, slot_grad], axis=1).reshape(
-            group_size, capacity, 6, age_here
-        ),
-        ("turb", "age"),
-        split_axis=0,
-        concat_axis=0,
-        tiled=True,
+    answered = staged_all_to_all(
+        jnp.concatenate([slot_velocity, slot_grad], axis=1)
     ).reshape(slot_count, 6, age_here)[slot_index]
     velocity = onehot_sum(target_ids, blocks_here, answered[:, 0:3])
     target_grad = onehot_sum(target_ids, blocks_here, answered[:, 3:6])

time: 120 us -> 149 us (1.24)
  blocking collectives: 0 us -> 33.6 us
  starting transfers between devices: 30.2 us -> 21.8 us
  waiting for transfers between devices: 32.9 us -> 34.9 us
  local copies, waits for them, and re-layouts: 20.5 us -> 22.3 us
    all_to_all x0 -> x1, blocking collectives: none -> 33.6 us  [staged_all_to_all(): lax.all_to_all(split, 'age', split_axis=1, concat_axis=1, tiled=True)]
    all_to_all x2 -> x3, waiting for transfers between devices: 10.3 us -> 32.3 us  [the longest x1 20.8 us: staged_all_to_all(): lax.all_to_all(split, 'age', split_axis=1, concat_axis=1, tiled=True)]
    ppermute x4, waiting for transfers between devices: 22.6 us -> 2.62 us  [shifted_2(): lax.ppermute(value, axis, [(source, source + steps) for source in range(l...]
    all_to_all x2 -> x3, starting transfers between devices: 21.1 us -> 13.8 us  [the longest x2 10.3 us: staged_all_to_all(): lax.all_to_all(split, 'turb', split_axis=0, concat_axis=0, tiled=True)]
    all_to_all x2 -> x4, local copies, waits for them, and re-layouts: 0.31 us -> 2.86 us  [the longest x2 2.33 us: staged_all_to_all(): lax.all_to_all(split, 'age', split_axis=1, concat_axis=1, tiled=True)]
  transfers between devices with their start and end apart: 6 -> 7, of which waited for: 4 -> 5; matrix products, arithmetic and copies ran while one was open for 7% -> 5% of each run, Pallas kernels for 0% -> 0%
where the time goes in v6:
time: 149 us
  waiting for transfers between devices  34.9 us (23%)
  blocking collectives  33.6 us (23%)
  Pallas kernels  28.7 us (19%)
  local copies, waits for them, and re-layouts  22.3 us (15%)
  starting transfers between devices  21.8 us (15%)
  other arithmetic  4.71 us (3%)
    all_to_all x1, blocking collectives, staged_all_to_all(): lax.all_to_all(split, 'age', split_axis=1, concat_axis=1, tiled=True)  33.6 us
    pallas_call x1, Pallas kernels, run_pairs(): pl.pallas_call(pair_kernel, grid=(number // step,), in_specs=[spec(3), sp...  28.7 us
    all_to_all x1, waiting for transfers between devices, staged_all_to_all(): lax.all_to_all(split, 'age', split_axis=1, concat_axis=1, tiled=True)  20.8 us
    all_to_all x2, waiting for transfers between devices, staged_all_to_all(): lax.all_to_all(split, 'turb', split_axis=0, concat_axis=0, tiled=True)  11.5 us
    all_to_all x2, starting transfers between devices, staged_all_to_all(): lax.all_to_all(split, 'turb', split_axis=0, concat_axis=0, tiled=True)  10.3 us
    ppermute x4, starting transfers between devices, shifted_2(): lax.ppermute(value, axis, [(source, source + steps) for source in range(l...  8 us
    unnamed x22, local copies, waits for them, and re-layouts  4.55 us
    scatter x1, local copies, waits for them, and re-layouts, local(): outgoing = jnp.zeros((slot_count, 7, age_here), jnp.float32).at[:, 6].set...  4.3 us
  transfers between devices with their start and end apart: 7, of which 5 were waited for; matrix products, arithmetic and copies ran while one was open for 5% of the time, Pallas kernels for 0%

profile of v6, /device:TPU:1, one launch (start us, length us, event | category | flops | bytes accessed | tf_op | source)
XLA Modules:
  0.0 148.6 jit_solution(15365702536497953288)
XLA Ops:
  0.7 1.0 copy.115
  1.7 0.7 fusion.17
  2.3 0.9 broadcast_multiply_fusion
  3.3 0.1 copy.116
  3.4 0.8 gather_fusion
  4.1 0.8 gather_fusion.1
  4.9 0.1 fusion.8
  5.0 0.2 reduce_window_sum.11
  5.2 0.2 select_reduce_fusion
  5.4 0.2 broadcast_in_dim.4
  5.6 0.2 pad_maximum_fusion.1
  5.8 0.8 copy-done
  6.6 4.3 %scatter_fusion = f32[256,7,128]{2,1,0:T(8,128)S(1)} fusion(f32[256,7,128]{2,1,0:T(8,128)S(1)} %copy-done, s32[128]{0:T(128)S(1)} %fusion.16, f32[128,7,128]{2,1,0:T(8,128)S(1)} %pad_maximum_fusion.1), kind=kCustom, calls=%fused_computation.4 | custom fusion | bytes 1376768 | tf_op jit(solution)/shard_map/scatter | solution.py:301
  10.9 0.2 copy.117
  11.2 33.6 %all_to_all.20 = f32[8,8,4,7,128]{4,2,0,3,1:T(4,128)S(1)} all-to-all(f32[8,8,4,7,128]{4,2,0,3,1:T(4,128)S(1)} %copy.117), channel_id=1, replica_groups=mesh['turb'=8,'age'=8,'span'=4] {'age'}, dimensions={1} | all-to-all | bytes 1835008 | tf_op jit(solution)/shard_map/all_to_all | solution.py:237
  44.8 1.2 copy.118
  46.0 6.4 %all-to-all-start.1 = ((f32[8,8,4,7,128]{4,2,1,3,0:T(4,128)}), f32[8,8,4,7,128]{4,2,1,3,0:T(4,128)S(1)}, u32[]{:S(2)}, u32[]{:S(2)}) async-start(f32[8,8,4,7,128]{4,2,1,3,0:T(4,128)} %copy.118), calls=%async_computation.1 | async-start | bytes 1835008 | tf_op jit(solution)/shard_map/all_to_all | solution.py:238
  52.3 0.2 copy.121
  52.5 1.3 collective-permute-start
  53.8 1.3 collective-permute-start.1
  55.2 0.1 slice_multiply_fusion
  55.3 0.1 slice.154
  55.4 0.1 copy.120
  55.5 1.7 %collective-permute-done = f32[3,2,3,16]{3,1,2,0:T(2,128)S(1)} collective-permute-done((f32[3,2,3,16]{3,1,2,0:T(2,128)S(1)}, f32[3,2,3,16]{3,1,2,0:T(2,128)S(1)}, u32[]{:S(2)}, u32[]{:S(2)}) %collective-permute-start) | collective-permute-done | bytes 1184 | tf_op jit(solution)/shard_map/ppermute | solution.py:21
  57.2 0.1 concatenate.42
  57.3 0.2 copy.123
  57.5 0.2 pad_maximum_fusion.2
  57.6 0.9 collective-permute-done.1
  58.6 0.1 copy.126
  58.7 1.2 concatenate.49
  59.9 6.0 %all-to-all-done.1 = f32[8,8,4,7,128]{4,2,1,3,0:T(4,128)S(1)} async-done(((f32[8,8,4,7,128]{4,2,1,3,0:T(4,128)}), f32[8,8,4,7,128]{4,2,1,3,0:T(4,128)S(1)}, u32[]{:S(2)}, u32[]{:S(2)}) %all-to-all-start.1) | async-done | bytes 917536 | tf_op jit(solution)/shard_map/all_to_all | solution.py:238
  65.9 0.1 copy.119
  66.0 0.1 fusion.5
  66.1 0.9 slice_bitcast_fusion
  67.1 1.0 gather_fusion.2
  68.1 1.7 %copy.143 = f32[256,12,128]{2,0,1:T(8,128)} copy(f32[256,12,128]{2,1,0:T(8,128)S(1)} %gather_fusion.2) | data formatting | bytes 3145728 | tf_op jit(solution)/shard_map/gather | solution.py:305
  69.8 28.7 %shard_map.94 = (f32[3,256,128]{2,1,0:T(8,128)}, f32[3,256,128]{2,1,0:T(8,128)}, f32[11,256,128]{2,1,0:T(8,128)}) custom-call(f32[3,256,128]{2,1,0:T(8,128)} %get-tuple-element.69.t_ref, f32[12,256,128]{2,1,0:T(8,128)} %bitcast.103, f32[3,256,128]{2,1,0:T(8,128)} %get-tuple-element.68.c_ref), custom_call_target="tpu_custom_call" | custom-call | tf_op jit(solution)/shard_map/pallas_call | solution.py:206
  98.5 1.2 pad_maximum_fusion
  99.6 1.1 copy.128
  100.8 3.5 %all-to-all-start.2 = ((f32[8,8,4,6,128]{4,2,0,3,1:T(4,128)}), f32[8,8,4,6,128]{4,2,0,3,1:T(4,128)S(1)}, u32[]{:S(2)}, u32[]{:S(2)}) async-start(f32[8,8,4,6,128]{4,2,0,3,1:T(4,128)} %copy.128), calls=%async_computation.2 | async-start | bytes 1572864 | tf_op jit(solution)/shard_map/all_to_all | solution.py:237
  104.3 1.8 %copy.138 = f32[256,11,128]{0,2,1:T(8,128)S(1)} copy(f32[256,11,128]{2,0,1:T(8,128)} %bitcast.111) | data formatting | bytes 2883584
  106.1 0.8 fusion.1
  107.0 20.8 %all-to-all-done.2 = f32[8,8,4,6,128]{4,2,0,3,1:T(4,128)S(1)} async-done(((f32[8,8,4,6,128]{4,2,0,3,1:T(4,128)}), f32[8,8,4,6,128]{4,2,0,3,1:T(4,128)S(1)}, u32[]{:S(2)}, u32[]{:S(2)}) %all-to-all-start.2) | async-done | bytes 786464 | tf_op jit(solution)/shard_map/all_to_all | solution.py:237
  127.8 1.1 copy.129
  128.9 3.9 %all-to-all-start.3 = ((f32[8,8,4,6,128]{4,2,1,3,0:T(4,128)}), f32[8,8,4,6,128]{4,2,1,3,0:T(4,128)S(1)}, u32[]{:S(2)}, u32[]{:S(2)}) async-start(f32[8,8,4,6,128]{4,2,1,3,0:T(4,128)} %copy.129), calls=%async_computation.3 | async-start | bytes 1572864 | tf_op jit(solution)/shard_map/all_to_all | solution.py:238
  132.9 0.1 split.56
  133.0 0.2 copy.134
  133.2 2.2 %collective-permute-start.2 = (f32[3,2,3,16]{3,1,2,0:T(2,128)S(1)}, f32[3,2,3,16]{3,1,2,0:T(2,128)S(1)}, u32[]{:S(2)}, u32[]{:S(2)}) collective-permute-start(f32[3,2,3,16]{3,1,2,0:T(2,128)S(1)} %bitcast.130), channel_id=1, source_target_pairs={{0,4},{4,8},{8,12},{12,16},{16,20},{20,24},{24,28},{1,5},{5,9},{9,... | collective-permute-start | bytes 3464 | tf_op jit(solution)/shard_map/ppermute | solution.py:21
  135.4 3.2 %collective-permute-start.3 = (f32[3,2,3,128]{3,1,2,0:T(2,128)S(1)}, f32[3,2,3,128]{3,1,2,0:T(2,128)S(1)}, u32[]{:S(2)}, u32[]{:S(2)}) collective-permute-start(f32[3,2,3,128]{3,1,2,0:T(2,128)S(1)} %bitcast.133), channel_id=1, source_target_pairs={{0,1},{1,2},{2,3},{4,5},{5,6},{6,7},{8,9},{9,10},{10,11},{12,13},{... | collective-permute-start | bytes 27656 | tf_op jit(solution)/shard_map/ppermute | solution.py:21
  138.7 0.1 broadcast_multiply_fusion.1
  138.7 0.6 pad_add_fusion
  139.4 0.2 copy.135
  139.6 5.5 %all-to-all-done.3 = f32[8,8,4,6,128]{4,2,1,3,0:T(4,128)S(1)} async-done(((f32[8,8,4,6,128]{4,2,1,3,0:T(4,128)}), f32[8,8,4,6,128]{4,2,1,3,0:T(4,128)S(1)}, u32[]{:S(2)}, u32[]{:S(2)}) %all-to-all-start.3) | async-done | bytes 786464 | tf_op jit(solution)/shard_map/all_to_all | solution.py:238
  145.1 0.5 copy.130
  145.6 0.8 gather_fusion.3
  146.3 0.1 fusion.21
  146.4 0.1 copy.133
  146.6 0.3 fusion.2
  146.9 0.1 add_add_fusion
  147.0 0.2 scatter-add.11
  147.3 0.1 copy.131
  147.4 0.3 convolution_multiply_fusion
  147.8 0.2 copy-done.2
  148.0 0.7 copy-done.4
  (42 shorter events, 0.3 us)
Async XLA Ops:
  0.6 4.3 %copy-start.9 = (s32[1,1,1,128]{3,2,1,0:T(1,128)S(1)}, s32[1,1,1,128]{3,2,1,0:T(1,128)}, u32[]{:S(2)}) copy-start(s32[1,1,1,128]{3,2,1,0:T(1,128)} %param.21) | copy-start | bytes 1540
  0.6 4.3 %copy-start.7 = (s32[1,1,1,128]{3,2,1,0:T(1,128)S(1)}, s32[1,1,1,128]{3,2,1,0:T(1,128)}, u32[]{:S(2)}) copy-start(s32[1,1,1,128]{3,2,1,0:T(1,128)} %param.20) | copy-start | bytes 1540
  5.4 1.2 copy-start
  44.8 7.6 %copy-start.1 = (f32[3,2,3,16,128]{4,3,2,1,0:T(8,128)S(1)}, f32[3,2,3,16,128]{4,3,2,1,0:T(8,128)}, u32[]{:S(2)}) copy-start(f32[3,2,3,16,128]{4,3,2,1,0:T(8,128)} %param.15) | copy-start | bytes 442372
  44.8 10.4 %copy-start.5 = (f32[2,2,3,16,128]{4,3,2,1,0:T(8,128)S(1)}, f32[2,2,3,16,128]{4,3,2,1,0:T(8,128)}, u32[]{:S(2)}) copy-start(f32[2,2,3,16,128]{4,3,2,1,0:T(8,128)} %param.16) | copy-start | bytes 294916
  46.0 19.9 %all-to-all-start.1 = ((f32[8,8,4,7,128]{4,2,1,3,0:T(4,128)}), f32[8,8,4,7,128]{4,2,1,3,0:T(4,128)S(1)}, u32[]{:S(2)}, u32[]{:S(2)}) async-start(f32[8,8,4,7,128]{4,2,1,3,0:T(4,128)} %copy.118), calls=%async_computation.1 | async-start | bytes 1835008 | tf_op jit(solution)/shard_map/all_to_all | solution.py:238
  52.3 6.4 %copy-start.6 = (f32[2,3,16,128]{3,2,1,0:T(8,128)S(1)}, f32[2,3,16,128]{3,2,1,0:T(8,128)}, u32[]{:S(2)}) copy-start(f32[2,3,16,128]{3,2,1,0:T(8,128)} %param.17) | copy-start | bytes 147460
  52.5 4.7 %collective-permute-start = (f32[3,2,3,16]{3,1,2,0:T(2,128)S(1)}, f32[3,2,3,16]{3,1,2,0:T(2,128)S(1)}, u32[]{:S(2)}, u32[]{:S(2)}) collective-permute-start(f32[3,2,3,16]{3,1,2,0:T(2,128)S(1)} %bitcast.129), channel_id=1, source_target_pairs={{4,0},{8,4},{12,8},{16,12},{20,16},{24,20},{28,24},{5,1},{9,5},{13... | collective-permute-start | bytes 3464 | tf_op jit(solution)/shard_map/ppermute | solution.py:21
  53.8 4.7 %collective-permute-start.1 = (f32[3,2,3,128]{3,1,2,0:T(2,128)S(1)}, f32[3,2,3,128]{3,1,2,0:T(2,128)S(1)}, u32[]{:S(2)}, u32[]{:S(2)}) collective-permute-start(f32[3,2,3,128]{3,1,2,0:T(2,128)S(1)} %bitcast.134), channel_id=1, source_target_pairs={{1,0},{2,1},{3,2},{5,4},{6,5},{7,6},{9,8},{10,9},{11,10},{13,12},{... | collective-permute-start | bytes 27656 | tf_op jit(solution)/shard_map/ppermute | solution.py:21
  100.8 27.0 %all-to-all-start.2 = ((f32[8,8,4,6,128]{4,2,0,3,1:T(4,128)}), f32[8,8,4,6,128]{4,2,0,3,1:T(4,128)S(1)}, u32[]{:S(2)}, u32[]{:S(2)}) async-start(f32[8,8,4,6,128]{4,2,0,3,1:T(4,128)} %copy.128), calls=%async_computation.2 | async-start | bytes 1572864 | tf_op jit(solution)/shard_map/all_to_all | solution.py:237
  128.9 16.1 %all-to-all-start.3 = ((f32[8,8,4,6,128]{4,2,1,3,0:T(4,128)}), f32[8,8,4,6,128]{4,2,1,3,0:T(4,128)S(1)}, u32[]{:S(2)}, u32[]{:S(2)}) async-start(f32[8,8,4,6,128]{4,2,1,3,0:T(4,128)} %copy.129), calls=%async_computation.3 | async-start | bytes 1572864 | tf_op jit(solution)/shard_map/all_to_all | solution.py:238
  133.2 6.2 %collective-permute-start.2 = (f32[3,2,3,16]{3,1,2,0:T(2,128)S(1)}, f32[3,2,3,16]{3,1,2,0:T(2,128)S(1)}, u32[]{:S(2)}, u32[]{:S(2)}) collective-permute-start(f32[3,2,3,16]{3,1,2,0:T(2,128)S(1)} %bitcast.130), channel_id=1, source_target_pairs={{0,4},{4,8},{8,12},{12,16},{16,20},{20,24},{24,28},{1,5},{5,9},{9,... | collective-permute-start | bytes 3464 | tf_op jit(solution)/shard_map/ppermute | solution.py:21
  135.4 11.7 %collective-permute-start.3 = (f32[3,2,3,128]{3,1,2,0:T(2,128)S(1)}, f32[3,2,3,128]{3,1,2,0:T(2,128)S(1)}, u32[]{:S(2)}, u32[]{:S(2)}) collective-permute-start(f32[3,2,3,128]{3,1,2,0:T(2,128)S(1)} %bitcast.133), channel_id=1, source_target_pairs={{0,1},{1,2},{2,3},{4,5},{5,6},{6,7},{8,9},{9,10},{10,11},{12,13},{... | collective-permute-start | bytes 27656 | tf_op jit(solution)/shard_map/ppermute | solution.py:21
  145.5 1.0 copy-start.8
  145.6 1.3 copy-start.3
  147.3 0.7 copy-start.2
  148.0 0.7 copy-start.4

commit v7 on v4

--- a/solution.py
+++ b/solution.py
@@ -172,53 +172,44 @@
     return velocity, grad_target, grad_rows
 
 
-def pair_kernel(t_ref, s_ref, c_ref, v_ref, gt_ref, gs_ref):
+def pair_kernel(t_ref, s_ref, v_ref, gs_ref):
     age_count = t_ref.shape[-1]
     lane = lax.broadcasted_iota(jnp.int32, (GROUP_PAIRS, age_count), 1)
 
     def body(group, carry):
         at = pl.ds(pl.multiple_of(group * GROUP_PAIRS, GROUP_PAIRS), GROUP_PAIRS)
-        target = [t_ref[i, at, :] for i in range(3)]
-        cotangent = [c_ref[i, at, :] for i in range(3)]
-        rows = [s_ref[i, at, :] for i in range(12)]
+        target = [t_ref[at, i, :] for i in range(3)]
+        cotangent = [t_ref[at, 3 + i, :] for i in range(3)]
+        rows = [s_ref[at, i, :] for i in range(12)]
         velocity, grad_target, grad_rows = pair_group(target, cotangent, rows, lane)
         for i in range(3):
-            v_ref[i, at, :] = velocity[i]
-            gt_ref[i, at, :] = grad_target[i]
+            v_ref[at, i, :] = velocity[i]
+            v_ref[at, 3 + i, :] = grad_target[i]
         for i in range(11):
-            gs_ref[i, at, :] = grad_rows[i]
+            gs_ref[at, i, :] = grad_rows[i]
         return carry
 
-    lax.fori_loop(0, t_ref.shape[1] // GROUP_PAIRS, body, 0)
-
-
-def run_pairs(targets, payload, cotangent):
-    number = targets.shape[0]
-    age_count = targets.shape[-1]
+    lax.fori_loop(0, t_ref.shape[0] // GROUP_PAIRS, body, 0)
+
+
+def run_pairs(received, payload):
+    number = received.shape[0]
+    age_count = received.shape[-1]
     step = min(number, BLOCK_PAIRS)
 
     def spec(rows):
-        return pl.BlockSpec((rows, step, age_count), lambda i: (0, i, 0))
-
-    t_rows = jnp.transpose(targets, (1, 0, 2))
-    s_rows = jnp.transpose(payload, (1, 0, 2))
-    c_rows = jnp.transpose(cotangent, (1, 0, 2))
-    velocity, grad_targets, grad_payload = pl.pallas_call(
+        return pl.BlockSpec((step, rows, age_count), lambda i: (i, 0, 0))
+
+    return pl.pallas_call(
         pair_kernel,
         grid=(number // step,),
-        in_specs=[spec(3), spec(12), spec(3)],
-        out_specs=[spec(3), spec(3), spec(11)],
+        in_specs=[spec(received.shape[1]), spec(12)],
+        out_specs=[spec(6), spec(11)],
         out_shape=[
-            jax.ShapeDtypeStruct((3, number, age_count), jnp.float32),
-            jax.ShapeDtypeStruct((3, number, age_count), jnp.float32),
-            jax.ShapeDtypeStruct((11, number, age_count), jnp.float32),
+            jax.ShapeDtypeStruct((number, 6, age_count), jnp.float32),
+            jax.ShapeDtypeStruct((number, 11, age_count), jnp.float32),
         ],
-    )(t_rows, s_rows, c_rows)
-    return (
-        jnp.transpose(velocity, (1, 0, 2)),
-        jnp.transpose(grad_targets, (1, 0, 2)),
-        jnp.transpose(grad_payload, (1, 0, 2)),
-    )
+    )(received, payload)
 
 
 def onehot_sum(indices, rows, values):
@@ -301,15 +292,13 @@
     ).reshape(slot_count, 7, age_here)
     asked = received[:, 6, 0].astype(jnp.int32)
     slot_payload = payload[jnp.clip(asked, 0, blocks_here - 1)]
-    slot_velocity, slot_grad, payload_terms = run_pairs(
-        received[:, 0:3], slot_payload, received[:, 3:6]
-    )
+    slot_answer, payload_terms = run_pairs(received, slot_payload)
     payload_terms = jnp.concatenate(
         [payload_terms, jnp.zeros_like(payload_terms[:, :1])], axis=1
     )
     payload_grad = onehot_sum(asked, blocks_here, payload_terms)
     answered = lax.all_to_all(
-        jnp.concatenate([slot_velocity, slot_grad], axis=1).reshape(
+        slot_answer.reshape(
             group_size, capacity, 6, age_here
         ),
         ("turb", "age"),

time: 120 us -> 136 us (1.13)
  other arithmetic: 4.71 us -> 13.9 us
  Pallas kernels: 28.6 us -> 35.8 us
    convert_element_type x1, other arithmetic: 0.15 us -> 9.14 us  [local(): asked = received[:, 6, 0].astype(jnp.int32)]
    pallas_call x1, Pallas kernels: 28.6 us -> 35.8 us  [run_pairs(): pl.pallas_call(pair_kernel, grid=(number // step,), in_specs=[spec(receiv...]
    reshape x1 -> x2, local copies, waits for them, and re-layouts: 1.02 us -> 2.79 us  [the longest x1 2.31 us: local(): slot_answer.reshape(group_size, capacity, 6, age_here)]
    unnamed x22 -> x24, local copies, waits for them, and re-layouts: 4.56 us -> 3.77 us
where the time goes in v7:
time: 136 us
  Pallas kernels  35.8 us (26%)
  waiting for transfers between devices  32 us (24%)
  starting transfers between devices  30.5 us (22%)
  local copies, waits for them, and re-layouts  20.9 us (15%)
  other arithmetic  13.9 us (10%)
  matrix products  1.4 us (1%)
    pallas_call x1, Pallas kernels, run_pairs(): pl.pallas_call(pair_kernel, grid=(number // step,), in_specs=[spec(receiv...  35.8 us
    ppermute x4, waiting for transfers between devices, shifted_2(): lax.ppermute(value, axis, [(source, source + steps) for source in range(l...  21.7 us
    all_to_all x1, starting transfers between devices, local(): lax.all_to_all(outgoing.reshape(group_size, capacity, 7, age_here), ('tur...  13.1 us
    ppermute x4, starting transfers between devices, shifted_2(): lax.ppermute(value, axis, [(source, source + steps) for source in range(l...  9.25 us
    convert_element_type x1, other arithmetic, local(): asked = received[:, 6, 0].astype(jnp.int32)  9.14 us
    all_to_all x1, starting transfers between devices, local(): lax.all_to_all(slot_answer.reshape(group_size, capacity, 6, age_here), ('...  8.13 us
    all_to_all x1, waiting for transfers between devices, local(): lax.all_to_all(slot_answer.reshape(group_size, capacity, 6, age_here), ('...  8.08 us
    scatter x1, local copies, waits for them, and re-layouts, local(): outgoing = jnp.zeros((slot_count, 7, age_here), jnp.float32).at[:, 6].set...  4.3 us
  transfers between devices with their start and end apart: 6, of which 4 were waited for; matrix products, arithmetic and copies ran while one was open for 7% of the time, Pallas kernels for 0%

profile of v7, /device:TPU:1, one launch (start us, length us, event | category | flops | bytes accessed | tf_op | source)
XLA Modules:
  0.0 135.7 jit_solution(7335852518511149614)
XLA Ops:
  0.6 0.0 copy-start.9
  0.6 1.0 copy.154
  1.7 0.7 fusion.17
  2.3 0.9 broadcast_multiply_fusion
  3.3 0.1 copy.155
  3.4 0.8 gather_fusion
  4.1 0.0 copy-start
  4.1 0.8 gather_fusion.1
  4.9 0.7 convert_bitcast_fusion
  5.6 0.7 fusion.8
  6.3 0.2 reduce_window_sum.11
  6.5 0.2 select_reduce_fusion
  6.7 0.2 broadcast_in_dim.4
  6.9 0.2 pad_maximum_fusion
  7.1 4.3 %scatter_fusion = f32[256,7,128]{2,1,0:T(8,128)S(1)} fusion(f32[256,7,128]{2,1,0:T(8,128)S(1)} %copy-done, s32[128]{0:T(128)S(1)} %fusion.16, f32[128,7,128]{2,1,0:T(8,128)S(1)} %pad_maximum_fusion), kind=kCustom, calls=%fused_computation.4 | custom fusion | bytes 1376768 | tf_op jit(solution)/shard_map/scatter | solution.py:284
  11.4 0.0 copy-start.2
  11.4 1.2 copy.156
  12.6 13.1 %all-to-all-start = ((f32[64,4,7,128]{3,1,2,0:T(4,128)}), f32[64,4,7,128]{3,1,2,0:T(4,128)S(1)}, u32[]{:S(2)}, u32[]{:S(2)}) async-start(f32[64,4,7,128]{3,1,2,0:T(4,128)} %copy.156), calls=%async_computation | async-start | bytes 1835008 | tf_op jit(solution)/shard_map/all_to_all | solution.py:286
  25.7 0.2 copy.159
  25.8 1.3 collective-permute-start
  27.2 1.5 %collective-permute-start.1 = (f32[3,2,3,128]{3,1,2,0:T(2,128)S(1)}, f32[3,2,3,128]{3,1,2,0:T(2,128)S(1)}, u32[]{:S(2)}, u32[]{:S(2)}) collective-permute-start(f32[3,2,3,128]{3,1,2,0:T(2,128)S(1)} %bitcast.120), channel_id=1, source_target_pairs={{1,0},{2,1},{3,2},{5,4},{6,5},{7,6},{9,8},{10,9},{11,10},{13,12},{... | collective-permute-start | bytes 27656 | tf_op jit(solution)/shard_map/ppermute | solution.py:21
  28.7 0.1 slice_multiply_fusion
  28.8 0.1 slice.147
  28.9 0.1 copy.158
  29.0 17.9 %collective-permute-done = f32[3,2,3,16]{3,1,2,0:T(2,128)S(1)} collective-permute-done((f32[3,2,3,16]{3,1,2,0:T(2,128)S(1)}, f32[3,2,3,16]{3,1,2,0:T(2,128)S(1)}, u32[]{:S(2)}, u32[]{:S(2)}) %collective-permute-start) | collective-permute-done | bytes 1184 | tf_op jit(solution)/shard_map/ppermute | solution.py:21
  46.9 0.1 concatenate.39
  47.0 0.2 copy.161
  47.2 0.2 pad_maximum_fusion.1
  47.4 0.1 copy.164
  47.5 1.2 concatenate.46
  48.8 2.2 %all-to-all-done = f32[64,4,7,128]{3,1,2,0:T(4,128)S(1)} async-done(((f32[64,4,7,128]{3,1,2,0:T(4,128)}), f32[64,4,7,128]{3,1,2,0:T(4,128)S(1)}, u32[]{:S(2)}, u32[]{:S(2)}) %all-to-all-start) | async-done | bytes 917536 | tf_op jit(solution)/shard_map/all_to_all | solution.py:286
  51.0 0.1 copy.157
  51.1 9.1 %fusion.7 = (s32[256]{0:T(256)S(1)}, s32[256]{0:T(256)S(1)}) fusion(f32[256,7,128]{2,1,0:T(8,128)S(1)} %bitcast.93), kind=kLoop, calls=%fused_computation.23 | loop fusion | flops 512 | bytes 3072 | tf_op jit(solution)/shard_map/convert_element_type | solution.py:293
  60.3 2.3 %gather_fusion.2 = f32[256,12,128]{2,1,0:T(8,128)} fusion(f32[96,12,128]{2,1,0:T(8,128)S(1)} %bitcast.91, s32[1024]{0:T(1024)S(1)} %pad_clamp_fusion.1), kind=kCustom, calls=%fused_computation.2 | custom fusion | bytes 3146752 | tf_op jit(solution)/shard_map/gather | solution.py:294
  62.6 35.8 %shard_map.94 = (f32[256,6,128]{2,1,0:T(8,128)}, f32[256,11,128]{2,1,0:T(8,128)}) custom-call(f32[256,7,128]{2,1,0:T(8,128)} %bitcast.94, f32[256,12,128]{2,1,0:T(8,128)} %gather_fusion.2), custom_call_target="tpu_custom_call" | custom-call | tf_op jit(solution)/shard_map/pallas_call | solution.py:203
  98.5 2.3 %copy.165 = f32[64,4,6,128]{3,1,2,0:T(4,128)} copy(f32[64,4,6,128]{3,2,1,0:T(8,128)} %bitcast.102) | data formatting | bytes 1572864 | tf_op jit(solution)/shard_map/reshape | solution.py:301
  100.8 8.1 %all-to-all-start.1 = ((f32[64,4,6,128]{3,1,2,0:T(4,128)}), f32[64,4,6,128]{3,1,2,0:T(4,128)S(1)}, u32[]{:S(2)}, u32[]{:S(2)}) async-start(f32[64,4,6,128]{3,1,2,0:T(4,128)} %copy.165), calls=%async_computation.1 | async-start | bytes 1572864 | tf_op jit(solution)/shard_map/all_to_all | solution.py:300
  108.9 1.8 %copy.175 = f32[256,11,128]{0,2,1:T(8,128)S(1)} copy(f32[256,11,128]{2,1,0:T(8,128)} %get-tuple-element.54) | data formatting | bytes 2883584
  110.8 0.8 fusion.1
  111.7 0.7 fusion.20
  112.3 0.1 split.56
  112.4 0.2 copy.171
  112.6 3.3 %collective-permute-start.2 = (f32[3,2,3,16]{3,1,2,0:T(2,128)S(1)}, f32[3,2,3,16]{3,1,2,0:T(2,128)S(1)}, u32[]{:S(2)}, u32[]{:S(2)}) collective-permute-start(f32[3,2,3,16]{3,1,2,0:T(2,128)S(1)} %bitcast.116), channel_id=1, source_target_pairs={{0,4},{4,8},{8,12},{12,16},{16,20},{20,24},{24,28},{1,5},{5,9},{9,... | collective-permute-start | bytes 3464 | tf_op jit(solution)/shard_map/ppermute | solution.py:21
  115.9 3.2 %collective-permute-start.3 = (f32[3,2,3,128]{3,1,2,0:T(2,128)S(1)}, f32[3,2,3,128]{3,1,2,0:T(2,128)S(1)}, u32[]{:S(2)}, u32[]{:S(2)}) collective-permute-start(f32[3,2,3,128]{3,1,2,0:T(2,128)S(1)} %bitcast.119), channel_id=1, source_target_pairs={{0,1},{1,2},{2,3},{4,5},{5,6},{6,7},{8,9},{9,10},{10,11},{12,13},{... | collective-permute-start | bytes 27656 | tf_op jit(solution)/shard_map/ppermute | solution.py:21
  119.2 0.1 broadcast_multiply_fusion.1
  119.2 0.6 pad_add_fusion
  119.9 3.8 %collective-permute-done.2 = f32[3,2,3,16]{3,1,2,0:T(2,128)S(1)} collective-permute-done((f32[3,2,3,16]{3,1,2,0:T(2,128)S(1)}, f32[3,2,3,16]{3,1,2,0:T(2,128)S(1)}, u32[]{:S(2)}, u32[]{:S(2)}) %collective-permute-start.2) | collective-permute-done | bytes 1184 | tf_op jit(solution)/shard_map/ppermute | solution.py:21
  123.7 0.2 copy.172
  123.9 8.1 %all-to-all-done.1 = f32[64,4,6,128]{3,1,2,0:T(4,128)S(1)} async-done(((f32[64,4,6,128]{3,1,2,0:T(4,128)}), f32[64,4,6,128]{3,1,2,0:T(4,128)S(1)}, u32[]{:S(2)}, u32[]{:S(2)}) %all-to-all-start.1) | async-done | bytes 786464 | tf_op jit(solution)/shard_map/all_to_all | solution.py:300
  132.0 0.1 copy.166
  132.1 0.0 copy-start.4
  132.1 0.0 copy-start.5
  132.2 0.5 copy.167
  132.6 0.8 gather_fusion.3
  133.4 0.1 fusion.21
  133.5 0.1 copy.170
  133.7 0.3 fusion.2
  134.0 0.1 add_add_fusion
  134.1 0.2 scatter-add.11
  134.3 0.1 scatter-add.14
  134.4 0.1 copy.168
  134.5 0.3 convolution_multiply_fusion
  134.8 0.2 copy-done.3
  135.0 0.7 copy-done.6
  (37 shorter events, 0.2 us)
Async XLA Ops:
  0.6 5.8 %copy-start.9 = (s32[1,1,1,128]{3,2,1,0:T(1,128)S(1)}, s32[1,1,1,128]{3,2,1,0:T(1,128)}, u32[]{:S(2)}) copy-start(s32[1,1,1,128]{3,2,1,0:T(1,128)} %param.20) | copy-start | bytes 1540
  4.1 2.9 %copy-start = (f32[256,7,128]{2,1,0:T(8,128)S(1)}, f32[256,7,128]{2,1,0:T(8,128)}, u32[]{:S(2)}) copy-start(f32[256,7,128]{2,1,0:T(8,128)} %constant.133.clone.1) | copy-start | bytes 2752516
  11.4 14.3 %copy-start.2 = (f32[3,2,3,16,128]{4,3,2,1,0:T(8,128)S(1)}, f32[3,2,3,16,128]{4,3,2,1,0:T(8,128)}, u32[]{:S(2)}) copy-start(f32[3,2,3,16,128]{4,3,2,1,0:T(8,128)} %param.15) | copy-start | bytes 442372
  11.4 17.3 %copy-start.7 = (f32[2,2,3,16,128]{4,3,2,1,0:T(8,128)S(1)}, f32[2,2,3,16,128]{4,3,2,1,0:T(8,128)}, u32[]{:S(2)}) copy-start(f32[2,2,3,16,128]{4,3,2,1,0:T(8,128)} %param.16) | copy-start | bytes 294916
  12.5 35.0 %copy-start.8 = (f32[2,3,16,128]{3,2,1,0:T(8,128)S(1)}, f32[2,3,16,128]{3,2,1,0:T(8,128)}, u32[]{:S(2)}) copy-start(f32[2,3,16,128]{3,2,1,0:T(8,128)} %param.17) | copy-start | bytes 147460
  12.6 38.4 %all-to-all-start = ((f32[64,4,7,128]{3,1,2,0:T(4,128)}), f32[64,4,7,128]{3,1,2,0:T(4,128)S(1)}, u32[]{:S(2)}, u32[]{:S(2)}) async-start(f32[64,4,7,128]{3,1,2,0:T(4,128)} %copy.156), calls=%async_computation | async-start | bytes 1835008 | tf_op jit(solution)/shard_map/all_to_all | solution.py:286
  25.8 21.1 %collective-permute-start = (f32[3,2,3,16]{3,1,2,0:T(2,128)S(1)}, f32[3,2,3,16]{3,1,2,0:T(2,128)S(1)}, u32[]{:S(2)}, u32[]{:S(2)}) collective-permute-start(f32[3,2,3,16]{3,1,2,0:T(2,128)S(1)} %bitcast.115), channel_id=1, source_target_pairs={{4,0},{8,4},{12,8},{16,12},{20,16},{24,20},{28,24},{5,1},{9,5},{13... | collective-permute-start | bytes 3464 | tf_op jit(solution)/shard_map/ppermute | solution.py:21
  27.2 20.2 %collective-permute-start.1 = (f32[3,2,3,128]{3,1,2,0:T(2,128)S(1)}, f32[3,2,3,128]{3,1,2,0:T(2,128)S(1)}, u32[]{:S(2)}, u32[]{:S(2)}) collective-permute-start(f32[3,2,3,128]{3,1,2,0:T(2,128)S(1)} %bitcast.120), channel_id=1, source_target_pairs={{1,0},{2,1},{3,2},{5,4},{6,5},{7,6},{9,8},{10,9},{11,10},{13,12},{... | collective-permute-start | bytes 27656 | tf_op jit(solution)/shard_map/ppermute | solution.py:21
  51.1 11.5 %copy-start.1 = (f32[64,4,7,128]{3,2,1,0:T(8,128)}, f32[64,4,7,128]{3,2,1,0:T(8,128)S(1)}, u32[]{:S(2)}) copy-start(f32[64,4,7,128]{3,2,1,0:T(8,128)S(1)} %copy.157) | copy-start | bytes 2752516
  100.8 31.2 %all-to-all-start.1 = ((f32[64,4,6,128]{3,1,2,0:T(4,128)}), f32[64,4,6,128]{3,1,2,0:T(4,128)S(1)}, u32[]{:S(2)}, u32[]{:S(2)}) async-start(f32[64,4,6,128]{3,1,2,0:T(4,128)} %copy.165), calls=%async_computation.1 | async-start | bytes 1572864 | tf_op jit(solution)/shard_map/all_to_all | solution.py:300
  112.6 11.1 %collective-permute-start.2 = (f32[3,2,3,16]{3,1,2,0:T(2,128)S(1)}, f32[3,2,3,16]{3,1,2,0:T(2,128)S(1)}, u32[]{:S(2)}, u32[]{:S(2)}) collective-permute-start(f32[3,2,3,16]{3,1,2,0:T(2,128)S(1)} %bitcast.116), channel_id=1, source_target_pairs={{0,4},{4,8},{8,12},{12,16},{16,20},{20,24},{24,28},{1,5},{5,9},{9,... | collective-permute-start | bytes 3464 | tf_op jit(solution)/shard_map/ppermute | solution.py:21
  115.9 18.4 %collective-permute-start.3 = (f32[3,2,3,128]{3,1,2,0:T(2,128)S(1)}, f32[3,2,3,128]{3,1,2,0:T(2,128)S(1)}, u32[]{:S(2)}, u32[]{:S(2)}) collective-permute-start(f32[3,2,3,128]{3,1,2,0:T(2,128)S(1)} %bitcast.119), channel_id=1, source_target_pairs={{0,1},{1,2},{2,3},{4,5},{5,6},{6,7},{8,9},{9,10},{10,11},{12,13},{... | collective-permute-start | bytes 27656 | tf_op jit(solution)/shard_map/ppermute | solution.py:21
  132.1 1.5 %copy-start.10 = (s32[1,1,1,128]{3,2,1,0:T(1,128)S(1)}, s32[1,1,1,128]{3,2,1,0:T(1,128)}, u32[]{:S(2)}) copy-start(s32[1,1,1,128]{3,2,1,0:T(1,128)} %param.19) | copy-start | bytes 1540
  132.1 1.8 %copy-start.4 = (f32[3,96,128]{2,1,0:T(8,128)S(1)}, f32[3,96,128]{2,1,0:T(8,128)}, u32[]{:S(2)}) copy-start(f32[3,96,128]{2,1,0:T(8,128)} %get-tuple-element.76) | copy-start | bytes 442372
  132.1 1.8 %copy-start.5 = (f32[3,2,3,16,128]{4,3,2,1,0:T(8,128)S(1)}, f32[3,2,3,16,128]{4,3,2,1,0:T(8,128)}, u32[]{:S(2)}) copy-start(f32[3,2,3,16,128]{4,3,2,1,0:T(8,128)} %param.18) | copy-start | bytes 442372
  134.4 0.7 copy-start.3
  135.0 0.7 copy-start.6

commit v8 on v5

--- a/solution.py
+++ b/solution.py
@@ -279,21 +279,28 @@
     rank_within = jnp.sum((jnp.cumsum(owner_onehot, axis=0) - owner_onehot) * owner_onehot, axis=1)
     slot_index = owner_ids * capacity + rank_within
     slot_count = group_size * capacity
-    pair_of_slot = (
-        jnp.full((slot_count,), pair_count, jnp.int32)
-        .at[slot_index]
-        .set(jnp.arange(pair_count, dtype=jnp.int32))
-    )
-    block_of_slot = jnp.concatenate([target_ids, jnp.zeros((1,), jnp.int32)])[pair_of_slot]
-    id_of_slot = jnp.concatenate(
-        [source_ids.astype(jnp.float32), jnp.full((1,), -1.0, jnp.float32)]
-    )[pair_of_slot]
+    slot_pick = (
+        jnp.arange(slot_count, dtype=jnp.int32)[:, None] == slot_index[None, :]
+    ).astype(jnp.float32)
+    block_pick = (
+        target_ids[:, None] == jnp.arange(blocks_here, dtype=jnp.int32)[None, :]
+    ).astype(jnp.float32)
+    slot_block = jnp.dot(slot_pick, block_pick, preferred_element_type=jnp.float32)
+    blocks_sent = jnp.concatenate([target_blocks, seed_blocks], axis=1)
+    rows_sent = jnp.dot(
+        slot_block,
+        blocks_sent.reshape(blocks_here, -1),
+        precision=lax.Precision.HIGHEST,
+        preferred_element_type=jnp.float32,
+    ).reshape(slot_count, 6, age_here)
+    ident = jnp.dot(
+        slot_pick,
+        (source_ids + 1).astype(jnp.float32),
+        precision=lax.Precision.HIGHEST,
+        preferred_element_type=jnp.float32,
+    )
     outgoing = jnp.concatenate(
-        [
-            target_blocks[block_of_slot],
-            seed_blocks[block_of_slot],
-            jnp.broadcast_to(id_of_slot[:, None, None], (slot_count, 1, age_here)),
-        ],
+        [rows_sent, jnp.broadcast_to(ident[:, None, None], (slot_count, 1, age_here))],
         axis=1,
     )
     received = lax.all_to_all(
@@ -303,7 +310,7 @@
         concat_axis=0,
         tiled=True,
     ).reshape(slot_count, 7, age_here)
-    asked = received[:, 6, 0].astype(jnp.int32)
+    asked = received[:, 6, 0].astype(jnp.int32) - 1
     slot_payload = payload[jnp.clip(asked, 0, blocks_here - 1)]
     slot_velocity, slot_grad, payload_terms = run_pairs(
         received[:, 0:3], slot_payload, received[:, 3:6]

time: 122 us -> 117 us (0.959)
  local copies, waits for them, and re-layouts: 20.9 us -> 13.7 us
  matrix products: 1.4 us -> 3.92 us
    gather x4 -> x0, local copies, waits for them, and re-layouts: 5.87 us -> none  [the longest x1 1.94 us: local(): jnp.concatenate([source_ids.astype(jnp.float32), jnp.full((1,), -1.0, jnp...]
    dot_general x0 -> x3, matrix products: none -> 2.53 us  [the longest x1 0.93 us: local(): jnp.dot(slot_pick, block_pick, preferred_element_type=jnp.float32)]
    unnamed x20 -> x18, local copies, waits for them, and re-layouts: 3.71 us -> 3.7 us
  transfers between devices with their start and end apart: 6 -> 6, of which waited for: 4 -> 4; matrix products, arithmetic and copies ran while one was open for 6% -> 7% of each run, Pallas kernels for 0% -> 0%
where the time goes in v8:
time: 117 us
  waiting for transfers between devices  32.9 us (28%)
  starting transfers between devices  30.2 us (26%)
  Pallas kernels  28.6 us (24%)
  local copies, waits for them, and re-layouts  13.7 us (12%)
  other arithmetic  6.05 us (5%)
  matrix products  3.92 us (3%)
    pallas_call x1, Pallas kernels, run_pairs(): pl.pallas_call(pair_kernel, grid=(number // step,), in_specs=[spec(3), sp...  28.6 us
    ppermute x4, waiting for transfers between devices, shifted_2(): lax.ppermute(value, axis, [(source, source + steps) for source in range(l...  22.6 us
    all_to_all x1, starting transfers between devices, local(): lax.all_to_all(outgoing.reshape(group_size, capacity, 7, age_here), ('tur...  13 us
    ppermute x4, starting transfers between devices, shifted_2(): lax.ppermute(value, axis, [(source, source + steps) for source in range(l...  9.06 us
    all_to_all x1, starting transfers between devices, local(): lax.all_to_all(jnp.concatenate([slot_velocity, slot_grad], axis=1).reshap...  8.13 us
    all_to_all x1, waiting for transfers between devices, local(): lax.all_to_all(jnp.concatenate([slot_velocity, slot_grad], axis=1).reshap...  8.08 us
    unnamed x18, local copies, waits for them, and re-layouts  3.7 us
    gather x2, local copies, waits for them, and re-layouts, local(): slot_payload = payload[jnp.clip(asked, 0, blocks_here - 1)]  2.67 us
  transfers between devices with their start and end apart: 6, of which 4 were waited for; matrix products, arithmetic and copies ran while one was open for 7% of the time, Pallas kernels for 0%

profile of v8, /device:TPU:1, one launch (start us, length us, event | category | flops | bytes accessed | tf_op | source)
XLA Modules:
  0.0 116.6 jit_solution(1001912573672302466)
XLA Ops:
  0.6 0.7 fusion.15
  1.4 0.2 reduce_window_sum.11
  1.5 0.8 select_reduce_fusion
  2.4 0.7 multiply_add_fusion
  3.0 1.0 copy.113
  4.1 0.9 broadcast_multiply_fusion
  5.0 0.1 copy.114
  5.1 0.9 convolution_bitcast_fusion
  6.0 0.8 fusion.9
  6.8 0.1 pad_maximum_fusion.2
  7.0 0.8 fusion.2
  7.8 0.1 broadcast_in_dim.4
  7.9 0.1 pad_maximum_fusion
  8.0 0.0 copy-start.4
  8.0 1.1 copy.116
  9.1 13.0 %all-to-all-start = ((f32[64,4,7,128]{3,1,2,0:T(4,128)}), f32[64,4,7,128]{3,1,2,0:T(4,128)S(1)}, u32[]{:S(2)}, u32[]{:S(2)}) async-start(f32[64,4,7,128]{3,1,2,0:T(4,128)} %copy.116), calls=%async_computation | async-start | bytes 1835008 | tf_op jit(solution)/shard_map/all_to_all | solution.py:306
  22.1 0.2 copy.119
  22.2 1.3 %collective-permute-start = (f32[3,2,3,16]{3,1,2,0:T(2,128)S(1)}, f32[3,2,3,16]{3,1,2,0:T(2,128)S(1)}, u32[]{:S(2)}, u32[]{:S(2)}) collective-permute-start(f32[3,2,3,16]{3,1,2,0:T(2,128)S(1)} %bitcast.147), channel_id=1, source_target_pairs={{4,0},{8,4},{12,8},{16,12},{20,16},{24,20},{28,24},{5,1},{9,5},{13... | collective-permute-start | bytes 3464 | tf_op jit(solution)/shard_map/ppermute | solution.py:21
  23.6 1.3 %collective-permute-start.1 = (f32[3,2,3,128]{3,1,2,0:T(2,128)S(1)}, f32[3,2,3,128]{3,1,2,0:T(2,128)S(1)}, u32[]{:S(2)}, u32[]{:S(2)}) collective-permute-start(f32[3,2,3,128]{3,1,2,0:T(2,128)S(1)} %bitcast.152), channel_id=1, source_target_pairs={{1,0},{2,1},{3,2},{5,4},{6,5},{7,6},{9,8},{10,9},{11,10},{13,12},{... | collective-permute-start | bytes 27656 | tf_op jit(solution)/shard_map/ppermute | solution.py:21
  24.9 0.1 slice_multiply_fusion
  25.0 0.1 slice.135
  25.1 0.1 copy.118
  25.2 18.1 %collective-permute-done = f32[3,2,3,16]{3,1,2,0:T(2,128)S(1)} collective-permute-done((f32[3,2,3,16]{3,1,2,0:T(2,128)S(1)}, f32[3,2,3,16]{3,1,2,0:T(2,128)S(1)}, u32[]{:S(2)}, u32[]{:S(2)}) %collective-permute-start) | collective-permute-done | bytes 1184 | tf_op jit(solution)/shard_map/ppermute | solution.py:21
  43.3 0.1 concatenate.44
  43.4 0.2 copy.121
  43.6 0.2 pad_maximum_fusion.3
  43.8 0.1 copy.124
  43.9 1.2 %concatenate.51 = f32[12,96,128]{2,0,1:T(8,128)S(1)} concatenate(f32[3,96,128]{2,0,1:T(4,128)S(1)} %bitcast.127, f32[3,96,128]{2,0,1:T(4,128)S(1)} %pad_maximum_fusion.3, f32[3,96,128]{2,0,1:T(4,128)S(1)} %bitcast.132, f32[1,96,128]{2,0,1:T(1,128)S(1)} %bitcast.143, f32[1,96,128]{2,0,1:T(1,128)S(1)} %bitcast.142, f32[1,96,128]{2,0,1:T(1,128)S(1)} %bitcast.146), dimensions={0} | concatenate | bytes 1179648 | tf_op jit(solution)/shard_map/jvp()/concatenate | solution.py:260
  45.1 2.2 %all-to-all-done = f32[64,4,7,128]{3,1,2,0:T(4,128)S(1)} async-done(((f32[64,4,7,128]{3,1,2,0:T(4,128)}), f32[64,4,7,128]{3,1,2,0:T(4,128)S(1)}, u32[]{:S(2)}, u32[]{:S(2)}) %all-to-all-start) | async-done | bytes 917536 | tf_op jit(solution)/shard_map/all_to_all | solution.py:306
  47.4 0.2 copy.117
  47.5 0.1 fusion.10
  47.7 0.9 slice_bitcast_fusion
  48.6 1.0 gather_fusion
  49.6 1.7 %copy.149 = f32[256,12,128]{2,0,1:T(8,128)} copy(f32[256,12,128]{2,1,0:T(8,128)S(1)} %gather_fusion) | data formatting | bytes 3145728 | tf_op jit(solution)/shard_map/gather | solution.py:314
  51.3 28.6 %shard_map.94 = (f32[3,256,128]{2,1,0:T(8,128)}, f32[3,256,128]{2,1,0:T(8,128)}, f32[11,256,128]{2,1,0:T(8,128)}) custom-call(f32[3,256,128]{2,1,0:T(8,128)} %get-tuple-element.57.t_ref, f32[12,256,128]{2,1,0:T(8,128)} %bitcast.119, f32[3,256,128]{2,1,0:T(8,128)} %get-tuple-element.56.c_ref), custom_call_target="tpu_custom_call" | custom-call | tf_op jit(solution)/shard_map/pallas_call | solution.py:206
  79.9 1.2 %pad_maximum_fusion.1 = f32[256,6,128]{2,0,1:T(8,128)S(1)} fusion(f32[256,3,128]{2,0,1:T(8,128)} %bitcast.141, f32[256,3,128]{2,0,1:T(8,128)} %bitcast.140), kind=kLoop, calls=%fused_computation.9 | loop fusion | flops 196608 | bytes 1572864 | tf_op jit(solution)/shard_map/concatenate | solution.py:323
  81.1 0.0 copy-start.7
  81.1 1.0 copy.126
  82.1 8.1 %all-to-all-start.1 = ((f32[64,4,6,128]{3,1,2,0:T(4,128)}), f32[64,4,6,128]{3,1,2,0:T(4,128)S(1)}, u32[]{:S(2)}, u32[]{:S(2)}) async-start(f32[64,4,6,128]{3,1,2,0:T(4,128)} %copy.126), calls=%async_computation.1 | async-start | bytes 1572864 | tf_op jit(solution)/shard_map/all_to_all | solution.py:322
  90.3 1.8 %copy.135 = f32[256,11,128]{0,2,1:T(8,128)S(1)} copy(f32[256,11,128]{2,0,1:T(8,128)} %bitcast.128) | data formatting | bytes 2883584
  92.1 0.8 fusion.1
  93.0 0.1 split.56
  93.1 0.2 copy.131
  93.3 3.3 %collective-permute-start.2 = (f32[3,2,3,16]{3,1,2,0:T(2,128)S(1)}, f32[3,2,3,16]{3,1,2,0:T(2,128)S(1)}, u32[]{:S(2)}, u32[]{:S(2)}) collective-permute-start(f32[3,2,3,16]{3,1,2,0:T(2,128)S(1)} %bitcast.148), channel_id=1, source_target_pairs={{0,4},{4,8},{8,12},{12,16},{16,20},{20,24},{24,28},{1,5},{5,9},{9,... | collective-permute-start | bytes 3464 | tf_op jit(solution)/shard_map/ppermute | solution.py:21
  96.6 3.2 %collective-permute-start.3 = (f32[3,2,3,128]{3,1,2,0:T(2,128)S(1)}, f32[3,2,3,128]{3,1,2,0:T(2,128)S(1)}, u32[]{:S(2)}, u32[]{:S(2)}) collective-permute-start(f32[3,2,3,128]{3,1,2,0:T(2,128)S(1)} %bitcast.151), channel_id=1, source_target_pairs={{0,1},{1,2},{2,3},{4,5},{5,6},{6,7},{8,9},{9,10},{10,11},{12,13},{... | collective-permute-start | bytes 27656 | tf_op jit(solution)/shard_map/ppermute | solution.py:21
  99.8 0.1 broadcast_multiply_fusion.1
  99.9 0.6 pad_add_fusion
  100.5 4.5 %collective-permute-done.2 = f32[3,2,3,16]{3,1,2,0:T(2,128)S(1)} collective-permute-done((f32[3,2,3,16]{3,1,2,0:T(2,128)S(1)}, f32[3,2,3,16]{3,1,2,0:T(2,128)S(1)}, u32[]{:S(2)}, u32[]{:S(2)}) %collective-permute-start.2) | collective-permute-done | bytes 1184 | tf_op jit(solution)/shard_map/ppermute | solution.py:21
  105.1 0.2 copy.132
  105.3 8.1 %all-to-all-done.1 = f32[64,4,6,128]{3,1,2,0:T(4,128)S(1)} async-done(((f32[64,4,6,128]{3,1,2,0:T(4,128)}), f32[64,4,6,128]{3,1,2,0:T(4,128)S(1)}, u32[]{:S(2)}, u32[]{:S(2)}) %all-to-all-start.1) | async-done | bytes 786464 | tf_op jit(solution)/shard_map/all_to_all | solution.py:322
  113.3 0.1 copy.127
  113.5 0.0 copy-start.6
  113.5 0.8 gather_fusion.1
  114.3 0.1 fusion.33
  114.4 0.1 copy.130
  114.5 0.3 fusion.5
  114.8 0.1 add_add_fusion
  115.0 0.2 scatter-add.11
  115.2 0.1 scatter-add.14
  115.2 0.0 copy-start.1
  115.2 0.1 copy.128
  115.4 0.3 convolution_multiply_fusion
  115.7 0.2 copy-done.1
  115.9 0.7 copy-done.3
  (32 shorter events, 0.3 us)
Async XLA Ops:
  8.0 14.1 %copy-start = (f32[3,2,3,16,128]{4,3,2,1,0:T(8,128)S(1)}, f32[3,2,3,16,128]{4,3,2,1,0:T(8,128)}, u32[]{:S(2)}) copy-start(f32[3,2,3,16,128]{4,3,2,1,0:T(8,128)} %param.13) | copy-start | bytes 442372
  8.0 16.9 %copy-start.4 = (f32[2,2,3,16,128]{4,3,2,1,0:T(8,128)S(1)}, f32[2,2,3,16,128]{4,3,2,1,0:T(8,128)}, u32[]{:S(2)}) copy-start(f32[2,2,3,16,128]{4,3,2,1,0:T(8,128)} %param.14) | copy-start | bytes 294916
  9.1 38.3 %all-to-all-start = ((f32[64,4,7,128]{3,1,2,0:T(4,128)}), f32[64,4,7,128]{3,1,2,0:T(4,128)S(1)}, u32[]{:S(2)}, u32[]{:S(2)}) async-start(f32[64,4,7,128]{3,1,2,0:T(4,128)} %copy.116), calls=%async_computation | async-start | bytes 1835008 | tf_op jit(solution)/shard_map/all_to_all | solution.py:306
  22.1 21.9 %copy-start.5 = (f32[2,3,16,128]{3,2,1,0:T(8,128)S(1)}, f32[2,3,16,128]{3,2,1,0:T(8,128)}, u32[]{:S(2)}) copy-start(f32[2,3,16,128]{3,2,1,0:T(8,128)} %param.15) | copy-start | bytes 147460
  22.2 21.1 %collective-permute-start = (f32[3,2,3,16]{3,1,2,0:T(2,128)S(1)}, f32[3,2,3,16]{3,1,2,0:T(2,128)S(1)}, u32[]{:S(2)}, u32[]{:S(2)}) collective-permute-start(f32[3,2,3,16]{3,1,2,0:T(2,128)S(1)} %bitcast.147), channel_id=1, source_target_pairs={{4,0},{8,4},{12,8},{16,12},{20,16},{24,20},{28,24},{5,1},{9,5},{13... | collective-permute-start | bytes 3464 | tf_op jit(solution)/shard_map/ppermute | solution.py:21
  23.6 20.2 %collective-permute-start.1 = (f32[3,2,3,128]{3,1,2,0:T(2,128)S(1)}, f32[3,2,3,128]{3,1,2,0:T(2,128)S(1)}, u32[]{:S(2)}, u32[]{:S(2)}) collective-permute-start(f32[3,2,3,128]{3,1,2,0:T(2,128)S(1)} %bitcast.152), channel_id=1, source_target_pairs={{1,0},{2,1},{3,2},{5,4},{6,5},{7,6},{9,8},{10,9},{11,10},{13,12},{... | collective-permute-start | bytes 27656 | tf_op jit(solution)/shard_map/ppermute | solution.py:21
  81.1 9.2 %copy-start.7 = (s32[1,1,1,128]{3,2,1,0:T(1,128)S(1)}, s32[1,1,1,128]{3,2,1,0:T(1,128)}, u32[]{:S(2)}) copy-start(s32[1,1,1,128]{3,2,1,0:T(1,128)} %param.18) | copy-start | bytes 1540
  82.1 31.2 %all-to-all-start.1 = ((f32[64,4,6,128]{3,1,2,0:T(4,128)}), f32[64,4,6,128]{3,1,2,0:T(4,128)S(1)}, u32[]{:S(2)}, u32[]{:S(2)}) async-start(f32[64,4,6,128]{3,1,2,0:T(4,128)} %copy.126), calls=%async_computation.1 | async-start | bytes 1572864 | tf_op jit(solution)/shard_map/all_to_all | solution.py:322
  93.3 11.8 %collective-permute-start.2 = (f32[3,2,3,16]{3,1,2,0:T(2,128)S(1)}, f32[3,2,3,16]{3,1,2,0:T(2,128)S(1)}, u32[]{:S(2)}, u32[]{:S(2)}) collective-permute-start(f32[3,2,3,16]{3,1,2,0:T(2,128)S(1)} %bitcast.148), channel_id=1, source_target_pairs={{0,4},{4,8},{8,12},{12,16},{16,20},{20,24},{24,28},{1,5},{5,9},{9,... | collective-permute-start | bytes 3464 | tf_op jit(solution)/shard_map/ppermute | solution.py:21
  96.6 18.5 %collective-permute-start.3 = (f32[3,2,3,128]{3,1,2,0:T(2,128)S(1)}, f32[3,2,3,128]{3,1,2,0:T(2,128)S(1)}, u32[]{:S(2)}, u32[]{:S(2)}) collective-permute-start(f32[3,2,3,128]{3,1,2,0:T(2,128)S(1)} %bitcast.151), channel_id=1, source_target_pairs={{0,1},{1,2},{2,3},{4,5},{5,6},{6,7},{8,9},{9,10},{10,11},{12,13},{... | collective-permute-start | bytes 27656 | tf_op jit(solution)/shard_map/ppermute | solution.py:21
  113.5 1.0 copy-start.6
  113.5 1.3 %copy-start.2 = (f32[3,2,3,16,128]{4,3,2,1,0:T(8,128)S(1)}, f32[3,2,3,16,128]{4,3,2,1,0:T(8,128)}, u32[]{:S(2)}) copy-start(f32[3,2,3,16,128]{4,3,2,1,0:T(8,128)} %param.16) | copy-start | bytes 442372
  115.2 0.7 copy-start.1
  115.9 0.7 copy-start.3

commit v9 on v8

--- a/solution.py
+++ b/solution.py
@@ -272,11 +272,14 @@
         return jnp.transpose(array, (1, 0, 2)).reshape(shape_here)
 
     target_blocks = to_rows(positions)
-    seed_blocks = to_rows(adjoint_seed) * time_step
-    owner_onehot = (owner_ids[:, None] == jnp.arange(group_size, dtype=jnp.int32)[None, :]).astype(
-        jnp.int32
-    )
-    rank_within = jnp.sum((jnp.cumsum(owner_onehot, axis=0) - owner_onehot) * owner_onehot, axis=1)
+    seed_blocks = to_rows(adjoint_seed)
+    earlier = (
+        jnp.arange(pair_count, dtype=jnp.int32)[:, None]
+        > jnp.arange(pair_count, dtype=jnp.int32)[None, :]
+    )
+    rank_within = jnp.sum(
+        ((owner_ids[:, None] == owner_ids[None, :]) & earlier).astype(jnp.int32), axis=1
+    )
     slot_index = owner_ids * capacity + rank_within
     slot_count = group_size * capacity
     slot_pick = (
@@ -313,7 +316,7 @@
     asked = received[:, 6, 0].astype(jnp.int32) - 1
     slot_payload = payload[jnp.clip(asked, 0, blocks_here - 1)]
     slot_velocity, slot_grad, payload_terms = run_pairs(
-        received[:, 0:3], slot_payload, received[:, 3:6]
+        received[:, 0:3], slot_payload, received[:, 3:6] * time_step
     )
     payload_terms = jnp.concatenate(
         [payload_terms, jnp.zeros_like(payload_terms[:, :1])], axis=1

time: 117 us -> 116 us (level)
    unnamed x18 -> x19, local copies, waits for them, and re-layouts: 3.7 us -> 4.71 us
where the time goes in v9:
time: 116 us
  waiting for transfers between devices  32.9 us (28%)
  starting transfers between devices  30.2 us (26%)
  Pallas kernels  28.7 us (25%)
  local copies, waits for them, and re-layouts  13.7 us (12%)
  other arithmetic  5.23 us (5%)
  matrix products  3.93 us (3%)
    pallas_call x1, Pallas kernels, run_pairs(): pl.pallas_call(pair_kernel, grid=(number // step,), in_specs=[spec(3), sp...  28.7 us
    ppermute x4, waiting for transfers between devices, shifted_2(): lax.ppermute(value, axis, [(source, source + steps) for source in range(l...  22.6 us
    all_to_all x1, starting transfers between devices, local(): lax.all_to_all(outgoing.reshape(group_size, capacity, 7, age_here), ('tur...  13 us
    ppermute x4, starting transfers between devices, shifted_2(): lax.ppermute(value, axis, [(source, source + steps) for source in range(l...  9.07 us
    all_to_all x1, starting transfers between devices, local(): lax.all_to_all(jnp.concatenate([slot_velocity, slot_grad], axis=1).reshap...  8.13 us
    all_to_all x1, waiting for transfers between devices, local(): lax.all_to_all(jnp.concatenate([slot_velocity, slot_grad], axis=1).reshap...  8.08 us
    unnamed x19, local copies, waits for them, and re-layouts  4.71 us
    gather x2, local copies, waits for them, and re-layouts, local(): slot_payload = payload[jnp.clip(asked, 0, blocks_here - 1)]  2.66 us
  transfers between devices with their start and end apart: 6, of which 4 were waited for; matrix products, arithmetic and copies ran while one was open for 7% of the time, Pallas kernels for 0%

profile of v9, /device:TPU:1, one launch (start us, length us, event | category | flops | bytes accessed | tf_op | source)
XLA Modules:
  0.0 115.7 jit_solution(11812729108307182181)
XLA Ops:
  0.6 1.0 copy.140
  1.6 0.9 convert_reduce_fusion
  2.6 0.7 multiply_add_fusion
  3.2 1.0 copy.141
  4.2 0.9 convolution_bitcast_fusion
  5.2 0.8 fusion.10
  6.0 0.1 pad_maximum_fusion.2
  6.1 0.8 fusion.3
  6.9 0.1 broadcast_in_dim.4
  7.0 0.1 pad_maximum_fusion
  7.1 0.0 copy-start
  7.1 0.0 copy-start.4
  7.1 1.1 copy.143
  8.2 13.0 %all-to-all-start = ((f32[64,4,7,128]{3,1,2,0:T(4,128)}), f32[64,4,7,128]{3,1,2,0:T(4,128)S(1)}, u32[]{:S(2)}, u32[]{:S(2)}) async-start(f32[64,4,7,128]{3,1,2,0:T(4,128)} %copy.143), calls=%async_computation | async-start | bytes 1835008 | tf_op jit(solution)/shard_map/all_to_all | solution.py:309
  21.2 0.0 copy-start.5
  21.2 0.2 copy.146
  21.4 1.3 %collective-permute-start = (f32[3,2,3,16]{3,1,2,0:T(2,128)S(1)}, f32[3,2,3,16]{3,1,2,0:T(2,128)S(1)}, u32[]{:S(2)}, u32[]{:S(2)}) collective-permute-start(f32[3,2,3,16]{3,1,2,0:T(2,128)S(1)} %bitcast.147), channel_id=1, source_target_pairs={{4,0},{8,4},{12,8},{16,12},{20,16},{24,20},{28,24},{5,1},{9,5},{13... | collective-permute-start | bytes 3464 | tf_op jit(solution)/shard_map/ppermute | solution.py:21
  22.7 1.3 %collective-permute-start.1 = (f32[3,2,3,128]{3,1,2,0:T(2,128)S(1)}, f32[3,2,3,128]{3,1,2,0:T(2,128)S(1)}, u32[]{:S(2)}, u32[]{:S(2)}) collective-permute-start(f32[3,2,3,128]{3,1,2,0:T(2,128)S(1)} %bitcast.152), channel_id=1, source_target_pairs={{1,0},{2,1},{3,2},{5,4},{6,5},{7,6},{9,8},{10,9},{11,10},{13,12},{... | collective-permute-start | bytes 27656 | tf_op jit(solution)/shard_map/ppermute | solution.py:21
  24.1 0.1 slice_multiply_fusion.1
  24.1 0.1 slice.135
  24.3 0.1 copy.145
  24.4 18.1 %collective-permute-done = f32[3,2,3,16]{3,1,2,0:T(2,128)S(1)} collective-permute-done((f32[3,2,3,16]{3,1,2,0:T(2,128)S(1)}, f32[3,2,3,16]{3,1,2,0:T(2,128)S(1)}, u32[]{:S(2)}, u32[]{:S(2)}) %collective-permute-start) | collective-permute-done | bytes 1184 | tf_op jit(solution)/shard_map/ppermute | solution.py:21
  42.4 0.1 concatenate.44
  42.5 0.2 copy.148
  42.7 0.2 pad_maximum_fusion.3
  42.9 0.1 copy.151
  43.0 1.2 %concatenate.51 = f32[12,96,128]{2,0,1:T(8,128)S(1)} concatenate(f32[3,96,128]{2,0,1:T(4,128)S(1)} %bitcast.127, f32[3,96,128]{2,0,1:T(4,128)S(1)} %pad_maximum_fusion.3, f32[3,96,128]{2,0,1:T(4,128)S(1)} %bitcast.132, f32[1,96,128]{2,0,1:T(1,128)S(1)} %bitcast.143, f32[1,96,128]{2,0,1:T(1,128)S(1)} %bitcast.142, f32[1,96,128]{2,0,1:T(1,128)S(1)} %bitcast.146), dimensions={0} | concatenate | bytes 1179648 | tf_op jit(solution)/shard_map/jvp()/concatenate | solution.py:260
  44.3 2.2 %all-to-all-done = f32[64,4,7,128]{3,1,2,0:T(4,128)S(1)} async-done(((f32[64,4,7,128]{3,1,2,0:T(4,128)}), f32[64,4,7,128]{3,1,2,0:T(4,128)S(1)}, u32[]{:S(2)}, u32[]{:S(2)}) %all-to-all-start) | async-done | bytes 917536 | tf_op jit(solution)/shard_map/all_to_all | solution.py:309
  46.5 0.2 copy.144
  46.7 0.1 fusion.11
  46.8 0.9 fusion.2
  47.8 1.0 gather_fusion
  48.8 1.6 %copy.176 = f32[256,12,128]{2,0,1:T(8,128)} copy(f32[256,12,128]{2,1,0:T(8,128)S(1)} %gather_fusion) | data formatting | bytes 3145728 | tf_op jit(solution)/shard_map/gather | solution.py:317
  50.4 28.7 %shard_map.94 = (f32[3,256,128]{2,1,0:T(8,128)}, f32[3,256,128]{2,1,0:T(8,128)}, f32[11,256,128]{2,1,0:T(8,128)}) custom-call(f32[3,256,128]{2,1,0:T(8,128)} %get-tuple-element.60.t_ref, f32[12,256,128]{2,1,0:T(8,128)} %bitcast.119, f32[3,256,128]{2,1,0:T(8,128)} %get-tuple-element.59.c_ref), custom_call_target="tpu_custom_call" | custom-call | tf_op jit(solution)/shard_map/pallas_call | solution.py:206
  79.1 1.2 %pad_maximum_fusion.1 = f32[256,6,128]{2,0,1:T(8,128)S(1)} fusion(f32[256,3,128]{2,0,1:T(8,128)} %bitcast.141, f32[256,3,128]{2,0,1:T(8,128)} %bitcast.140), kind=kLoop, calls=%fused_computation.9 | loop fusion | flops 196608 | bytes 1572864 | tf_op jit(solution)/shard_map/concatenate | solution.py:326
  80.3 0.0 copy-start.7
  80.3 1.0 copy.153
  81.3 8.1 %all-to-all-start.1 = ((f32[64,4,6,128]{3,1,2,0:T(4,128)}), f32[64,4,6,128]{3,1,2,0:T(4,128)S(1)}, u32[]{:S(2)}, u32[]{:S(2)}) async-start(f32[64,4,6,128]{3,1,2,0:T(4,128)} %copy.153), calls=%async_computation.1 | async-start | bytes 1572864 | tf_op jit(solution)/shard_map/all_to_all | solution.py:325
  89.5 1.8 %copy.162 = f32[256,11,128]{0,2,1:T(8,128)S(1)} copy(f32[256,11,128]{2,0,1:T(8,128)} %bitcast.128) | data formatting | bytes 2883584
  91.3 0.8 fusion.1
  92.2 0.1 split.56
  92.3 0.2 copy.158
  92.5 3.3 %collective-permute-start.2 = (f32[3,2,3,16]{3,1,2,0:T(2,128)S(1)}, f32[3,2,3,16]{3,1,2,0:T(2,128)S(1)}, u32[]{:S(2)}, u32[]{:S(2)}) collective-permute-start(f32[3,2,3,16]{3,1,2,0:T(2,128)S(1)} %bitcast.148), channel_id=1, source_target_pairs={{0,4},{4,8},{8,12},{12,16},{16,20},{20,24},{24,28},{1,5},{5,9},{9,... | collective-permute-start | bytes 3464 | tf_op jit(solution)/shard_map/ppermute | solution.py:21
  95.8 3.2 %collective-permute-start.3 = (f32[3,2,3,128]{3,1,2,0:T(2,128)S(1)}, f32[3,2,3,128]{3,1,2,0:T(2,128)S(1)}, u32[]{:S(2)}, u32[]{:S(2)}) collective-permute-start(f32[3,2,3,128]{3,1,2,0:T(2,128)S(1)} %bitcast.151), channel_id=1, source_target_pairs={{0,1},{1,2},{2,3},{4,5},{5,6},{6,7},{8,9},{9,10},{10,11},{12,13},{... | collective-permute-start | bytes 27656 | tf_op jit(solution)/shard_map/ppermute | solution.py:21
  99.0 0.1 broadcast_multiply_fusion
  99.1 0.6 pad_add_fusion
  99.7 4.5 %collective-permute-done.2 = f32[3,2,3,16]{3,1,2,0:T(2,128)S(1)} collective-permute-done((f32[3,2,3,16]{3,1,2,0:T(2,128)S(1)}, f32[3,2,3,16]{3,1,2,0:T(2,128)S(1)}, u32[]{:S(2)}, u32[]{:S(2)}) %collective-permute-start.2) | collective-permute-done | bytes 1184 | tf_op jit(solution)/shard_map/ppermute | solution.py:21
  104.2 0.2 copy.159
  104.4 8.1 %all-to-all-done.1 = f32[64,4,6,128]{3,1,2,0:T(4,128)S(1)} async-done(((f32[64,4,6,128]{3,1,2,0:T(4,128)}), f32[64,4,6,128]{3,1,2,0:T(4,128)S(1)}, u32[]{:S(2)}, u32[]{:S(2)}) %all-to-all-start.1) | async-done | bytes 786464 | tf_op jit(solution)/shard_map/all_to_all | solution.py:325
  112.5 0.1 copy.154
  112.7 0.0 copy-start.6
  112.7 0.0 copy-start.2
  112.7 0.8 gather_fusion.1
  113.4 0.1 fusion.34
  113.6 0.1 copy.157
  113.7 0.3 fusion.6
  114.0 0.1 add_add_fusion
  114.1 0.2 scatter-add.11
  114.3 0.1 scatter-add.14
  114.4 0.0 copy-start.1
  114.4 0.1 copy.155
  114.6 0.3 convolution_multiply_fusion
  114.9 0.2 copy-done.1
  115.1 0.7 copy-done.3
  (29 shorter events, 0.2 us)
Async XLA Ops:
  7.1 14.1 %copy-start = (f32[3,2,3,16,128]{4,3,2,1,0:T(8,128)S(1)}, f32[3,2,3,16,128]{4,3,2,1,0:T(8,128)}, u32[]{:S(2)}) copy-start(f32[3,2,3,16,128]{4,3,2,1,0:T(8,128)} %param.13) | copy-start | bytes 442372
  7.1 16.9 %copy-start.4 = (f32[2,2,3,16,128]{4,3,2,1,0:T(8,128)S(1)}, f32[2,2,3,16,128]{4,3,2,1,0:T(8,128)}, u32[]{:S(2)}) copy-start(f32[2,2,3,16,128]{4,3,2,1,0:T(8,128)} %param.14) | copy-start | bytes 294916
  8.2 38.3 %all-to-all-start = ((f32[64,4,7,128]{3,1,2,0:T(4,128)}), f32[64,4,7,128]{3,1,2,0:T(4,128)S(1)}, u32[]{:S(2)}, u32[]{:S(2)}) async-start(f32[64,4,7,128]{3,1,2,0:T(4,128)} %copy.143), calls=%async_computation | async-start | bytes 1835008 | tf_op jit(solution)/shard_map/all_to_all | solution.py:309
  21.2 21.9 %copy-start.5 = (f32[2,3,16,128]{3,2,1,0:T(8,128)S(1)}, f32[2,3,16,128]{3,2,1,0:T(8,128)}, u32[]{:S(2)}) copy-start(f32[2,3,16,128]{3,2,1,0:T(8,128)} %param.15) | copy-start | bytes 147460
  21.4 21.1 %collective-permute-start = (f32[3,2,3,16]{3,1,2,0:T(2,128)S(1)}, f32[3,2,3,16]{3,1,2,0:T(2,128)S(1)}, u32[]{:S(2)}, u32[]{:S(2)}) collective-permute-start(f32[3,2,3,16]{3,1,2,0:T(2,128)S(1)} %bitcast.147), channel_id=1, source_target_pairs={{4,0},{8,4},{12,8},{16,12},{20,16},{24,20},{28,24},{5,1},{9,5},{13... | collective-permute-start | bytes 3464 | tf_op jit(solution)/shard_map/ppermute | solution.py:21
  22.7 20.2 %collective-permute-start.1 = (f32[3,2,3,128]{3,1,2,0:T(2,128)S(1)}, f32[3,2,3,128]{3,1,2,0:T(2,128)S(1)}, u32[]{:S(2)}, u32[]{:S(2)}) collective-permute-start(f32[3,2,3,128]{3,1,2,0:T(2,128)S(1)} %bitcast.152), channel_id=1, source_target_pairs={{1,0},{2,1},{3,2},{5,4},{6,5},{7,6},{9,8},{10,9},{11,10},{13,12},{... | collective-permute-start | bytes 27656 | tf_op jit(solution)/shard_map/ppermute | solution.py:21
  80.3 9.2 %copy-start.7 = (s32[1,1,1,128]{3,2,1,0:T(1,128)S(1)}, s32[1,1,1,128]{3,2,1,0:T(1,128)}, u32[]{:S(2)}) copy-start(s32[1,1,1,128]{3,2,1,0:T(1,128)} %param.18) | copy-start | bytes 1540
  81.3 31.2 %all-to-all-start.1 = ((f32[64,4,6,128]{3,1,2,0:T(4,128)}), f32[64,4,6,128]{3,1,2,0:T(4,128)S(1)}, u32[]{:S(2)}, u32[]{:S(2)}) async-start(f32[64,4,6,128]{3,1,2,0:T(4,128)} %copy.153), calls=%async_computation.1 | async-start | bytes 1572864 | tf_op jit(solution)/shard_map/all_to_all | solution.py:325
  92.5 11.8 %collective-permute-start.2 = (f32[3,2,3,16]{3,1,2,0:T(2,128)S(1)}, f32[3,2,3,16]{3,1,2,0:T(2,128)S(1)}, u32[]{:S(2)}, u32[]{:S(2)}) collective-permute-start(f32[3,2,3,16]{3,1,2,0:T(2,128)S(1)} %bitcast.148), channel_id=1, source_target_pairs={{0,4},{4,8},{8,12},{12,16},{16,20},{20,24},{24,28},{1,5},{5,9},{9,... | collective-permute-start | bytes 3464 | tf_op jit(solution)/shard_map/ppermute | solution.py:21
  95.8 18.5 %collective-permute-start.3 = (f32[3,2,3,128]{3,1,2,0:T(2,128)S(1)}, f32[3,2,3,128]{3,1,2,0:T(2,128)S(1)}, u32[]{:S(2)}, u32[]{:S(2)}) collective-permute-start(f32[3,2,3,128]{3,1,2,0:T(2,128)S(1)} %bitcast.151), channel_id=1, source_target_pairs={{0,1},{1,2},{2,3},{4,5},{5,6},{6,7},{8,9},{9,10},{10,11},{12,13},{... | collective-permute-start | bytes 27656 | tf_op jit(solution)/shard_map/ppermute | solution.py:21
  112.7 1.0 copy-start.6
  112.7 1.3 %copy-start.2 = (f32[3,2,3,16,128]{4,3,2,1,0:T(8,128)S(1)}, f32[3,2,3,16,128]{4,3,2,1,0:T(8,128)}, u32[]{:S(2)}) copy-start(f32[3,2,3,16,128]{4,3,2,1,0:T(8,128)} %param.16) | copy-start | bytes 442372
  114.4 0.7 copy-start.1
  115.1 0.7 copy-start.3

commit v10 on v9

--- a/solution.py
+++ b/solution.py
@@ -330,9 +330,15 @@
         split_axis=0,
         concat_axis=0,
         tiled=True,
-    ).reshape(slot_count, 6, age_here)[slot_index]
-    velocity = onehot_sum(target_ids, blocks_here, answered[:, 0:3])
-    target_grad = onehot_sum(target_ids, blocks_here, answered[:, 3:6])
+    ).reshape(slot_count, 6, age_here)
+    summed = jnp.dot(
+        slot_block.T,
+        answered.reshape(slot_count, -1),
+        precision=lax.Precision.HIGHEST,
+        preferred_element_type=jnp.float32,
+    ).reshape(blocks_here, 6, age_here)
+    velocity = summed[:, 0:3]
+    target_grad = summed[:, 3:6]
     advected = positions + time_step * from_rows(velocity)
     advected = advected.at[0].add(time_step)
     grad_nodes, grad_after_age, grad_after_station, grad_strengths = build_pullback(payload_grad)

time: 116 us -> 116 us (level)
    unnamed x19 -> x18, local copies, waits for them, and re-layouts: 4.71 us -> 5.05 us
where the time goes in v10:
time: 116 us
  waiting for transfers between devices  32.3 us (28%)
  starting transfers between devices  30.2 us (26%)
  Pallas kernels  28.7 us (25%)
  local copies, waits for them, and re-layouts  13.9 us (12%)
  other arithmetic  5.18 us (4%)
  matrix products  4.3 us (4%)
    pallas_call x1, Pallas kernels, run_pairs(): pl.pallas_call(pair_kernel, grid=(number // step,), in_specs=[spec(3), sp...  28.7 us
    ppermute x4, waiting for transfers between devices, shifted_2(): lax.ppermute(value, axis, [(source, source + steps) for source in range(l...  22 us
    all_to_all x1, starting transfers between devices, local(): lax.all_to_all(outgoing.reshape(group_size, capacity, 7, age_here), ('tur...  13 us
    ppermute x4, starting transfers between devices, shifted_2(): lax.ppermute(value, axis, [(source, source + steps) for source in range(l...  9.07 us
    all_to_all x1, starting transfers between devices, local(): lax.all_to_all(jnp.concatenate([slot_velocity, slot_grad], axis=1).reshap...  8.13 us
    all_to_all x1, waiting for transfers between devices, local(): lax.all_to_all(jnp.concatenate([slot_velocity, slot_grad], axis=1).reshap...  8.08 us
    unnamed x18, local copies, waits for them, and re-layouts  5.05 us
    gather x2, local copies, waits for them, and re-layouts, local(): slot_payload = payload[jnp.clip(asked, 0, blocks_here - 1)]  2.67 us
  transfers between devices with their start and end apart: 6, of which 4 were waited for; matrix products, arithmetic and copies ran while one was open for 7% of the time, Pallas kernels for 0%

profile of v10, /device:TPU:1, one launch (start us, length us, event | category | flops | bytes accessed | tf_op | source)
XLA Modules:
  0.0 115.6 jit_solution(697422162187836295)
XLA Ops:
  0.6 0.9 convert_reduce_fusion
  1.5 0.7 multiply_add_fusion
  2.2 0.8 fusion.7
  3.0 1.0 convolution_bitcast_fusion
  4.0 1.0 copy.133
  5.0 1.0 copy.134
  6.0 0.1 pad_maximum_fusion.2
  6.1 0.8 fusion.3
  6.9 0.1 broadcast_in_dim.4
  7.0 0.1 pad_maximum_fusion
  7.1 0.0 copy-start
  7.1 0.0 copy-start.5
  7.1 1.1 copy.136
  8.2 13.0 %all-to-all-start = ((f32[64,4,7,128]{3,1,2,0:T(4,128)}), f32[64,4,7,128]{3,1,2,0:T(4,128)S(1)}, u32[]{:S(2)}, u32[]{:S(2)}) async-start(f32[64,4,7,128]{3,1,2,0:T(4,128)} %copy.136), calls=%async_computation | async-start | bytes 1835008 | tf_op jit(solution)/shard_map/all_to_all | solution.py:309
  21.2 0.0 copy-done
  21.2 0.0 copy-start.6
  21.2 1.3 %collective-permute-start.1 = (f32[3,2,3,128]{3,1,2,0:T(2,128)S(1)}, f32[3,2,3,128]{3,1,2,0:T(2,128)S(1)}, u32[]{:S(2)}, u32[]{:S(2)}) collective-permute-start(f32[3,2,3,128]{3,1,2,0:T(2,128)S(1)} %bitcast.138), channel_id=1, source_target_pairs={{1,0},{2,1},{3,2},{5,4},{6,5},{7,6},{9,8},{10,9},{11,10},{13,12},{... | collective-permute-start | bytes 27656 | tf_op jit(solution)/shard_map/ppermute | solution.py:21
  22.5 0.2 copy.139
  22.7 1.3 %collective-permute-start = (f32[3,2,3,16]{3,1,2,0:T(2,128)S(1)}, f32[3,2,3,16]{3,1,2,0:T(2,128)S(1)}, u32[]{:S(2)}, u32[]{:S(2)}) collective-permute-start(f32[3,2,3,16]{3,1,2,0:T(2,128)S(1)} %bitcast.133), channel_id=1, source_target_pairs={{4,0},{8,4},{12,8},{16,12},{20,16},{24,20},{28,24},{5,1},{9,5},{13... | collective-permute-start | bytes 3464 | tf_op jit(solution)/shard_map/ppermute | solution.py:21
  24.1 0.1 slice_multiply_fusion.2
  24.2 0.1 slice.135
  24.3 0.1 copy.138
  24.4 18.1 %collective-permute-done = f32[3,2,3,16]{3,1,2,0:T(2,128)S(1)} collective-permute-done((f32[3,2,3,16]{3,1,2,0:T(2,128)S(1)}, f32[3,2,3,16]{3,1,2,0:T(2,128)S(1)}, u32[]{:S(2)}, u32[]{:S(2)}) %collective-permute-start) | collective-permute-done | bytes 1184 | tf_op jit(solution)/shard_map/ppermute | solution.py:21
  42.4 0.1 concatenate.44
  42.5 0.2 copy.141
  42.7 0.2 pad_maximum_fusion.3
  42.9 0.0 collective-permute-done.1
  42.9 0.1 copy.144
  43.1 1.2 %concatenate.51 = f32[12,96,128]{2,0,1:T(8,128)S(1)} concatenate(f32[3,96,128]{2,0,1:T(4,128)S(1)} %bitcast.113, f32[3,96,128]{2,0,1:T(4,128)S(1)} %pad_maximum_fusion.3, f32[3,96,128]{2,0,1:T(4,128)S(1)} %bitcast.118, f32[1,96,128]{2,0,1:T(1,128)S(1)} %bitcast.129, f32[1,96,128]{2,0,1:T(1,128)S(1)} %bitcast.128, f32[1,96,128]{2,0,1:T(1,128)S(1)} %bitcast.132), dimensions={0} | concatenate | bytes 1179648 | tf_op jit(solution)/shard_map/jvp()/concatenate | solution.py:260
  44.3 2.2 %all-to-all-done = f32[64,4,7,128]{3,1,2,0:T(4,128)S(1)} async-done(((f32[64,4,7,128]{3,1,2,0:T(4,128)}), f32[64,4,7,128]{3,1,2,0:T(4,128)S(1)}, u32[]{:S(2)}, u32[]{:S(2)}) %all-to-all-start) | async-done | bytes 917536 | tf_op jit(solution)/shard_map/all_to_all | solution.py:309
  46.5 0.2 copy.137
  46.7 0.1 fusion.8
  46.8 0.9 fusion.2
  47.8 1.0 gather_fusion
  48.8 1.7 %copy.170 = f32[256,12,128]{2,0,1:T(8,128)} copy(f32[256,12,128]{2,1,0:T(8,128)S(1)} %gather_fusion) | data formatting | bytes 3145728 | tf_op jit(solution)/shard_map/gather | solution.py:317
  50.4 28.7 %shard_map.94 = (f32[3,256,128]{2,1,0:T(8,128)}, f32[3,256,128]{2,1,0:T(8,128)}, f32[11,256,128]{2,1,0:T(8,128)}) custom-call(f32[3,256,128]{2,1,0:T(8,128)} %get-tuple-element.60.t_ref, f32[12,256,128]{2,1,0:T(8,128)} %bitcast.103, f32[3,256,128]{2,1,0:T(8,128)} %get-tuple-element.59.c_ref), custom_call_target="tpu_custom_call" | custom-call | tf_op jit(solution)/shard_map/pallas_call | solution.py:206
  79.2 1.2 %pad_maximum_fusion.1 = f32[256,6,128]{2,0,1:T(8,128)S(1)} fusion(f32[256,3,128]{2,0,1:T(8,128)} %bitcast.127, f32[256,3,128]{2,0,1:T(8,128)} %bitcast.126), kind=kLoop, calls=%fused_computation.8 | loop fusion | flops 196608 | bytes 1572864 | tf_op jit(solution)/shard_map/concatenate | solution.py:326
  80.3 1.0 copy.146
  81.4 8.1 %all-to-all-start.1 = ((f32[64,4,6,128]{3,1,2,0:T(4,128)}), f32[64,4,6,128]{3,1,2,0:T(4,128)S(1)}, u32[]{:S(2)}, u32[]{:S(2)}) async-start(f32[64,4,6,128]{3,1,2,0:T(4,128)} %copy.146), calls=%async_computation.1 | async-start | bytes 1572864 | tf_op jit(solution)/shard_map/all_to_all | solution.py:325
  89.5 1.8 %copy.154 = f32[256,11,128]{0,2,1:T(8,128)S(1)} copy(f32[256,11,128]{2,0,1:T(8,128)} %bitcast.114) | data formatting | bytes 2883584
  91.3 0.8 fusion.1
  92.2 0.7 fusion.24
  92.9 3.2 %collective-permute-start.3 = (f32[3,2,3,128]{3,1,2,0:T(2,128)S(1)}, f32[3,2,3,128]{3,1,2,0:T(2,128)S(1)}, u32[]{:S(2)}, u32[]{:S(2)}) collective-permute-start(f32[3,2,3,128]{3,1,2,0:T(2,128)S(1)} %bitcast.137), channel_id=1, source_target_pairs={{0,1},{1,2},{2,3},{4,5},{5,6},{6,7},{8,9},{9,10},{10,11},{12,13},{... | collective-permute-start | bytes 27656 | tf_op jit(solution)/shard_map/ppermute | solution.py:21
  96.1 0.1 split.56
  96.2 0.2 copy.150
  96.4 3.3 %collective-permute-start.2 = (f32[3,2,3,16]{3,1,2,0:T(2,128)S(1)}, f32[3,2,3,16]{3,1,2,0:T(2,128)S(1)}, u32[]{:S(2)}, u32[]{:S(2)}) collective-permute-start(f32[3,2,3,16]{3,1,2,0:T(2,128)S(1)} %bitcast.134), channel_id=1, source_target_pairs={{0,4},{4,8},{8,12},{12,16},{16,20},{20,24},{24,28},{1,5},{5,9},{9,... | collective-permute-start | bytes 3464 | tf_op jit(solution)/shard_map/ppermute | solution.py:21
  99.7 0.1 broadcast_multiply_fusion
  99.7 0.6 pad_add_fusion
  100.4 3.9 %collective-permute-done.2 = f32[3,2,3,16]{3,1,2,0:T(2,128)S(1)} collective-permute-done((f32[3,2,3,16]{3,1,2,0:T(2,128)S(1)}, f32[3,2,3,16]{3,1,2,0:T(2,128)S(1)}, u32[]{:S(2)}, u32[]{:S(2)}) %collective-permute-start.2) | collective-permute-done | bytes 1184 | tf_op jit(solution)/shard_map/ppermute | solution.py:21
  104.3 0.2 copy.151
  104.5 8.1 %all-to-all-done.1 = f32[64,4,6,128]{3,1,2,0:T(4,128)S(1)} async-done(((f32[64,4,6,128]{3,1,2,0:T(4,128)}), f32[64,4,6,128]{3,1,2,0:T(4,128)S(1)}, u32[]{:S(2)}, u32[]{:S(2)}) %all-to-all-start.1) | async-done | bytes 786464 | tf_op jit(solution)/shard_map/all_to_all | solution.py:325
  112.6 0.1 copy.147
  112.7 0.2 copy.171
  112.9 0.0 copy-start.2
  112.9 0.0 copy-start.3
  112.9 0.3 copy.148
  113.2 0.9 fusion.26
  114.1 0.1 add_add_fusion
  114.3 0.0 copy-start.4
  114.3 0.2 scatter-add.11
  114.5 0.0 collective-permute-done.3
  114.5 0.1 scatter-add.14
  114.6 0.4 copy-done.4
  114.9 0.7 copy-done.1
  (23 shorter events, 0.2 us)
Async XLA Ops:
  7.1 14.1 %copy-start = (f32[3,2,3,16,128]{4,3,2,1,0:T(8,128)S(1)}, f32[3,2,3,16,128]{4,3,2,1,0:T(8,128)}, u32[]{:S(2)}) copy-start(f32[3,2,3,16,128]{4,3,2,1,0:T(8,128)} %param.13) | copy-start | bytes 442372
  7.1 16.9 %copy-start.5 = (f32[2,2,3,16,128]{4,3,2,1,0:T(8,128)S(1)}, f32[2,2,3,16,128]{4,3,2,1,0:T(8,128)}, u32[]{:S(2)}) copy-start(f32[2,2,3,16,128]{4,3,2,1,0:T(8,128)} %param.14) | copy-start | bytes 294916
  8.2 38.3 %all-to-all-start = ((f32[64,4,7,128]{3,1,2,0:T(4,128)}), f32[64,4,7,128]{3,1,2,0:T(4,128)S(1)}, u32[]{:S(2)}, u32[]{:S(2)}) async-start(f32[64,4,7,128]{3,1,2,0:T(4,128)} %copy.136), calls=%async_computation | async-start | bytes 1835008 | tf_op jit(solution)/shard_map/all_to_all | solution.py:309
  21.2 21.8 %copy-start.6 = (f32[2,3,16,128]{3,2,1,0:T(8,128)S(1)}, f32[2,3,16,128]{3,2,1,0:T(8,128)}, u32[]{:S(2)}) copy-start(f32[2,3,16,128]{3,2,1,0:T(8,128)} %param.15) | copy-start | bytes 147460
  21.2 21.6 %collective-permute-start.1 = (f32[3,2,3,128]{3,1,2,0:T(2,128)S(1)}, f32[3,2,3,128]{3,1,2,0:T(2,128)S(1)}, u32[]{:S(2)}, u32[]{:S(2)}) collective-permute-start(f32[3,2,3,128]{3,1,2,0:T(2,128)S(1)} %bitcast.138), channel_id=1, source_target_pairs={{1,0},{2,1},{3,2},{5,4},{6,5},{7,6},{9,8},{10,9},{11,10},{13,12},{... | collective-permute-start | bytes 27656 | tf_op jit(solution)/shard_map/ppermute | solution.py:21
  22.7 19.7 %collective-permute-start = (f32[3,2,3,16]{3,1,2,0:T(2,128)S(1)}, f32[3,2,3,16]{3,1,2,0:T(2,128)S(1)}, u32[]{:S(2)}, u32[]{:S(2)}) collective-permute-start(f32[3,2,3,16]{3,1,2,0:T(2,128)S(1)} %bitcast.133), channel_id=1, source_target_pairs={{4,0},{8,4},{12,8},{16,12},{20,16},{24,20},{28,24},{5,1},{9,5},{13... | collective-permute-start | bytes 3464 | tf_op jit(solution)/shard_map/ppermute | solution.py:21
  81.4 31.2 %all-to-all-start.1 = ((f32[64,4,6,128]{3,1,2,0:T(4,128)}), f32[64,4,6,128]{3,1,2,0:T(4,128)S(1)}, u32[]{:S(2)}, u32[]{:S(2)}) async-start(f32[64,4,6,128]{3,1,2,0:T(4,128)} %copy.146), calls=%async_computation.1 | async-start | bytes 1572864 | tf_op jit(solution)/shard_map/all_to_all | solution.py:325
  92.9 21.6 %collective-permute-start.3 = (f32[3,2,3,128]{3,1,2,0:T(2,128)S(1)}, f32[3,2,3,128]{3,1,2,0:T(2,128)S(1)}, u32[]{:S(2)}, u32[]{:S(2)}) collective-permute-start(f32[3,2,3,128]{3,1,2,0:T(2,128)S(1)} %bitcast.137), channel_id=1, source_target_pairs={{0,1},{1,2},{2,3},{4,5},{5,6},{6,7},{8,9},{9,10},{10,11},{12,13},{... | collective-permute-start | bytes 27656 | tf_op jit(solution)/shard_map/ppermute | solution.py:21
  96.4 7.9 %collective-permute-start.2 = (f32[3,2,3,16]{3,1,2,0:T(2,128)S(1)}, f32[3,2,3,16]{3,1,2,0:T(2,128)S(1)}, u32[]{:S(2)}, u32[]{:S(2)}) collective-permute-start(f32[3,2,3,16]{3,1,2,0:T(2,128)S(1)} %bitcast.134), channel_id=1, source_target_pairs={{0,4},{4,8},{8,12},{12,16},{16,20},{20,24},{24,28},{1,5},{5,9},{9,... | collective-permute-start | bytes 3464 | tf_op jit(solution)/shard_map/ppermute | solution.py:21
  112.9 1.2 %copy-start.2 = (f32[3,96,128]{2,1,0:T(8,128)S(1)}, f32[3,96,128]{2,1,0:T(8,128)}, u32[]{:S(2)}) copy-start(f32[3,96,128]{2,1,0:T(8,128)} %get-tuple-element.65) | copy-start | bytes 442372
  112.9 1.2 %copy-start.3 = (f32[3,2,3,16,128]{4,3,2,1,0:T(8,128)S(1)}, f32[3,2,3,16,128]{4,3,2,1,0:T(8,128)}, u32[]{:S(2)}) copy-start(f32[3,2,3,16,128]{4,3,2,1,0:T(8,128)} %param.16) | copy-start | bytes 442372
  114.3 0.7 copy-start.4
  114.9 0.7 copy-start.1

commit v11 on v9

--- a/solution.py
+++ b/solution.py
@@ -193,17 +193,14 @@
 
 
 def run_pairs(targets, payload, cotangent):
-    number = targets.shape[0]
+    number = targets.shape[1]
     age_count = targets.shape[-1]
     step = min(number, BLOCK_PAIRS)
 
     def spec(rows):
         return pl.BlockSpec((rows, step, age_count), lambda i: (0, i, 0))
 
-    t_rows = jnp.transpose(targets, (1, 0, 2))
-    s_rows = jnp.transpose(payload, (1, 0, 2))
-    c_rows = jnp.transpose(cotangent, (1, 0, 2))
-    velocity, grad_targets, grad_payload = pl.pallas_call(
+    return pl.pallas_call(
         pair_kernel,
         grid=(number // step,),
         in_specs=[spec(3), spec(12), spec(3)],
@@ -213,12 +210,7 @@
             jax.ShapeDtypeStruct((3, number, age_count), jnp.float32),
             jax.ShapeDtypeStruct((11, number, age_count), jnp.float32),
         ],
-    )(t_rows, s_rows, c_rows)
-    return (
-        jnp.transpose(velocity, (1, 0, 2)),
-        jnp.transpose(grad_targets, (1, 0, 2)),
-        jnp.transpose(grad_payload, (1, 0, 2)),
-    )
+    )(targets, payload, cotangent)
 
 
 def onehot_sum(indices, rows, values):
@@ -261,15 +253,33 @@
             [nodes, trail_end, shed_end, trail_gamma[None], shed_gamma[None], core_radius[None]],
             axis=0,
         )
-        return jnp.transpose(stacked.reshape(12, blocks_here, age_here), (1, 0, 2))
+        return stacked.reshape(12, blocks_here, age_here)
 
     payload, build_pullback = jax.vjp(build, positions, next_ages, next_stations, strengths)
 
     def to_rows(array):
-        return jnp.transpose(array.reshape(array.shape[0], blocks_here, age_here), (1, 0, 2))
+        return array.reshape(array.shape[0], blocks_here, age_here)
 
     def from_rows(array):
-        return jnp.transpose(array, (1, 0, 2)).reshape(shape_here)
+        return array.reshape(shape_here)
+
+    def pick_rows(selector, values):
+        return jnp.einsum(
+            "sb,rba->rsa",
+            selector,
+            values,
+            precision=lax.Precision.HIGHEST,
+            preferred_element_type=jnp.float32,
+        )
+
+    def sum_rows(selector, values):
+        return jnp.einsum(
+            "sb,rsa->rba",
+            selector,
+            values,
+            precision=lax.Precision.HIGHEST,
+            preferred_element_type=jnp.float32,
+        )
 
     target_blocks = to_rows(positions)
     seed_blocks = to_rows(adjoint_seed)
@@ -289,13 +299,7 @@
         target_ids[:, None] == jnp.arange(blocks_here, dtype=jnp.int32)[None, :]
     ).astype(jnp.float32)
     slot_block = jnp.dot(slot_pick, block_pick, preferred_element_type=jnp.float32)
-    blocks_sent = jnp.concatenate([target_blocks, seed_blocks], axis=1)
-    rows_sent = jnp.dot(
-        slot_block,
-        blocks_sent.reshape(blocks_here, -1),
-        precision=lax.Precision.HIGHEST,
-        preferred_element_type=jnp.float32,
-    ).reshape(slot_count, 6, age_here)
+    rows_sent = pick_rows(slot_block, jnp.concatenate([target_blocks, seed_blocks], axis=0))
     ident = jnp.dot(
         slot_pick,
         (source_ids + 1).astype(jnp.float32),
@@ -303,36 +307,40 @@
         preferred_element_type=jnp.float32,
     )
     outgoing = jnp.concatenate(
-        [rows_sent, jnp.broadcast_to(ident[:, None, None], (slot_count, 1, age_here))],
-        axis=1,
+        [rows_sent, jnp.broadcast_to(ident[None, :, None], (1, slot_count, age_here))],
+        axis=0,
     )
     received = lax.all_to_all(
-        outgoing.reshape(group_size, capacity, 7, age_here),
+        outgoing.reshape(7, group_size, capacity, age_here),
         ("turb", "age"),
-        split_axis=0,
-        concat_axis=0,
+        split_axis=1,
+        concat_axis=1,
         tiled=True,
-    ).reshape(slot_count, 7, age_here)
-    asked = received[:, 6, 0].astype(jnp.int32) - 1
-    slot_payload = payload[jnp.clip(asked, 0, blocks_here - 1)]
+    ).reshape(7, slot_count, age_here)
+    asked = received[6, :, 0].astype(jnp.int32) - 1
+    slot_payload = payload[:, jnp.clip(asked, 0, blocks_here - 1)]
     slot_velocity, slot_grad, payload_terms = run_pairs(
-        received[:, 0:3], slot_payload, received[:, 3:6] * time_step
+        received[0:3], slot_payload, received[3:6] * time_step
     )
     payload_terms = jnp.concatenate(
-        [payload_terms, jnp.zeros_like(payload_terms[:, :1])], axis=1
-    )
-    payload_grad = onehot_sum(asked, blocks_here, payload_terms)
+        [payload_terms, jnp.zeros_like(payload_terms[:1])], axis=0
+    )
+    asked_pick = (
+        asked[:, None] == jnp.arange(blocks_here, dtype=jnp.int32)[None, :]
+    ).astype(jnp.float32)
+    payload_grad = sum_rows(asked_pick, payload_terms)
     answered = lax.all_to_all(
-        jnp.concatenate([slot_velocity, slot_grad], axis=1).reshape(
-            group_size, capacity, 6, age_here
+        jnp.concatenate([slot_velocity, slot_grad], axis=0).reshape(
+            6, group_size, capacity, age_here
         ),
         ("turb", "age"),
-        split_axis=0,
-        concat_axis=0,
+        split_axis=1,
+        concat_axis=1,
         tiled=True,
-    ).reshape(slot_count, 6, age_here)[slot_index]
-    velocity = onehot_sum(target_ids, blocks_here, answered[:, 0:3])
-    target_grad = onehot_sum(target_ids, blocks_here, answered[:, 3:6])
+    ).reshape(6, slot_count, age_here)
+    summed = sum_rows(slot_block, answered)
+    velocity = summed[0:3]
+    target_grad = summed[3:6]
     advected = positions + time_step * from_rows(velocity)
     advected = advected.at[0].add(time_step)
     grad_nodes, grad_after_age, grad_after_station, grad_strengths = build_pullback(payload_grad)

time: 116 us -> 117 us (level)
  waiting for transfers between devices: 32.9 us -> 36.1 us
    unnamed x19 -> x18, local copies, waits for them, and re-layouts: 4.71 us -> 1.11 us
    gather x3 -> x2, local copies, waits for them, and re-layouts: 3.42 us -> 5.59 us  [local(): slot_payload = payload[:, jnp.clip(asked, 0, blocks_here - 1)]]
    ppermute x4, waiting for transfers between devices: 22.6 us -> 24.7 us  [shifted_2(): lax.ppermute(value, axis, [(source, source + steps) for source in range(l...]
    dot_general x4 -> x3, matrix products: 2.22 us -> 3.04 us  [the longest x1 1.8 us: pick_rows(): jnp.einsum('sb,rba->rsa', selector, values, precision=lax.Precision.HIGHE...]
  transfers between devices with their start and end apart: 6 -> 6, of which waited for: 4 -> 4; matrix products, arithmetic and copies ran while one was open for 7% -> 3% of each run, Pallas kernels for 0% -> 0%
where the time goes in v11:
time: 117 us
  waiting for transfers between devices  36.1 us (31%)
  starting transfers between devices  29.1 us (25%)
  Pallas kernels  28.7 us (25%)
  local copies, waits for them, and re-layouts  12.8 us (11%)
  matrix products  4.81 us (4%)
  other arithmetic  4.15 us (4%)
    pallas_call x1, Pallas kernels, run_pairs(): pl.pallas_call(pair_kernel, grid=(number // step,), in_specs=[spec(3), sp...  28.7 us
    ppermute x4, waiting for transfers between devices, shifted_2(): lax.ppermute(value, axis, [(source, source + steps) for source in range(l...  24.7 us
    all_to_all x1, starting transfers between devices, local(): lax.all_to_all(outgoing.reshape(7, group_size, capacity, age_here), ('tur...  13 us
    ppermute x4, starting transfers between devices, shifted_2(): lax.ppermute(value, axis, [(source, source + steps) for source in range(l...  9.07 us
    all_to_all x1, waiting for transfers between devices, local(): lax.all_to_all(jnp.concatenate([slot_velocity, slot_grad], axis=0).reshap...  8.07 us
    all_to_all x1, starting transfers between devices, local(): lax.all_to_all(jnp.concatenate([slot_velocity, slot_grad], axis=0).reshap...  7.04 us
    gather x2, local copies, waits for them, and re-layouts, local(): slot_payload = payload[:, jnp.clip(asked, 0, blocks_here - 1)]  5.59 us
    all_to_all x1, waiting for transfers between devices, local(): lax.all_to_all(outgoing.reshape(7, group_size, capacity, age_here), ('tur...  3.31 us
  transfers between devices with their start and end apart: 6, of which 4 were waited for; matrix products, arithmetic and copies ran while one was open for 3% of the time, Pallas kernels for 0%

profile of v11, /device:TPU:1, one launch (start us, length us, event | category | flops | bytes accessed | tf_op | source)
XLA Modules:
  0.0 116.8 jit_solution(15772524206792317836)
XLA Ops:
  0.6 0.9 convert_reduce_fusion
  1.5 0.7 multiply_add_fusion
  2.2 0.8 fusion.4
  3.0 1.0 convolution_bitcast_fusion.3
  4.0 1.8 %convolution_bitcast_fusion = f32[6,256,128]{1,2,0:T(8,128)S(1)} fusion(f32[256,96,1]{0,1,2:T(8,128)S(1)} %convolution_bitcast_fusion.3, f32[3,96,128]{2,1,0:T(8,128)} %bitcast.77, f32[3,96,128]{2,1,0:T(8,128)} %bitcast.64), kind=kOutput, calls=%fused_computation.2 | convolution fusion | flops 226566144 | bytes 1179648 | tf_op jit(solution)/shard_map/sb,rba->rsa/dot_general | solution.py:267
  5.8 0.1 pad_maximum_fusion
  5.9 0.3 copy.160
  6.2 0.0 copy-start
  6.2 0.0 copy-start.5
  6.2 1.1 copy.161
  7.3 13.0 %all-to-all-start = ((f32[7,64,4,128]{3,2,0,1:T(4,128)}), f32[7,64,4,128]{3,2,0,1:T(4,128)S(1)}, u32[]{:S(2)}, u32[]{:S(2)}) async-start(f32[7,64,4,128]{3,2,0,1:T(4,128)} %copy.161), calls=%async_computation | async-start | bytes 1835008 | tf_op jit(solution)/shard_map/all_to_all | solution.py:313
  20.3 0.0 copy-done
  20.3 0.0 copy-start.6
  20.3 1.3 %collective-permute-start.1 = (f32[3,2,3,128]{3,1,2,0:T(2,128)S(1)}, f32[3,2,3,128]{3,1,2,0:T(2,128)S(1)}, u32[]{:S(2)}, u32[]{:S(2)}) collective-permute-start(f32[3,2,3,128]{3,1,2,0:T(2,128)S(1)} %bitcast.93), channel_id=1, source_target_pairs={{1,0},{2,1},{3,2},{5,4},{6,5},{7,6},{9,8},{10,9},{11,10},{13,12},{... | collective-permute-start | bytes 27656 | tf_op jit(solution)/shard_map/ppermute | solution.py:21
  21.6 0.2 copy.163
  21.8 1.3 %collective-permute-start = (f32[3,2,3,16]{3,1,2,0:T(2,128)S(1)}, f32[3,2,3,16]{3,1,2,0:T(2,128)S(1)}, u32[]{:S(2)}, u32[]{:S(2)}) collective-permute-start(f32[3,2,3,16]{3,1,2,0:T(2,128)S(1)} %bitcast.88), channel_id=1, source_target_pairs={{4,0},{8,4},{12,8},{16,12},{20,16},{24,20},{28,24},{5,1},{9,5},{13... | collective-permute-start | bytes 3464 | tf_op jit(solution)/shard_map/ppermute | solution.py:21
  23.1 0.0 copy-done.5
  23.2 0.1 slice_multiply_fusion.1
  23.3 0.1 slice.140
  23.4 18.2 %collective-permute-done = f32[3,2,3,16]{3,1,2,0:T(2,128)S(1)} collective-permute-done((f32[3,2,3,16]{3,1,2,0:T(2,128)S(1)}, f32[3,2,3,16]{3,1,2,0:T(2,128)S(1)}, u32[]{:S(2)}, u32[]{:S(2)}) %collective-permute-start) | collective-permute-done | bytes 1184 | tf_op jit(solution)/shard_map/ppermute | solution.py:21
  41.5 0.1 concatenate.54
  41.7 0.1 maximum_dynamic-update-slice_fusion
  41.8 0.0 collective-permute-done.1
  41.9 0.0 copy-done.6
  41.9 0.4 copy.169
  42.3 3.3 %all-to-all-done = f32[7,64,4,128]{3,2,0,1:T(4,128)S(1)} async-done(((f32[7,64,4,128]{3,2,0,1:T(4,128)}), f32[7,64,4,128]{3,2,0,1:T(4,128)S(1)}, u32[]{:S(2)}, u32[]{:S(2)}) %all-to-all-start) | async-done | bytes 917536 | tf_op jit(solution)/shard_map/all_to_all | solution.py:313
  45.6 0.2 copy.168
  45.8 0.1 fusion.5
  45.9 0.1 fusion.20
  46.1 1.0 copy.172
  47.1 0.8 copy.162
  47.9 2.3 %gather_fusion = f32[256,12,128]{2,1,0:T(8,128)} fusion(f32[12,96,128]{2,0,1:T(8,128)S(1)} %copy.169, s32[1024]{0:T(1024)S(1)} %pad_clamp_fusion), kind=kCustom, calls=%fused_computation | custom fusion | bytes 3146752 | tf_op jit(solution)/shard_map/gather | solution.py:321
  50.2 3.3 %copy.185 = f32[256,12,128]{2,0,1:T(8,128)} copy(f32[256,12,128]{2,1,0:T(8,128)} %gather_fusion) | data formatting | bytes 3145728 | tf_op jit(solution)/shard_map/gather | solution.py:321
  53.5 28.7 %shard_map.94 = (f32[3,256,128]{2,1,0:T(8,128)}, f32[3,256,128]{2,1,0:T(8,128)}, f32[11,256,128]{2,1,0:T(8,128)}) custom-call(f32[3,256,128]{2,1,0:T(8,128)} %bitcast.71, f32[12,256,128]{2,1,0:T(8,128)} %bitcast.63, f32[3,256,128]{2,1,0:T(8,128)} %bitcast.70), custom_call_target="tpu_custom_call" | custom-call | tf_op jit(solution)/shard_map/pallas_call | solution.py:203
  82.2 1.2 pad_maximum_fusion.1
  83.4 0.0 copy-start.1
  83.4 1.0 copy.173
  84.4 7.0 %all-to-all-start.1 = ((f32[6,64,4,128]{3,2,0,1:T(4,128)}), f32[6,64,4,128]{3,2,0,1:T(4,128)S(1)}, u32[]{:S(2)}, u32[]{:S(2)}) async-start(f32[6,64,4,128]{3,2,0,1:T(4,128)} %copy.173), calls=%async_computation.1 | async-start | bytes 1572864 | tf_op jit(solution)/shard_map/all_to_all | solution.py:332
  91.5 0.0 copy-done.1
  91.5 0.6 convolution_bitcast_fusion.1
  92.2 3.2 %collective-permute-start.3 = (f32[3,2,3,128]{3,1,2,0:T(2,128)S(1)}, f32[3,2,3,128]{3,1,2,0:T(2,128)S(1)}, u32[]{:S(2)}, u32[]{:S(2)}) collective-permute-start(f32[3,2,3,128]{3,1,2,0:T(2,128)S(1)} %bitcast.92), channel_id=1, source_target_pairs={{0,1},{1,2},{2,3},{4,5},{5,6},{6,7},{8,9},{9,10},{10,11},{12,13},{... | collective-permute-start | bytes 27656 | tf_op jit(solution)/shard_map/ppermute | solution.py:21
  95.4 0.1 split.56
  95.5 0.2 copy.175
  95.7 3.3 %collective-permute-start.2 = (f32[3,2,3,16]{3,1,2,0:T(2,128)S(1)}, f32[3,2,3,16]{3,1,2,0:T(2,128)S(1)}, u32[]{:S(2)}, u32[]{:S(2)}) collective-permute-start(f32[3,2,3,16]{3,1,2,0:T(2,128)S(1)} %bitcast.89), channel_id=1, source_target_pairs={{0,4},{4,8},{8,12},{12,16},{16,20},{20,24},{24,28},{1,5},{5,9},{9,... | collective-permute-start | bytes 3464 | tf_op jit(solution)/shard_map/ppermute | solution.py:21
  99.0 0.1 broadcast_multiply_fusion
  99.0 0.6 pad_add_fusion
  99.7 6.6 %collective-permute-done.2 = f32[3,2,3,16]{3,1,2,0:T(2,128)S(1)} collective-permute-done((f32[3,2,3,16]{3,1,2,0:T(2,128)S(1)}, f32[3,2,3,16]{3,1,2,0:T(2,128)S(1)}, u32[]{:S(2)}, u32[]{:S(2)}) %collective-permute-start.2) | collective-permute-done | bytes 1184 | tf_op jit(solution)/shard_map/ppermute | solution.py:21
  106.3 0.2 copy.176
  106.4 0.0 copy-start.3
  106.4 8.1 %all-to-all-done.1 = f32[6,64,4,128]{3,2,0,1:T(4,128)S(1)} async-done(((f32[6,64,4,128]{3,2,0,1:T(4,128)}), f32[6,64,4,128]{3,2,0,1:T(4,128)S(1)}, u32[]{:S(2)}, u32[]{:S(2)}) %all-to-all-start.1) | async-done | bytes 786464 | tf_op jit(solution)/shard_map/all_to_all | solution.py:332
  114.5 0.1 copy.174
  114.6 0.6 convolution_bitcast_fusion.2
  115.3 0.0 copy-done.3
  115.3 0.1 add_add_fusion
  115.5 0.0 copy-start.4
  115.5 0.2 scatter-add.11
  115.7 0.0 collective-permute-done.3
  115.7 0.1 scatter-add.14
  115.8 0.4 copy-done.4
  116.1 0.0 copy-start.2
  116.1 0.7 copy-done.2
  (26 shorter events, 0.3 us)
Async XLA Ops:
  6.2 14.1 %copy-start = (f32[3,2,3,16,128]{4,3,2,1,0:T(8,128)S(1)}, f32[3,2,3,16,128]{4,3,2,1,0:T(8,128)}, u32[]{:S(2)}) copy-start(f32[3,2,3,16,128]{4,3,2,1,0:T(8,128)} %param.13) | copy-start | bytes 442372
  6.2 16.9 %copy-start.5 = (f32[2,2,3,16,128]{4,3,2,1,0:T(8,128)S(1)}, f32[2,2,3,16,128]{4,3,2,1,0:T(8,128)}, u32[]{:S(2)}) copy-start(f32[2,2,3,16,128]{4,3,2,1,0:T(8,128)} %param.14) | copy-start | bytes 294916
  7.3 38.3 %all-to-all-start = ((f32[7,64,4,128]{3,2,0,1:T(4,128)}), f32[7,64,4,128]{3,2,0,1:T(4,128)S(1)}, u32[]{:S(2)}, u32[]{:S(2)}) async-start(f32[7,64,4,128]{3,2,0,1:T(4,128)} %copy.161), calls=%async_computation | async-start | bytes 1835008 | tf_op jit(solution)/shard_map/all_to_all | solution.py:313
  20.3 21.6 %copy-start.6 = (f32[2,3,16,128]{3,2,1,0:T(8,128)S(1)}, f32[2,3,16,128]{3,2,1,0:T(8,128)}, u32[]{:S(2)}) copy-start(f32[2,3,16,128]{3,2,1,0:T(8,128)} %param.15) | copy-start | bytes 147460
  20.3 21.5 %collective-permute-start.1 = (f32[3,2,3,128]{3,1,2,0:T(2,128)S(1)}, f32[3,2,3,128]{3,1,2,0:T(2,128)S(1)}, u32[]{:S(2)}, u32[]{:S(2)}) collective-permute-start(f32[3,2,3,128]{3,1,2,0:T(2,128)S(1)} %bitcast.93), channel_id=1, source_target_pairs={{1,0},{2,1},{3,2},{5,4},{6,5},{7,6},{9,8},{10,9},{11,10},{13,12},{... | collective-permute-start | bytes 27656 | tf_op jit(solution)/shard_map/ppermute | solution.py:21
  21.8 19.7 %collective-permute-start = (f32[3,2,3,16]{3,1,2,0:T(2,128)S(1)}, f32[3,2,3,16]{3,1,2,0:T(2,128)S(1)}, u32[]{:S(2)}, u32[]{:S(2)}) collective-permute-start(f32[3,2,3,16]{3,1,2,0:T(2,128)S(1)} %bitcast.88), channel_id=1, source_target_pairs={{4,0},{8,4},{12,8},{16,12},{20,16},{24,20},{28,24},{5,1},{9,5},{13... | collective-permute-start | bytes 3464 | tf_op jit(solution)/shard_map/ppermute | solution.py:21
  83.4 8.1 %copy-start.1 = (f32[11,256,128]{2,1,0:T(8,128)S(1)}, f32[11,256,128]{2,1,0:T(8,128)}, u32[]{:S(2)}) copy-start(f32[11,256,128]{2,1,0:T(8,128)} %get-tuple-element.44) | copy-start | bytes 4325380
  84.4 30.1 %all-to-all-start.1 = ((f32[6,64,4,128]{3,2,0,1:T(4,128)}), f32[6,64,4,128]{3,2,0,1:T(4,128)S(1)}, u32[]{:S(2)}, u32[]{:S(2)}) async-start(f32[6,64,4,128]{3,2,0,1:T(4,128)} %copy.173), calls=%async_computation.1 | async-start | bytes 1572864 | tf_op jit(solution)/shard_map/all_to_all | solution.py:332
  92.2 23.5 %collective-permute-start.3 = (f32[3,2,3,128]{3,1,2,0:T(2,128)S(1)}, f32[3,2,3,128]{3,1,2,0:T(2,128)S(1)}, u32[]{:S(2)}, u32[]{:S(2)}) collective-permute-start(f32[3,2,3,128]{3,1,2,0:T(2,128)S(1)} %bitcast.92), channel_id=1, source_target_pairs={{0,1},{1,2},{2,3},{4,5},{5,6},{6,7},{8,9},{9,10},{10,11},{12,13},{... | collective-permute-start | bytes 27656 | tf_op jit(solution)/shard_map/ppermute | solution.py:21
  95.7 10.6 %collective-permute-start.2 = (f32[3,2,3,16]{3,1,2,0:T(2,128)S(1)}, f32[3,2,3,16]{3,1,2,0:T(2,128)S(1)}, u32[]{:S(2)}, u32[]{:S(2)}) collective-permute-start(f32[3,2,3,16]{3,1,2,0:T(2,128)S(1)} %bitcast.89), channel_id=1, source_target_pairs={{0,4},{4,8},{8,12},{12,16},{16,20},{20,24},{24,28},{1,5},{5,9},{9,... | collective-permute-start | bytes 3464 | tf_op jit(solution)/shard_map/ppermute | solution.py:21
  106.4 8.9 %copy-start.3 = (f32[3,2,3,16,128]{4,3,2,1,0:T(8,128)S(1)}, f32[3,2,3,16,128]{4,3,2,1,0:T(8,128)}, u32[]{:S(2)}) copy-start(f32[3,2,3,16,128]{4,3,2,1,0:T(8,128)} %param.16) | copy-start | bytes 442372
  115.5 0.7 copy-start.4
  116.1 0.7 copy-start.2

commit v12 on v11

--- a/solution.py
+++ b/solution.py
@@ -318,7 +318,11 @@
         tiled=True,
     ).reshape(7, slot_count, age_here)
     asked = received[6, :, 0].astype(jnp.int32) - 1
-    slot_payload = payload[:, jnp.clip(asked, 0, blocks_here - 1)]
+    safe_pick = (
+        jnp.clip(asked, 0, blocks_here - 1)[:, None]
+        == jnp.arange(blocks_here, dtype=jnp.int32)[None, :]
+    ).astype(jnp.float32)
+    slot_payload = pick_rows(safe_pick, payload)
     slot_velocity, slot_grad, payload_terms = run_pairs(
         received[0:3], slot_payload, received[3:6] * time_step
     )

time: 117 us -> 114 us (0.974)
  local copies, waits for them, and re-layouts: 12.8 us -> 7.1 us
  matrix products: 4.81 us -> 6.82 us
    gather x2 -> x0, local copies, waits for them, and re-layouts: 5.59 us -> none  [local(): slot_payload = payload[:, jnp.clip(asked, 0, blocks_here - 1)]]
    dot_general x1 -> x2, matrix products: 1.8 us -> 3.81 us  [pick_rows(): jnp.einsum('sb,rba->rsa', selector, values, precision=lax.Precision.HIGHE...]
where the time goes in v12:
time: 114 us; the launch traced here: 113 us
  waiting for transfers between devices  36.5 us (32%)
  starting transfers between devices  29.1 us (26%)
  Pallas kernels  28.7 us (25%)
  local copies, waits for them, and re-layouts  7.1 us (6%)
  matrix products  6.82 us (6%)
  other arithmetic  4.11 us (4%)
    pallas_call x1, Pallas kernels, run_pairs(): pl.pallas_call(pair_kernel, grid=(number // step,), in_specs=[spec(3), sp...  28.7 us
    ppermute x4, waiting for transfers between devices, shifted_2(): lax.ppermute(value, axis, [(source, source + steps) for source in range(l...  24.7 us
    all_to_all x1, starting transfers between devices, local(): lax.all_to_all(outgoing.reshape(7, group_size, capacity, age_here), ('tur...  13.1 us
    ppermute x4, starting transfers between devices, shifted_2(): lax.ppermute(value, axis, [(source, source + steps) for source in range(l...  9.07 us
    all_to_all x1, waiting for transfers between devices, local(): lax.all_to_all(jnp.concatenate([slot_velocity, slot_grad], axis=0).reshap...  8.08 us
    all_to_all x1, starting transfers between devices, local(): lax.all_to_all(jnp.concatenate([slot_velocity, slot_grad], axis=0).reshap...  6.9 us
    dot_general x2, matrix products, pick_rows(): jnp.einsum('sb,rba->rsa', selector, values, precision=lax.Precision.HIGHE...  3.81 us
    all_to_all x1, waiting for transfers between devices, local(): lax.all_to_all(outgoing.reshape(7, group_size, capacity, age_here), ('tur...  3.68 us
  transfers between devices with their start and end apart: 6, of which 4 were waited for; matrix products, arithmetic and copies ran while one was open for 3% of the time, Pallas kernels for 0%

profile of v12, /device:TPU:1, one launch (start us, length us, event | category | flops | bytes accessed | tf_op | source)
XLA Modules:
  0.0 113.4 jit_solution(12920420633249628047)
XLA Ops:
  0.6 0.9 convert_reduce_fusion
  1.5 0.7 multiply_add_fusion
  2.2 0.8 fusion.5
  3.0 1.0 convolution_bitcast_fusion.4
  4.0 1.8 %convolution_bitcast_fusion.1 = f32[6,256,128]{1,2,0:T(8,128)S(1)} fusion(f32[256,96,1]{0,1,2:T(8,128)S(1)} %convolution_bitcast_fusion.4, f32[3,96,128]{2,1,0:T(8,128)} %bitcast.77, f32[3,96,128]{2,1,0:T(8,128)} %bitcast.64), kind=kOutput, calls=%fused_computation.1 | convolution fusion | flops 226566144 | bytes 1179648 | tf_op jit(solution)/shard_map/sb,rba->rsa/dot_general | solution.py:267
  5.8 0.1 pad_maximum_fusion
  5.9 0.3 copy.132
  6.2 0.0 copy-start
  6.2 1.1 copy.133
  7.3 0.0 copy-start.5
  7.3 13.1 %all-to-all-start = ((f32[7,64,4,128]{3,2,0,1:T(4,128)}), f32[7,64,4,128]{3,2,0,1:T(4,128)S(1)}, u32[]{:S(2)}, u32[]{:S(2)}) async-start(f32[7,64,4,128]{3,2,0,1:T(4,128)} %copy.133), calls=%async_computation | async-start | bytes 1835008 | tf_op jit(solution)/shard_map/all_to_all | solution.py:313
  20.4 0.0 copy-done
  20.4 0.0 copy-start.6
  20.5 1.3 %collective-permute-start.1 = (f32[3,2,3,128]{3,1,2,0:T(2,128)S(1)}, f32[3,2,3,128]{3,1,2,0:T(2,128)S(1)}, u32[]{:S(2)}, u32[]{:S(2)}) collective-permute-start(f32[3,2,3,128]{3,1,2,0:T(2,128)S(1)} %bitcast.93), channel_id=1, source_target_pairs={{1,0},{2,1},{3,2},{5,4},{6,5},{7,6},{9,8},{10,9},{11,10},{13,12},{... | collective-permute-start | bytes 27656 | tf_op jit(solution)/shard_map/ppermute | solution.py:21
  21.8 0.2 copy.135
  21.9 1.3 %collective-permute-start = (f32[3,2,3,16]{3,1,2,0:T(2,128)S(1)}, f32[3,2,3,16]{3,1,2,0:T(2,128)S(1)}, u32[]{:S(2)}, u32[]{:S(2)}) collective-permute-start(f32[3,2,3,16]{3,1,2,0:T(2,128)S(1)} %bitcast.88), channel_id=1, source_target_pairs={{4,0},{8,4},{12,8},{16,12},{20,16},{24,20},{28,24},{5,1},{9,5},{13... | collective-permute-start | bytes 3464 | tf_op jit(solution)/shard_map/ppermute | solution.py:21
  23.3 0.0 copy-done.5
  23.3 0.1 slice_multiply_fusion.1
  23.4 0.1 slice.140
  23.5 18.2 %collective-permute-done = f32[3,2,3,16]{3,1,2,0:T(2,128)S(1)} collective-permute-done((f32[3,2,3,16]{3,1,2,0:T(2,128)S(1)}, f32[3,2,3,16]{3,1,2,0:T(2,128)S(1)}, u32[]{:S(2)}, u32[]{:S(2)}) %collective-permute-start) | collective-permute-done | bytes 1184 | tf_op jit(solution)/shard_map/ppermute | solution.py:21
  41.7 0.1 concatenate.54
  41.8 0.1 maximum_dynamic-update-slice_fusion
  41.9 0.0 collective-permute-done.1
  42.0 0.0 copy-done.6
  42.0 3.7 %all-to-all-done = f32[7,64,4,128]{3,2,0,1:T(4,128)S(1)} async-done(((f32[7,64,4,128]{3,2,0,1:T(4,128)}), f32[7,64,4,128]{3,2,0,1:T(4,128)S(1)}, u32[]{:S(2)}, u32[]{:S(2)}) %all-to-all-start) | async-done | bytes 917536 | tf_op jit(solution)/shard_map/all_to_all | solution.py:313
  45.7 0.2 copy.140
  45.9 0.1 fusion.4
  46.0 0.1 fusion.23
  46.1 1.0 copy.143
  47.1 0.8 copy.134
  47.9 2.0 %convolution_bitcast_fusion.s_ref = f32[12,256,128]{2,1,0:T(8,128)} fusion(f32[12,96,128]{2,1,0:T(8,128)S(1)} %constant_dynamic-update-slice_fusion, s32[256]{0:T(256)S(1)} %broadcast_clamp_fusion), kind=kOutput, calls=%fused_computation | convolution fusion | flops 453009408 | bytes 2163712 | tf_op jit(solution)/shard_map/sb,rba->rsa/dot_general | solution.py:267
  50.0 28.7 %shard_map.94 = (f32[3,256,128]{2,1,0:T(8,128)}, f32[3,256,128]{2,1,0:T(8,128)}, f32[11,256,128]{2,1,0:T(8,128)}) custom-call(f32[3,256,128]{2,1,0:T(8,128)} %bitcast.71, f32[12,256,128]{2,1,0:T(8,128)} %convolution_bitcast_fusion.s_ref, f32[3,256,128]{2,1,0:T(8,128)} %bitcast.70), custom_call_target="tpu_custom_call" | custom-call | tf_op jit(solution)/shard_map/pallas_call | solution.py:203
  78.7 1.2 %pad_maximum_fusion.1 = f32[6,256,128]{2,1,0:T(8,128)S(1)} fusion(f32[3,256,128]{2,1,0:T(8,128)} %get-tuple-element.43, f32[3,256,128]{2,1,0:T(8,128)} %get-tuple-element.42), kind=kLoop, calls=%fused_computation.6 | loop fusion | flops 196608 | bytes 1572864 | tf_op jit(solution)/shard_map/concatenate | solution.py:337
  79.8 0.0 copy-start.1
  79.8 1.0 copy.144
  80.9 6.9 %all-to-all-start.1 = ((f32[6,64,4,128]{3,2,0,1:T(4,128)}), f32[6,64,4,128]{3,2,0,1:T(4,128)S(1)}, u32[]{:S(2)}, u32[]{:S(2)}) async-start(f32[6,64,4,128]{3,2,0,1:T(4,128)} %copy.144), calls=%async_computation.1 | async-start | bytes 1572864 | tf_op jit(solution)/shard_map/all_to_all | solution.py:336
  87.8 0.0 copy-done.1
  87.8 0.6 convolution_bitcast_fusion.2
  88.5 3.2 %collective-permute-start.3 = (f32[3,2,3,128]{3,1,2,0:T(2,128)S(1)}, f32[3,2,3,128]{3,1,2,0:T(2,128)S(1)}, u32[]{:S(2)}, u32[]{:S(2)}) collective-permute-start(f32[3,2,3,128]{3,1,2,0:T(2,128)S(1)} %bitcast.92), channel_id=1, source_target_pairs={{0,1},{1,2},{2,3},{4,5},{5,6},{6,7},{8,9},{9,10},{10,11},{12,13},{... | collective-permute-start | bytes 27656 | tf_op jit(solution)/shard_map/ppermute | solution.py:21
  91.7 0.1 split.56
  91.8 0.2 copy.146
  92.0 3.3 %collective-permute-start.2 = (f32[3,2,3,16]{3,1,2,0:T(2,128)S(1)}, f32[3,2,3,16]{3,1,2,0:T(2,128)S(1)}, u32[]{:S(2)}, u32[]{:S(2)}) collective-permute-start(f32[3,2,3,16]{3,1,2,0:T(2,128)S(1)} %bitcast.89), channel_id=1, source_target_pairs={{0,4},{4,8},{8,12},{12,16},{16,20},{20,24},{24,28},{1,5},{5,9},{9,... | collective-permute-start | bytes 3464 | tf_op jit(solution)/shard_map/ppermute | solution.py:21
  95.3 0.1 broadcast_multiply_fusion
  95.3 0.6 pad_add_fusion
  96.0 6.6 %collective-permute-done.2 = f32[3,2,3,16]{3,1,2,0:T(2,128)S(1)} collective-permute-done((f32[3,2,3,16]{3,1,2,0:T(2,128)S(1)}, f32[3,2,3,16]{3,1,2,0:T(2,128)S(1)}, u32[]{:S(2)}, u32[]{:S(2)}) %collective-permute-start.2) | collective-permute-done | bytes 1184 | tf_op jit(solution)/shard_map/ppermute | solution.py:21
  102.6 0.2 copy.147
  102.7 8.1 %all-to-all-done.1 = f32[6,64,4,128]{3,2,0,1:T(4,128)S(1)} async-done(((f32[6,64,4,128]{3,2,0,1:T(4,128)}), f32[6,64,4,128]{3,2,0,1:T(4,128)S(1)}, u32[]{:S(2)}, u32[]{:S(2)}) %all-to-all-start.1) | async-done | bytes 786464 | tf_op jit(solution)/shard_map/all_to_all | solution.py:336
  110.8 0.1 copy.145
  111.0 0.0 copy-start.3
  111.0 0.6 convolution_bitcast_fusion.3
  111.6 0.2 copy-done.3
  111.9 0.1 add_add_fusion
  112.0 0.0 copy-start.4
  112.0 0.2 scatter-add.11
  112.2 0.0 collective-permute-done.3
  112.2 0.1 scatter-add.14
  112.3 0.4 copy-done.4
  112.7 0.0 copy-start.2
  112.7 0.7 copy-done.2
  (25 shorter events, 0.3 us)
Async XLA Ops:
  6.2 14.2 %copy-start = (f32[3,2,3,16,128]{4,3,2,1,0:T(8,128)S(1)}, f32[3,2,3,16,128]{4,3,2,1,0:T(8,128)}, u32[]{:S(2)}) copy-start(f32[3,2,3,16,128]{4,3,2,1,0:T(8,128)} %param.13) | copy-start | bytes 442372
  7.3 16.0 %copy-start.5 = (f32[2,2,3,16,128]{4,3,2,1,0:T(8,128)S(1)}, f32[2,2,3,16,128]{4,3,2,1,0:T(8,128)}, u32[]{:S(2)}) copy-start(f32[2,2,3,16,128]{4,3,2,1,0:T(8,128)} %param.14) | copy-start | bytes 294916
  7.3 38.4 %all-to-all-start = ((f32[7,64,4,128]{3,2,0,1:T(4,128)}), f32[7,64,4,128]{3,2,0,1:T(4,128)S(1)}, u32[]{:S(2)}, u32[]{:S(2)}) async-start(f32[7,64,4,128]{3,2,0,1:T(4,128)} %copy.133), calls=%async_computation | async-start | bytes 1835008 | tf_op jit(solution)/shard_map/all_to_all | solution.py:313
  20.4 21.6 %copy-start.6 = (f32[2,3,16,128]{3,2,1,0:T(8,128)S(1)}, f32[2,3,16,128]{3,2,1,0:T(8,128)}, u32[]{:S(2)}) copy-start(f32[2,3,16,128]{3,2,1,0:T(8,128)} %param.15) | copy-start | bytes 147460
  20.5 21.5 %collective-permute-start.1 = (f32[3,2,3,128]{3,1,2,0:T(2,128)S(1)}, f32[3,2,3,128]{3,1,2,0:T(2,128)S(1)}, u32[]{:S(2)}, u32[]{:S(2)}) collective-permute-start(f32[3,2,3,128]{3,1,2,0:T(2,128)S(1)} %bitcast.93), channel_id=1, source_target_pairs={{1,0},{2,1},{3,2},{5,4},{6,5},{7,6},{9,8},{10,9},{11,10},{13,12},{... | collective-permute-start | bytes 27656 | tf_op jit(solution)/shard_map/ppermute | solution.py:21
  21.9 19.7 %collective-permute-start = (f32[3,2,3,16]{3,1,2,0:T(2,128)S(1)}, f32[3,2,3,16]{3,1,2,0:T(2,128)S(1)}, u32[]{:S(2)}, u32[]{:S(2)}) collective-permute-start(f32[3,2,3,16]{3,1,2,0:T(2,128)S(1)} %bitcast.88), channel_id=1, source_target_pairs={{4,0},{8,4},{12,8},{16,12},{20,16},{24,20},{28,24},{5,1},{9,5},{13... | collective-permute-start | bytes 3464 | tf_op jit(solution)/shard_map/ppermute | solution.py:21
  79.8 8.0 %copy-start.1 = (f32[11,256,128]{2,1,0:T(8,128)S(1)}, f32[11,256,128]{2,1,0:T(8,128)}, u32[]{:S(2)}) copy-start(f32[11,256,128]{2,1,0:T(8,128)} %get-tuple-element.44) | copy-start | bytes 4325380
  80.9 29.9 %all-to-all-start.1 = ((f32[6,64,4,128]{3,2,0,1:T(4,128)}), f32[6,64,4,128]{3,2,0,1:T(4,128)S(1)}, u32[]{:S(2)}, u32[]{:S(2)}) async-start(f32[6,64,4,128]{3,2,0,1:T(4,128)} %copy.144), calls=%async_computation.1 | async-start | bytes 1572864 | tf_op jit(solution)/shard_map/all_to_all | solution.py:336
  88.5 23.7 %collective-permute-start.3 = (f32[3,2,3,128]{3,1,2,0:T(2,128)S(1)}, f32[3,2,3,128]{3,1,2,0:T(2,128)S(1)}, u32[]{:S(2)}, u32[]{:S(2)}) collective-permute-start(f32[3,2,3,128]{3,1,2,0:T(2,128)S(1)} %bitcast.92), channel_id=1, source_target_pairs={{0,1},{1,2},{2,3},{4,5},{5,6},{6,7},{8,9},{9,10},{10,11},{12,13},{... | collective-permute-start | bytes 27656 | tf_op jit(solution)/shard_map/ppermute | solution.py:21
  92.0 10.6 %collective-permute-start.2 = (f32[3,2,3,16]{3,1,2,0:T(2,128)S(1)}, f32[3,2,3,16]{3,1,2,0:T(2,128)S(1)}, u32[]{:S(2)}, u32[]{:S(2)}) collective-permute-start(f32[3,2,3,16]{3,1,2,0:T(2,128)S(1)} %bitcast.89), channel_id=1, source_target_pairs={{0,4},{4,8},{8,12},{12,16},{16,20},{20,24},{24,28},{1,5},{5,9},{9,... | collective-permute-start | bytes 3464 | tf_op jit(solution)/shard_map/ppermute | solution.py:21
  111.0 0.9 copy-start.3
  112.0 0.7 copy-start.4
  112.7 0.7 copy-start.2

commit v13 on v12

--- a/solution.py
+++ b/solution.py
@@ -172,7 +172,7 @@
     return velocity, grad_target, grad_rows
 
 
-def pair_kernel(t_ref, s_ref, c_ref, v_ref, gt_ref, gs_ref):
+def pair_kernel(t_ref, s_ref, c_ref, v_ref, gs_ref):
     age_count = t_ref.shape[-1]
     lane = lax.broadcasted_iota(jnp.int32, (GROUP_PAIRS, age_count), 1)
 
@@ -184,7 +184,7 @@
         velocity, grad_target, grad_rows = pair_group(target, cotangent, rows, lane)
         for i in range(3):
             v_ref[i, at, :] = velocity[i]
-            gt_ref[i, at, :] = grad_target[i]
+            v_ref[3 + i, at, :] = grad_target[i]
         for i in range(11):
             gs_ref[i, at, :] = grad_rows[i]
         return carry
@@ -204,10 +204,9 @@
         pair_kernel,
         grid=(number // step,),
         in_specs=[spec(3), spec(12), spec(3)],
-        out_specs=[spec(3), spec(3), spec(11)],
+        out_specs=[spec(6), spec(11)],
         out_shape=[
-            jax.ShapeDtypeStruct((3, number, age_count), jnp.float32),
-            jax.ShapeDtypeStruct((3, number, age_count), jnp.float32),
+            jax.ShapeDtypeStruct((6, number, age_count), jnp.float32),
             jax.ShapeDtypeStruct((11, number, age_count), jnp.float32),
         ],
     )(targets, payload, cotangent)
@@ -323,7 +322,7 @@
         == jnp.arange(blocks_here, dtype=jnp.int32)[None, :]
     ).astype(jnp.float32)
     slot_payload = pick_rows(safe_pick, payload)
-    slot_velocity, slot_grad, payload_terms = run_pairs(
+    slot_answer, payload_terms = run_pairs(
         received[0:3], slot_payload, received[3:6] * time_step
     )
     payload_terms = jnp.concatenate(
@@ -334,7 +333,7 @@
     ).astype(jnp.float32)
     payload_grad = sum_rows(asked_pick, payload_terms)
     answered = lax.all_to_all(
-        jnp.concatenate([slot_velocity, slot_grad], axis=0).reshape(
+        slot_answer.reshape(
             6, group_size, capacity, age_here
         ),
         ("turb", "age"),

time: 114 us -> 114 us (level)
  local copies, waits for them, and re-layouts: 7.1 us -> 8.37 us
  other arithmetic: 4.11 us -> 2.94 us
    reshape x1, local copies, waits for them, and re-layouts: 1.04 us -> 2.28 us  [local(): slot_answer.reshape(6, group_size, capacity, age_here)]
    concatenate x1 -> x0, other arithmetic: 1.17 us -> none  [local(): jnp.concatenate([slot_velocity, slot_grad], axis=0)]
where the time goes in v13:
time: 114 us; the launch traced here: 113 us
  waiting for transfers between devices  36.5 us (32%)
  starting transfers between devices  29.1 us (26%)
  Pallas kernels  28.7 us (25%)
  local copies, waits for them, and re-layouts  8.37 us (7%)
  matrix products  6.82 us (6%)
  other arithmetic  2.94 us (3%)
    pallas_call x1, Pallas kernels, run_pairs(): pl.pallas_call(pair_kernel, grid=(number // step,), in_specs=[spec(3), sp...  28.7 us
    ppermute x4, waiting for transfers between devices, shifted_2(): lax.ppermute(value, axis, [(source, source + steps) for source in range(l...  24.7 us
    all_to_all x1, starting transfers between devices, local(): lax.all_to_all(outgoing.reshape(7, group_size, capacity, age_here), ('tur...  13.1 us
    ppermute x4, starting transfers between devices, shifted_2(): lax.ppermute(value, axis, [(source, source + steps) for source in range(l...  9.06 us
    all_to_all x1, waiting for transfers between devices, local(): lax.all_to_all(slot_answer.reshape(6, group_size, capacity, age_here), ('...  8.08 us
    all_to_all x1, starting transfers between devices, local(): lax.all_to_all(slot_answer.reshape(6, group_size, capacity, age_here), ('...  6.9 us
    dot_general x2, matrix products, pick_rows(): jnp.einsum('sb,rba->rsa', selector, values, precision=lax.Precision.HIGHE...  3.81 us
    all_to_all x1, waiting for transfers between devices, local(): lax.all_to_all(outgoing.reshape(7, group_size, capacity, age_here), ('tur...  3.68 us
  transfers between devices with their start and end apart: 6, of which 4 were waited for; matrix products, arithmetic and copies ran while one was open for 3% of the time, Pallas kernels for 0%

profile of v13, /device:TPU:1, one launch (start us, length us, event | category | flops | bytes accessed | tf_op | source)
XLA Modules:
  0.0 113.4 jit_solution(3331872911270911535)
XLA Ops:
  0.6 0.9 convert_reduce_fusion
  1.5 0.7 multiply_add_fusion
  2.2 0.8 fusion.5
  3.0 1.0 convolution_bitcast_fusion.4
  4.0 1.8 %convolution_bitcast_fusion.1 = f32[6,256,128]{1,2,0:T(8,128)S(1)} fusion(f32[256,96,1]{0,1,2:T(8,128)S(1)} %convolution_bitcast_fusion.4, f32[3,96,128]{2,1,0:T(8,128)} %bitcast.77, f32[3,96,128]{2,1,0:T(8,128)} %bitcast.64), kind=kOutput, calls=%fused_computation.1 | convolution fusion | flops 226566144 | bytes 1179648 | tf_op jit(solution)/shard_map/sb,rba->rsa/dot_general | solution.py:266
  5.8 0.1 pad_maximum_fusion
  5.9 0.3 copy.132
  6.2 0.0 copy-start
  6.2 1.1 copy.133
  7.3 0.0 copy-start.5
  7.3 13.1 %all-to-all-start = ((f32[7,64,4,128]{3,2,0,1:T(4,128)}), f32[7,64,4,128]{3,2,0,1:T(4,128)S(1)}, u32[]{:S(2)}, u32[]{:S(2)}) async-start(f32[7,64,4,128]{3,2,0,1:T(4,128)} %copy.133), calls=%async_computation | async-start | bytes 1835008 | tf_op jit(solution)/shard_map/all_to_all | solution.py:312
  20.4 0.0 copy-done
  20.4 0.0 copy-start.6
  20.5 1.3 %collective-permute-start.1 = (f32[3,2,3,128]{3,1,2,0:T(2,128)S(1)}, f32[3,2,3,128]{3,1,2,0:T(2,128)S(1)}, u32[]{:S(2)}, u32[]{:S(2)}) collective-permute-start(f32[3,2,3,128]{3,1,2,0:T(2,128)S(1)} %bitcast.93), channel_id=1, source_target_pairs={{1,0},{2,1},{3,2},{5,4},{6,5},{7,6},{9,8},{10,9},{11,10},{13,12},{... | collective-permute-start | bytes 27656 | tf_op jit(solution)/shard_map/ppermute | solution.py:21
  21.8 0.2 copy.135
  21.9 1.3 %collective-permute-start = (f32[3,2,3,16]{3,1,2,0:T(2,128)S(1)}, f32[3,2,3,16]{3,1,2,0:T(2,128)S(1)}, u32[]{:S(2)}, u32[]{:S(2)}) collective-permute-start(f32[3,2,3,16]{3,1,2,0:T(2,128)S(1)} %bitcast.88), channel_id=1, source_target_pairs={{4,0},{8,4},{12,8},{16,12},{20,16},{24,20},{28,24},{5,1},{9,5},{13... | collective-permute-start | bytes 3464 | tf_op jit(solution)/shard_map/ppermute | solution.py:21
  23.3 0.0 copy-done.5
  23.3 0.1 slice_multiply_fusion.1
  23.4 0.1 slice.140
  23.5 18.2 %collective-permute-done = f32[3,2,3,16]{3,1,2,0:T(2,128)S(1)} collective-permute-done((f32[3,2,3,16]{3,1,2,0:T(2,128)S(1)}, f32[3,2,3,16]{3,1,2,0:T(2,128)S(1)}, u32[]{:S(2)}, u32[]{:S(2)}) %collective-permute-start) | collective-permute-done | bytes 1184 | tf_op jit(solution)/shard_map/ppermute | solution.py:21
  41.7 0.1 concatenate.50
  41.8 0.1 maximum_dynamic-update-slice_fusion
  41.9 0.0 collective-permute-done.1
  42.0 0.0 copy-done.6
  42.0 3.7 %all-to-all-done = f32[7,64,4,128]{3,2,0,1:T(4,128)S(1)} async-done(((f32[7,64,4,128]{3,2,0,1:T(4,128)}), f32[7,64,4,128]{3,2,0,1:T(4,128)S(1)}, u32[]{:S(2)}, u32[]{:S(2)}) %all-to-all-start) | async-done | bytes 917536 | tf_op jit(solution)/shard_map/all_to_all | solution.py:312
  45.7 0.2 copy.140
  45.9 0.1 fusion.4
  46.0 0.1 fusion.23
  46.1 1.0 copy.143
  47.2 0.8 copy.134
  48.0 2.0 %convolution_bitcast_fusion.s_ref = f32[12,256,128]{2,1,0:T(8,128)} fusion(f32[12,96,128]{2,1,0:T(8,128)S(1)} %constant_dynamic-update-slice_fusion, s32[256]{0:T(256)S(1)} %broadcast_clamp_fusion), kind=kOutput, calls=%fused_computation | convolution fusion | flops 453009408 | bytes 2163712 | tf_op jit(solution)/shard_map/sb,rba->rsa/dot_general | solution.py:266
  50.0 28.7 %shard_map.94 = (f32[6,256,128]{2,1,0:T(8,128)}, f32[11,256,128]{2,1,0:T(8,128)}) custom-call(f32[3,256,128]{2,1,0:T(8,128)} %bitcast.70, f32[12,256,128]{2,1,0:T(8,128)} %convolution_bitcast_fusion.s_ref, f32[3,256,128]{2,1,0:T(8,128)} %bitcast.69), custom_call_target="tpu_custom_call" | custom-call | tf_op jit(solution)/shard_map/pallas_call | solution.py:203
  78.7 0.0 copy-start.1
  78.7 2.3 %copy.144 = f32[6,64,4,128]{3,2,0,1:T(4,128)} copy(f32[6,64,4,128]{3,2,1,0:T(4,128)} %bitcast.74) | data formatting | bytes 1572864 | tf_op jit(solution)/shard_map/reshape | solution.py:336
  80.9 6.9 %all-to-all-start.1 = ((f32[6,64,4,128]{3,2,0,1:T(4,128)}), f32[6,64,4,128]{3,2,0,1:T(4,128)S(1)}, u32[]{:S(2)}, u32[]{:S(2)}) async-start(f32[6,64,4,128]{3,2,0,1:T(4,128)} %copy.144), calls=%async_computation.1 | async-start | bytes 1572864 | tf_op jit(solution)/shard_map/all_to_all | solution.py:335
  87.8 0.0 copy-done.1
  87.9 0.6 convolution_bitcast_fusion.2
  88.6 3.2 %collective-permute-start.3 = (f32[3,2,3,128]{3,1,2,0:T(2,128)S(1)}, f32[3,2,3,128]{3,1,2,0:T(2,128)S(1)}, u32[]{:S(2)}, u32[]{:S(2)}) collective-permute-start(f32[3,2,3,128]{3,1,2,0:T(2,128)S(1)} %bitcast.92), channel_id=1, source_target_pairs={{0,1},{1,2},{2,3},{4,5},{5,6},{6,7},{8,9},{9,10},{10,11},{12,13},{... | collective-permute-start | bytes 27656 | tf_op jit(solution)/shard_map/ppermute | solution.py:21
  91.8 0.1 split.56
  91.9 0.2 copy.146
  92.0 3.3 %collective-permute-start.2 = (f32[3,2,3,16]{3,1,2,0:T(2,128)S(1)}, f32[3,2,3,16]{3,1,2,0:T(2,128)S(1)}, u32[]{:S(2)}, u32[]{:S(2)}) collective-permute-start(f32[3,2,3,16]{3,1,2,0:T(2,128)S(1)} %bitcast.89), channel_id=1, source_target_pairs={{0,4},{4,8},{8,12},{12,16},{16,20},{20,24},{24,28},{1,5},{5,9},{9,... | collective-permute-start | bytes 3464 | tf_op jit(solution)/shard_map/ppermute | solution.py:21
  95.3 0.1 broadcast_multiply_fusion
  95.4 0.6 pad_add_fusion
  96.1 6.6 %collective-permute-done.2 = f32[3,2,3,16]{3,1,2,0:T(2,128)S(1)} collective-permute-done((f32[3,2,3,16]{3,1,2,0:T(2,128)S(1)}, f32[3,2,3,16]{3,1,2,0:T(2,128)S(1)}, u32[]{:S(2)}, u32[]{:S(2)}) %collective-permute-start.2) | collective-permute-done | bytes 1184 | tf_op jit(solution)/shard_map/ppermute | solution.py:21
  102.6 0.2 copy.147
  102.8 8.1 %all-to-all-done.1 = f32[6,64,4,128]{3,2,0,1:T(4,128)S(1)} async-done(((f32[6,64,4,128]{3,2,0,1:T(4,128)}), f32[6,64,4,128]{3,2,0,1:T(4,128)S(1)}, u32[]{:S(2)}, u32[]{:S(2)}) %all-to-all-start.1) | async-done | bytes 786464 | tf_op jit(solution)/shard_map/all_to_all | solution.py:335
  110.9 0.1 copy.145
  111.0 0.0 copy-start.3
  111.0 0.6 convolution_bitcast_fusion.3
  111.7 0.2 copy-done.3
  111.9 0.1 add_add_fusion
  112.1 0.0 copy-start.4
  112.1 0.2 scatter-add.11
  112.3 0.0 collective-permute-done.3
  112.3 0.1 scatter-add.14
  112.4 0.4 copy-done.4
  112.8 0.0 copy-start.2
  112.8 0.7 copy-done.2
  (25 shorter events, 0.3 us)
Async XLA Ops:
  6.2 14.2 %copy-start = (f32[3,2,3,16,128]{4,3,2,1,0:T(8,128)S(1)}, f32[3,2,3,16,128]{4,3,2,1,0:T(8,128)}, u32[]{:S(2)}) copy-start(f32[3,2,3,16,128]{4,3,2,1,0:T(8,128)} %param.13) | copy-start | bytes 442372
  7.3 16.0 %copy-start.5 = (f32[2,2,3,16,128]{4,3,2,1,0:T(8,128)S(1)}, f32[2,2,3,16,128]{4,3,2,1,0:T(8,128)}, u32[]{:S(2)}) copy-start(f32[2,2,3,16,128]{4,3,2,1,0:T(8,128)} %param.14) | copy-start | bytes 294916
  7.3 38.4 %all-to-all-start = ((f32[7,64,4,128]{3,2,0,1:T(4,128)}), f32[7,64,4,128]{3,2,0,1:T(4,128)S(1)}, u32[]{:S(2)}, u32[]{:S(2)}) async-start(f32[7,64,4,128]{3,2,0,1:T(4,128)} %copy.133), calls=%async_computation | async-start | bytes 1835008 | tf_op jit(solution)/shard_map/all_to_all | solution.py:312
  20.4 21.6 %copy-start.6 = (f32[2,3,16,128]{3,2,1,0:T(8,128)S(1)}, f32[2,3,16,128]{3,2,1,0:T(8,128)}, u32[]{:S(2)}) copy-start(f32[2,3,16,128]{3,2,1,0:T(8,128)} %param.15) | copy-start | bytes 147460
  20.5 21.5 %collective-permute-start.1 = (f32[3,2,3,128]{3,1,2,0:T(2,128)S(1)}, f32[3,2,3,128]{3,1,2,0:T(2,128)S(1)}, u32[]{:S(2)}, u32[]{:S(2)}) collective-permute-start(f32[3,2,3,128]{3,1,2,0:T(2,128)S(1)} %bitcast.93), channel_id=1, source_target_pairs={{1,0},{2,1},{3,2},{5,4},{6,5},{7,6},{9,8},{10,9},{11,10},{13,12},{... | collective-permute-start | bytes 27656 | tf_op jit(solution)/shard_map/ppermute | solution.py:21
  21.9 19.7 %collective-permute-start = (f32[3,2,3,16]{3,1,2,0:T(2,128)S(1)}, f32[3,2,3,16]{3,1,2,0:T(2,128)S(1)}, u32[]{:S(2)}, u32[]{:S(2)}) collective-permute-start(f32[3,2,3,16]{3,1,2,0:T(2,128)S(1)} %bitcast.88), channel_id=1, source_target_pairs={{4,0},{8,4},{12,8},{16,12},{20,16},{24,20},{28,24},{5,1},{9,5},{13... | collective-permute-start | bytes 3464 | tf_op jit(solution)/shard_map/ppermute | solution.py:21
  78.7 9.2 %copy-start.1 = (f32[11,256,128]{2,1,0:T(8,128)S(1)}, f32[11,256,128]{2,1,0:T(8,128)}, u32[]{:S(2)}) copy-start(f32[11,256,128]{2,1,0:T(8,128)} %get-tuple-element.42) | copy-start | bytes 4325380
  80.9 29.9 %all-to-all-start.1 = ((f32[6,64,4,128]{3,2,0,1:T(4,128)}), f32[6,64,4,128]{3,2,0,1:T(4,128)S(1)}, u32[]{:S(2)}, u32[]{:S(2)}) async-start(f32[6,64,4,128]{3,2,0,1:T(4,128)} %copy.144), calls=%async_computation.1 | async-start | bytes 1572864 | tf_op jit(solution)/shard_map/all_to_all | solution.py:335
  88.6 23.7 %collective-permute-start.3 = (f32[3,2,3,128]{3,1,2,0:T(2,128)S(1)}, f32[3,2,3,128]{3,1,2,0:T(2,128)S(1)}, u32[]{:S(2)}, u32[]{:S(2)}) collective-permute-start(f32[3,2,3,128]{3,1,2,0:T(2,128)S(1)} %bitcast.92), channel_id=1, source_target_pairs={{0,1},{1,2},{2,3},{4,5},{5,6},{6,7},{8,9},{9,10},{10,11},{12,13},{... | collective-permute-start | bytes 27656 | tf_op jit(solution)/shard_map/ppermute | solution.py:21
  92.0 10.6 %collective-permute-start.2 = (f32[3,2,3,16]{3,1,2,0:T(2,128)S(1)}, f32[3,2,3,16]{3,1,2,0:T(2,128)S(1)}, u32[]{:S(2)}, u32[]{:S(2)}) collective-permute-start(f32[3,2,3,16]{3,1,2,0:T(2,128)S(1)} %bitcast.89), channel_id=1, source_target_pairs={{0,4},{4,8},{8,12},{12,16},{16,20},{20,24},{24,28},{1,5},{5,9},{9,... | collective-permute-start | bytes 3464 | tf_op jit(solution)/shard_map/ppermute | solution.py:21
  111.0 0.9 copy-start.3
  112.1 0.7 copy-start.4
  112.8 0.7 copy-start.2

commit v14 on v12

--- a/solution.py
+++ b/solution.py
@@ -179,7 +179,7 @@
     def body(group, carry):
         at = pl.ds(pl.multiple_of(group * GROUP_PAIRS, GROUP_PAIRS), GROUP_PAIRS)
         target = [t_ref[i, at, :] for i in range(3)]
-        cotangent = [c_ref[i, at, :] for i in range(3)]
+        cotangent = [c_ref[i, at, :] * time_step for i in range(3)]
         rows = [s_ref[i, at, :] for i in range(12)]
         velocity, grad_target, grad_rows = pair_group(target, cotangent, rows, lane)
         for i in range(3):
@@ -203,7 +203,11 @@
     return pl.pallas_call(
         pair_kernel,
         grid=(number // step,),
-        in_specs=[spec(3), spec(12), spec(3)],
+        in_specs=[
+            spec(3),
+            spec(12),
+            pl.BlockSpec((3, step, age_count), lambda i: (1, i, 0)),
+        ],
         out_specs=[spec(3), spec(3), spec(11)],
         out_shape=[
             jax.ShapeDtypeStruct((3, number, age_count), jnp.float32),
@@ -324,7 +328,7 @@
     ).astype(jnp.float32)
     slot_payload = pick_rows(safe_pick, payload)
     slot_velocity, slot_grad, payload_terms = run_pairs(
-        received[0:3], slot_payload, received[3:6] * time_step
+        received, slot_payload, received
     )
     payload_terms = jnp.concatenate(
         [payload_terms, jnp.zeros_like(payload_terms[:1])], axis=0

time: 114 us -> 112 us (0.982)
  local copies, waits for them, and re-layouts: 7.1 us -> 5.22 us
where the time goes in v14:
time: 112 us
  waiting for transfers between devices  36.5 us (33%)
  starting transfers between devices  29.1 us (26%)
  Pallas kernels  28.8 us (26%)
  matrix products  6.82 us (6%)
  local copies, waits for them, and re-layouts  5.22 us (5%)
  other arithmetic  4.07 us (4%)
    pallas_call x1, Pallas kernels, run_pairs(): pl.pallas_call(pair_kernel, grid=(number // step,), in_specs=[spec(3), sp...  28.8 us
    ppermute x4, waiting for transfers between devices, shifted_2(): lax.ppermute(value, axis, [(source, source + steps) for source in range(l...  24.7 us
    all_to_all x1, starting transfers between devices, local(): lax.all_to_all(outgoing.reshape(7, group_size, capacity, age_here), ('tur...  13.1 us
    ppermute x4, starting transfers between devices, shifted_2(): lax.ppermute(value, axis, [(source, source + steps) for source in range(l...  9.06 us
    all_to_all x1, waiting for transfers between devices, local(): lax.all_to_all(jnp.concatenate([slot_velocity, slot_grad], axis=0).reshap...  8.08 us
    all_to_all x1, starting transfers between devices, local(): lax.all_to_all(jnp.concatenate([slot_velocity, slot_grad], axis=0).reshap...  6.89 us
    dot_general x2, matrix products, pick_rows(): jnp.einsum('sb,rba->rsa', selector, values, precision=lax.Precision.HIGHE...  3.81 us
    all_to_all x1, waiting for transfers between devices, local(): lax.all_to_all(outgoing.reshape(7, group_size, capacity, age_here), ('tur...  3.68 us
  transfers between devices with their start and end apart: 6, of which 4 were waited for; matrix products, arithmetic and copies ran while one was open for 3% of the time, Pallas kernels for 0%

profile of v14, /device:TPU:1, one launch (start us, length us, event | category | flops | bytes accessed | tf_op | source)
XLA Modules:
  0.0 111.5 jit_solution(1672069230850974803)
XLA Ops:
  0.6 0.9 convert_reduce_fusion
  1.5 0.7 multiply_add_fusion
  2.2 0.8 fusion.5
  3.0 1.0 convolution_bitcast_fusion.4
  4.0 1.8 %convolution_bitcast_fusion.1 = f32[6,256,128]{1,2,0:T(8,128)S(1)} fusion(f32[256,96,1]{0,1,2:T(8,128)S(1)} %convolution_bitcast_fusion.4, f32[3,96,128]{2,1,0:T(8,128)} %bitcast.75, f32[3,96,128]{2,1,0:T(8,128)} %bitcast.65), kind=kOutput, calls=%fused_computation.1 | convolution fusion | flops 226566144 | bytes 1179648 | tf_op jit(solution)/shard_map/sb,rba->rsa/dot_general | solution.py:271
  5.8 0.1 pad_maximum_fusion
  5.9 0.3 copy.102
  6.2 0.0 copy-start.1
  6.2 1.1 copy.103
  7.3 0.0 copy-start.6
  7.3 13.1 %all-to-all-start = ((f32[7,64,4,128]{3,2,0,1:T(4,128)}), f32[7,64,4,128]{3,2,0,1:T(4,128)S(1)}, u32[]{:S(2)}, u32[]{:S(2)}) async-start(f32[7,64,4,128]{3,2,0,1:T(4,128)} %copy.103), calls=%async_computation | async-start | bytes 1835008 | tf_op jit(solution)/shard_map/all_to_all | solution.py:317
  20.4 0.0 copy-done.1
  20.4 0.0 copy-start.7
  20.5 1.3 %collective-permute-start.1 = (f32[3,2,3,128]{3,1,2,0:T(2,128)S(1)}, f32[3,2,3,128]{3,1,2,0:T(2,128)S(1)}, u32[]{:S(2)}, u32[]{:S(2)}) collective-permute-start(f32[3,2,3,128]{3,1,2,0:T(2,128)S(1)} %bitcast.91), channel_id=1, source_target_pairs={{1,0},{2,1},{3,2},{5,4},{6,5},{7,6},{9,8},{10,9},{11,10},{13,12},{... | collective-permute-start | bytes 27656 | tf_op jit(solution)/shard_map/ppermute | solution.py:21
  21.8 0.2 copy.105
  21.9 1.3 %collective-permute-start = (f32[3,2,3,16]{3,1,2,0:T(2,128)S(1)}, f32[3,2,3,16]{3,1,2,0:T(2,128)S(1)}, u32[]{:S(2)}, u32[]{:S(2)}) collective-permute-start(f32[3,2,3,16]{3,1,2,0:T(2,128)S(1)} %bitcast.86), channel_id=1, source_target_pairs={{4,0},{8,4},{12,8},{16,12},{20,16},{24,20},{28,24},{5,1},{9,5},{13... | collective-permute-start | bytes 3464 | tf_op jit(solution)/shard_map/ppermute | solution.py:21
  23.3 0.0 copy-done.6
  23.3 0.1 slice_multiply_fusion.1
  23.4 0.1 slice.128
  23.5 18.2 %collective-permute-done = f32[3,2,3,16]{3,1,2,0:T(2,128)S(1)} collective-permute-done((f32[3,2,3,16]{3,1,2,0:T(2,128)S(1)}, f32[3,2,3,16]{3,1,2,0:T(2,128)S(1)}, u32[]{:S(2)}, u32[]{:S(2)}) %collective-permute-start) | collective-permute-done | bytes 1184 | tf_op jit(solution)/shard_map/ppermute | solution.py:21
  41.7 0.1 concatenate.54
  41.8 0.1 maximum_dynamic-update-slice_fusion
  41.9 0.0 collective-permute-done.1
  42.0 0.0 copy-done.7
  42.0 3.7 %all-to-all-done = f32[7,64,4,128]{3,2,0,1:T(4,128)S(1)} async-done(((f32[7,64,4,128]{3,2,0,1:T(4,128)}), f32[7,64,4,128]{3,2,0,1:T(4,128)S(1)}, u32[]{:S(2)}, u32[]{:S(2)}) %all-to-all-start) | async-done | bytes 917536 | tf_op jit(solution)/shard_map/all_to_all | solution.py:317
  45.7 0.2 copy.104
  45.9 0.0 copy-start
  45.9 0.1 fusion.4
  46.0 2.0 %convolution_bitcast_fusion.s_ref = f32[12,256,128]{2,1,0:T(8,128)} fusion(f32[12,96,128]{2,1,0:T(8,128)S(1)} %constant_dynamic-update-slice_fusion, s32[256]{0:T(256)S(1)} %broadcast_clamp_fusion), kind=kOutput, calls=%fused_computation | convolution fusion | flops 453009408 | bytes 2163712 | tf_op jit(solution)/shard_map/sb,rba->rsa/dot_general | solution.py:271
  48.0 0.0 copy-done
  48.0 28.8 %shard_map.94 = (f32[3,256,128]{2,1,0:T(8,128)}, f32[3,256,128]{2,1,0:T(8,128)}, f32[11,256,128]{2,1,0:T(8,128)}) custom-call(f32[7,256,128]{2,1,0:T(8,128)} %bitcast.63, f32[12,256,128]{2,1,0:T(8,128)} %convolution_bitcast_fusion.s_ref, f32[7,256,128]{2,1,0:T(8,128)} %bitcast.64), custom_call_target="tpu_custom_call" | custom-call | tf_op jit(solution)/shard_map/pallas_call | solution.py:203
  76.9 1.2 %pad_maximum_fusion.1 = f32[6,256,128]{2,1,0:T(8,128)S(1)} fusion(f32[3,256,128]{2,1,0:T(8,128)} %get-tuple-element.43, f32[3,256,128]{2,1,0:T(8,128)} %get-tuple-element.42), kind=kLoop, calls=%fused_computation.6 | loop fusion | flops 196608 | bytes 1572864 | tf_op jit(solution)/shard_map/concatenate | solution.py:341
  78.0 0.0 copy-start.2
  78.0 1.0 copy.111
  79.1 6.9 %all-to-all-start.1 = ((f32[6,64,4,128]{3,2,0,1:T(4,128)}), f32[6,64,4,128]{3,2,0,1:T(4,128)S(1)}, u32[]{:S(2)}, u32[]{:S(2)}) async-start(f32[6,64,4,128]{3,2,0,1:T(4,128)} %copy.111), calls=%async_computation.1 | async-start | bytes 1572864 | tf_op jit(solution)/shard_map/all_to_all | solution.py:340
  86.0 0.0 copy-done.2
  86.0 0.6 convolution_bitcast_fusion.2
  86.7 3.2 %collective-permute-start.3 = (f32[3,2,3,128]{3,1,2,0:T(2,128)S(1)}, f32[3,2,3,128]{3,1,2,0:T(2,128)S(1)}, u32[]{:S(2)}, u32[]{:S(2)}) collective-permute-start(f32[3,2,3,128]{3,1,2,0:T(2,128)S(1)} %bitcast.90), channel_id=1, source_target_pairs={{0,1},{1,2},{2,3},{4,5},{5,6},{6,7},{8,9},{9,10},{10,11},{12,13},{... | collective-permute-start | bytes 27656 | tf_op jit(solution)/shard_map/ppermute | solution.py:21
  89.9 0.1 split.56
  90.0 0.2 copy.113
  90.2 3.3 %collective-permute-start.2 = (f32[3,2,3,16]{3,1,2,0:T(2,128)S(1)}, f32[3,2,3,16]{3,1,2,0:T(2,128)S(1)}, u32[]{:S(2)}, u32[]{:S(2)}) collective-permute-start(f32[3,2,3,16]{3,1,2,0:T(2,128)S(1)} %bitcast.87), channel_id=1, source_target_pairs={{0,4},{4,8},{8,12},{12,16},{16,20},{20,24},{24,28},{1,5},{5,9},{9,... | collective-permute-start | bytes 3464 | tf_op jit(solution)/shard_map/ppermute | solution.py:21
  93.5 0.1 broadcast_multiply_fusion
  93.5 0.6 pad_add_fusion
  94.2 6.6 %collective-permute-done.2 = f32[3,2,3,16]{3,1,2,0:T(2,128)S(1)} collective-permute-done((f32[3,2,3,16]{3,1,2,0:T(2,128)S(1)}, f32[3,2,3,16]{3,1,2,0:T(2,128)S(1)}, u32[]{:S(2)}, u32[]{:S(2)}) %collective-permute-start.2) | collective-permute-done | bytes 1184 | tf_op jit(solution)/shard_map/ppermute | solution.py:21
  100.8 0.2 copy.114
  100.9 8.1 %all-to-all-done.1 = f32[6,64,4,128]{3,2,0,1:T(4,128)S(1)} async-done(((f32[6,64,4,128]{3,2,0,1:T(4,128)}), f32[6,64,4,128]{3,2,0,1:T(4,128)S(1)}, u32[]{:S(2)}, u32[]{:S(2)}) %all-to-all-start.1) | async-done | bytes 786464 | tf_op jit(solution)/shard_map/all_to_all | solution.py:340
  109.0 0.1 copy.112
  109.2 0.0 copy-start.4
  109.2 0.6 convolution_bitcast_fusion.3
  109.8 0.2 copy-done.4
  110.1 0.1 add_add_fusion
  110.2 0.0 copy-start.5
  110.2 0.2 scatter-add.11
  110.4 0.0 collective-permute-done.3
  110.4 0.1 scatter-add.14
  110.5 0.4 copy-done.5
  110.9 0.0 copy-start.3
  110.9 0.7 copy-done.3
  (24 shorter events, 0.3 us)
Async XLA Ops:
  6.2 14.2 %copy-start.1 = (f32[3,2,3,16,128]{4,3,2,1,0:T(8,128)S(1)}, f32[3,2,3,16,128]{4,3,2,1,0:T(8,128)}, u32[]{:S(2)}) copy-start(f32[3,2,3,16,128]{4,3,2,1,0:T(8,128)} %param.13) | copy-start | bytes 442372
  7.3 16.0 %copy-start.6 = (f32[2,2,3,16,128]{4,3,2,1,0:T(8,128)S(1)}, f32[2,2,3,16,128]{4,3,2,1,0:T(8,128)}, u32[]{:S(2)}) copy-start(f32[2,2,3,16,128]{4,3,2,1,0:T(8,128)} %param.14) | copy-start | bytes 294916
  7.3 38.4 %all-to-all-start = ((f32[7,64,4,128]{3,2,0,1:T(4,128)}), f32[7,64,4,128]{3,2,0,1:T(4,128)S(1)}, u32[]{:S(2)}, u32[]{:S(2)}) async-start(f32[7,64,4,128]{3,2,0,1:T(4,128)} %copy.103), calls=%async_computation | async-start | bytes 1835008 | tf_op jit(solution)/shard_map/all_to_all | solution.py:317
  20.4 21.6 %copy-start.7 = (f32[2,3,16,128]{3,2,1,0:T(8,128)S(1)}, f32[2,3,16,128]{3,2,1,0:T(8,128)}, u32[]{:S(2)}) copy-start(f32[2,3,16,128]{3,2,1,0:T(8,128)} %param.15) | copy-start | bytes 147460
  20.5 21.5 %collective-permute-start.1 = (f32[3,2,3,128]{3,1,2,0:T(2,128)S(1)}, f32[3,2,3,128]{3,1,2,0:T(2,128)S(1)}, u32[]{:S(2)}, u32[]{:S(2)}) collective-permute-start(f32[3,2,3,128]{3,1,2,0:T(2,128)S(1)} %bitcast.91), channel_id=1, source_target_pairs={{1,0},{2,1},{3,2},{5,4},{6,5},{7,6},{9,8},{10,9},{11,10},{13,12},{... | collective-permute-start | bytes 27656 | tf_op jit(solution)/shard_map/ppermute | solution.py:21
  21.9 19.7 %collective-permute-start = (f32[3,2,3,16]{3,1,2,0:T(2,128)S(1)}, f32[3,2,3,16]{3,1,2,0:T(2,128)S(1)}, u32[]{:S(2)}, u32[]{:S(2)}) collective-permute-start(f32[3,2,3,16]{3,1,2,0:T(2,128)S(1)} %bitcast.86), channel_id=1, source_target_pairs={{4,0},{8,4},{12,8},{16,12},{20,16},{24,20},{28,24},{5,1},{9,5},{13... | collective-permute-start | bytes 3464 | tf_op jit(solution)/shard_map/ppermute | solution.py:21
  45.9 2.2 %copy-start = (f32[7,64,4,128]{3,2,1,0:T(4,128)}, f32[7,64,4,128]{3,2,1,0:T(4,128)S(1)}, u32[]{:S(2)}) copy-start(f32[7,64,4,128]{3,2,1,0:T(4,128)S(1)} %copy.104) | copy-start | bytes 2752516
  78.0 8.0 %copy-start.2 = (f32[11,256,128]{2,1,0:T(8,128)S(1)}, f32[11,256,128]{2,1,0:T(8,128)}, u32[]{:S(2)}) copy-start(f32[11,256,128]{2,1,0:T(8,128)} %get-tuple-element.44) | copy-start | bytes 4325380
  79.1 29.9 %all-to-all-start.1 = ((f32[6,64,4,128]{3,2,0,1:T(4,128)}), f32[6,64,4,128]{3,2,0,1:T(4,128)S(1)}, u32[]{:S(2)}, u32[]{:S(2)}) async-start(f32[6,64,4,128]{3,2,0,1:T(4,128)} %copy.111), calls=%async_computation.1 | async-start | bytes 1572864 | tf_op jit(solution)/shard_map/all_to_all | solution.py:340
  86.7 23.7 %collective-permute-start.3 = (f32[3,2,3,128]{3,1,2,0:T(2,128)S(1)}, f32[3,2,3,128]{3,1,2,0:T(2,128)S(1)}, u32[]{:S(2)}, u32[]{:S(2)}) collective-permute-start(f32[3,2,3,128]{3,1,2,0:T(2,128)S(1)} %bitcast.90), channel_id=1, source_target_pairs={{0,1},{1,2},{2,3},{4,5},{5,6},{6,7},{8,9},{9,10},{10,11},{12,13},{... | collective-permute-start | bytes 27656 | tf_op jit(solution)/shard_map/ppermute | solution.py:21
  90.2 10.6 %collective-permute-start.2 = (f32[3,2,3,16]{3,1,2,0:T(2,128)S(1)}, f32[3,2,3,16]{3,1,2,0:T(2,128)S(1)}, u32[]{:S(2)}, u32[]{:S(2)}) collective-permute-start(f32[3,2,3,16]{3,1,2,0:T(2,128)S(1)} %bitcast.87), channel_id=1, source_target_pairs={{0,4},{4,8},{8,12},{12,16},{16,20},{20,24},{24,28},{1,5},{5,9},{9,... | collective-permute-start | bytes 3464 | tf_op jit(solution)/shard_map/ppermute | solution.py:21
  109.2 0.9 copy-start.4
  110.2 0.7 copy-start.5
  110.9 0.7 copy-start.3

commit v15 on v14

--- a/solution.py
+++ b/solution.py
@@ -77,7 +77,7 @@
 
 
 GROUP_PAIRS = 8
-BLOCK_PAIRS = 64
+BLOCK_PAIRS = 128
 
 
 def dot3(a, b):

time: 112 us -> 112 us (level)
  no operation moved by 1% of the time
where the time goes in v15:
time: 112 us
  waiting for transfers between devices  36.5 us (33%)
  starting transfers between devices  29.1 us (26%)
  Pallas kernels  29.1 us (26%)
  matrix products  6.82 us (6%)
  local copies, waits for them, and re-layouts  5.21 us (5%)
  other arithmetic  4.07 us (4%)
    pallas_call x1, Pallas kernels, run_pairs(): pl.pallas_call(pair_kernel, grid=(number // step,), in_specs=[spec(3), sp...  29.1 us
    ppermute x4, waiting for transfers between devices, shifted_2(): lax.ppermute(value, axis, [(source, source + steps) for source in range(l...  24.7 us
    all_to_all x1, starting transfers between devices, local(): lax.all_to_all(outgoing.reshape(7, group_size, capacity, age_here), ('tur...  13.1 us
    ppermute x4, starting transfers between devices, shifted_2(): lax.ppermute(value, axis, [(source, source + steps) for source in range(l...  9.06 us
    all_to_all x1, waiting for transfers between devices, local(): lax.all_to_all(jnp.concatenate([slot_velocity, slot_grad], axis=0).reshap...  8.08 us
    all_to_all x1, starting transfers between devices, local(): lax.all_to_all(jnp.concatenate([slot_velocity, slot_grad], axis=0).reshap...  6.89 us
    dot_general x2, matrix products, pick_rows(): jnp.einsum('sb,rba->rsa', selector, values, precision=lax.Precision.HIGHE...  3.81 us
    all_to_all x1, waiting for transfers between devices, local(): lax.all_to_all(outgoing.reshape(7, group_size, capacity, age_here), ('tur...  3.68 us
  transfers between devices with their start and end apart: 6, of which 4 were waited for; matrix products, arithmetic and copies ran while one was open for 3% of the time, Pallas kernels for 0%

profile of v15, /device:TPU:1, one launch (start us, length us, event | category | flops | bytes accessed | tf_op | source)
XLA Modules:
  0.0 111.8 jit_solution(18177797831535378240)
XLA Ops:
  0.6 0.9 convert_reduce_fusion
  1.5 0.7 multiply_add_fusion
  2.2 0.8 fusion.5
  3.0 1.0 convolution_bitcast_fusion.4
  4.0 1.8 %convolution_bitcast_fusion.1 = f32[6,256,128]{1,2,0:T(8,128)S(1)} fusion(f32[256,96,1]{0,1,2:T(8,128)S(1)} %convolution_bitcast_fusion.4, f32[3,96,128]{2,1,0:T(8,128)} %bitcast.75, f32[3,96,128]{2,1,0:T(8,128)} %bitcast.65), kind=kOutput, calls=%fused_computation.1 | convolution fusion | flops 226566144 | bytes 1179648 | tf_op jit(solution)/shard_map/sb,rba->rsa/dot_general | solution.py:271
  5.8 0.1 pad_maximum_fusion
  5.9 0.3 copy.102
  6.2 0.0 copy-start.1
  6.2 1.1 copy.103
  7.3 0.0 copy-start.6
  7.3 13.1 %all-to-all-start = ((f32[7,64,4,128]{3,2,0,1:T(4,128)}), f32[7,64,4,128]{3,2,0,1:T(4,128)S(1)}, u32[]{:S(2)}, u32[]{:S(2)}) async-start(f32[7,64,4,128]{3,2,0,1:T(4,128)} %copy.103), calls=%async_computation | async-start | bytes 1835008 | tf_op jit(solution)/shard_map/all_to_all | solution.py:317
  20.4 0.0 copy-done.1
  20.4 0.0 copy-start.7
  20.5 1.3 %collective-permute-start.1 = (f32[3,2,3,128]{3,1,2,0:T(2,128)S(1)}, f32[3,2,3,128]{3,1,2,0:T(2,128)S(1)}, u32[]{:S(2)}, u32[]{:S(2)}) collective-permute-start(f32[3,2,3,128]{3,1,2,0:T(2,128)S(1)} %bitcast.91), channel_id=1, source_target_pairs={{1,0},{2,1},{3,2},{5,4},{6,5},{7,6},{9,8},{10,9},{11,10},{13,12},{... | collective-permute-start | bytes 27656 | tf_op jit(solution)/shard_map/ppermute | solution.py:21
  21.8 0.2 copy.105
  21.9 1.3 %collective-permute-start = (f32[3,2,3,16]{3,1,2,0:T(2,128)S(1)}, f32[3,2,3,16]{3,1,2,0:T(2,128)S(1)}, u32[]{:S(2)}, u32[]{:S(2)}) collective-permute-start(f32[3,2,3,16]{3,1,2,0:T(2,128)S(1)} %bitcast.86), channel_id=1, source_target_pairs={{4,0},{8,4},{12,8},{16,12},{20,16},{24,20},{28,24},{5,1},{9,5},{13... | collective-permute-start | bytes 3464 | tf_op jit(solution)/shard_map/ppermute | solution.py:21
  23.3 0.0 copy-done.6
  23.3 0.1 slice_multiply_fusion.1
  23.4 0.1 slice.128
  23.5 18.2 %collective-permute-done = f32[3,2,3,16]{3,1,2,0:T(2,128)S(1)} collective-permute-done((f32[3,2,3,16]{3,1,2,0:T(2,128)S(1)}, f32[3,2,3,16]{3,1,2,0:T(2,128)S(1)}, u32[]{:S(2)}, u32[]{:S(2)}) %collective-permute-start) | collective-permute-done | bytes 1184 | tf_op jit(solution)/shard_map/ppermute | solution.py:21
  41.7 0.1 concatenate.54
  41.8 0.1 maximum_dynamic-update-slice_fusion
  41.9 0.0 collective-permute-done.1
  42.0 0.0 copy-done.7
  42.0 3.7 %all-to-all-done = f32[7,64,4,128]{3,2,0,1:T(4,128)S(1)} async-done(((f32[7,64,4,128]{3,2,0,1:T(4,128)}), f32[7,64,4,128]{3,2,0,1:T(4,128)S(1)}, u32[]{:S(2)}, u32[]{:S(2)}) %all-to-all-start) | async-done | bytes 917536 | tf_op jit(solution)/shard_map/all_to_all | solution.py:317
  45.7 0.2 copy.104
  45.9 0.0 copy-start
  45.9 0.1 fusion.4
  46.0 2.0 %convolution_bitcast_fusion.s_ref = f32[12,256,128]{2,1,0:T(8,128)} fusion(f32[12,96,128]{2,1,0:T(8,128)S(1)} %constant_dynamic-update-slice_fusion, s32[256]{0:T(256)S(1)} %broadcast_clamp_fusion), kind=kOutput, calls=%fused_computation | convolution fusion | flops 453009408 | bytes 2163712 | tf_op jit(solution)/shard_map/sb,rba->rsa/dot_general | solution.py:271
  48.0 0.0 copy-done
  48.0 29.1 %shard_map.94 = (f32[3,256,128]{2,1,0:T(8,128)}, f32[3,256,128]{2,1,0:T(8,128)}, f32[11,256,128]{2,1,0:T(8,128)}) custom-call(f32[7,256,128]{2,1,0:T(8,128)} %bitcast.63, f32[12,256,128]{2,1,0:T(8,128)} %convolution_bitcast_fusion.s_ref, f32[7,256,128]{2,1,0:T(8,128)} %bitcast.64), custom_call_target="tpu_custom_call" | custom-call | tf_op jit(solution)/shard_map/pallas_call | solution.py:203
  77.2 1.2 %pad_maximum_fusion.1 = f32[6,256,128]{2,1,0:T(8,128)S(1)} fusion(f32[3,256,128]{2,1,0:T(8,128)} %get-tuple-element.43, f32[3,256,128]{2,1,0:T(8,128)} %get-tuple-element.42), kind=kLoop, calls=%fused_computation.6 | loop fusion | flops 196608 | bytes 1572864 | tf_op jit(solution)/shard_map/concatenate | solution.py:341
  78.3 0.0 copy-start.2
  78.3 1.0 copy.111
  79.4 6.9 %all-to-all-start.1 = ((f32[6,64,4,128]{3,2,0,1:T(4,128)}), f32[6,64,4,128]{3,2,0,1:T(4,128)S(1)}, u32[]{:S(2)}, u32[]{:S(2)}) async-start(f32[6,64,4,128]{3,2,0,1:T(4,128)} %copy.111), calls=%async_computation.1 | async-start | bytes 1572864 | tf_op jit(solution)/shard_map/all_to_all | solution.py:340
  86.3 0.0 copy-done.2
  86.3 0.6 convolution_bitcast_fusion.2
  87.0 3.2 %collective-permute-start.3 = (f32[3,2,3,128]{3,1,2,0:T(2,128)S(1)}, f32[3,2,3,128]{3,1,2,0:T(2,128)S(1)}, u32[]{:S(2)}, u32[]{:S(2)}) collective-permute-start(f32[3,2,3,128]{3,1,2,0:T(2,128)S(1)} %bitcast.90), channel_id=1, source_target_pairs={{0,1},{1,2},{2,3},{4,5},{5,6},{6,7},{8,9},{9,10},{10,11},{12,13},{... | collective-permute-start | bytes 27656 | tf_op jit(solution)/shard_map/ppermute | solution.py:21
  90.2 0.1 split.56
  90.3 0.2 copy.113
  90.5 3.3 %collective-permute-start.2 = (f32[3,2,3,16]{3,1,2,0:T(2,128)S(1)}, f32[3,2,3,16]{3,1,2,0:T(2,128)S(1)}, u32[]{:S(2)}, u32[]{:S(2)}) collective-permute-start(f32[3,2,3,16]{3,1,2,0:T(2,128)S(1)} %bitcast.87), channel_id=1, source_target_pairs={{0,4},{4,8},{8,12},{12,16},{16,20},{20,24},{24,28},{1,5},{5,9},{9,... | collective-permute-start | bytes 3464 | tf_op jit(solution)/shard_map/ppermute | solution.py:21
  93.8 0.1 broadcast_multiply_fusion
  93.8 0.6 pad_add_fusion
  94.5 6.6 %collective-permute-done.2 = f32[3,2,3,16]{3,1,2,0:T(2,128)S(1)} collective-permute-done((f32[3,2,3,16]{3,1,2,0:T(2,128)S(1)}, f32[3,2,3,16]{3,1,2,0:T(2,128)S(1)}, u32[]{:S(2)}, u32[]{:S(2)}) %collective-permute-start.2) | collective-permute-done | bytes 1184 | tf_op jit(solution)/shard_map/ppermute | solution.py:21
  101.1 0.2 copy.114
  101.2 8.1 %all-to-all-done.1 = f32[6,64,4,128]{3,2,0,1:T(4,128)S(1)} async-done(((f32[6,64,4,128]{3,2,0,1:T(4,128)}), f32[6,64,4,128]{3,2,0,1:T(4,128)S(1)}, u32[]{:S(2)}, u32[]{:S(2)}) %all-to-all-start.1) | async-done | bytes 786464 | tf_op jit(solution)/shard_map/all_to_all | solution.py:340
  109.3 0.1 copy.112
  109.5 0.0 copy-start.4
  109.5 0.6 convolution_bitcast_fusion.3
  110.1 0.2 copy-done.4
  110.4 0.1 add_add_fusion
  110.5 0.0 copy-start.5
  110.5 0.2 scatter-add.11
  110.7 0.0 collective-permute-done.3
  110.7 0.1 scatter-add.14
  110.8 0.4 copy-done.5
  111.2 0.0 copy-start.3
  111.2 0.7 copy-done.3
  (24 shorter events, 0.3 us)
Async XLA Ops:
  6.2 14.2 %copy-start.1 = (f32[3,2,3,16,128]{4,3,2,1,0:T(8,128)S(1)}, f32[3,2,3,16,128]{4,3,2,1,0:T(8,128)}, u32[]{:S(2)}) copy-start(f32[3,2,3,16,128]{4,3,2,1,0:T(8,128)} %param.13) | copy-start | bytes 442372
  7.3 16.0 %copy-start.6 = (f32[2,2,3,16,128]{4,3,2,1,0:T(8,128)S(1)}, f32[2,2,3,16,128]{4,3,2,1,0:T(8,128)}, u32[]{:S(2)}) copy-start(f32[2,2,3,16,128]{4,3,2,1,0:T(8,128)} %param.14) | copy-start | bytes 294916
  7.3 38.4 %all-to-all-start = ((f32[7,64,4,128]{3,2,0,1:T(4,128)}), f32[7,64,4,128]{3,2,0,1:T(4,128)S(1)}, u32[]{:S(2)}, u32[]{:S(2)}) async-start(f32[7,64,4,128]{3,2,0,1:T(4,128)} %copy.103), calls=%async_computation | async-start | bytes 1835008 | tf_op jit(solution)/shard_map/all_to_all | solution.py:317
  20.4 21.6 %copy-start.7 = (f32[2,3,16,128]{3,2,1,0:T(8,128)S(1)}, f32[2,3,16,128]{3,2,1,0:T(8,128)}, u32[]{:S(2)}) copy-start(f32[2,3,16,128]{3,2,1,0:T(8,128)} %param.15) | copy-start | bytes 147460
  20.5 21.5 %collective-permute-start.1 = (f32[3,2,3,128]{3,1,2,0:T(2,128)S(1)}, f32[3,2,3,128]{3,1,2,0:T(2,128)S(1)}, u32[]{:S(2)}, u32[]{:S(2)}) collective-permute-start(f32[3,2,3,128]{3,1,2,0:T(2,128)S(1)} %bitcast.91), channel_id=1, source_target_pairs={{1,0},{2,1},{3,2},{5,4},{6,5},{7,6},{9,8},{10,9},{11,10},{13,12},{... | collective-permute-start | bytes 27656 | tf_op jit(solution)/shard_map/ppermute | solution.py:21
  21.9 19.7 %collective-permute-start = (f32[3,2,3,16]{3,1,2,0:T(2,128)S(1)}, f32[3,2,3,16]{3,1,2,0:T(2,128)S(1)}, u32[]{:S(2)}, u32[]{:S(2)}) collective-permute-start(f32[3,2,3,16]{3,1,2,0:T(2,128)S(1)} %bitcast.86), channel_id=1, source_target_pairs={{4,0},{8,4},{12,8},{16,12},{20,16},{24,20},{28,24},{5,1},{9,5},{13... | collective-permute-start | bytes 3464 | tf_op jit(solution)/shard_map/ppermute | solution.py:21
  45.9 2.2 %copy-start = (f32[7,64,4,128]{3,2,1,0:T(4,128)}, f32[7,64,4,128]{3,2,1,0:T(4,128)S(1)}, u32[]{:S(2)}) copy-start(f32[7,64,4,128]{3,2,1,0:T(4,128)S(1)} %copy.104) | copy-start | bytes 2752516
  78.3 8.0 %copy-start.2 = (f32[11,256,128]{2,1,0:T(8,128)S(1)}, f32[11,256,128]{2,1,0:T(8,128)}, u32[]{:S(2)}) copy-start(f32[11,256,128]{2,1,0:T(8,128)} %get-tuple-element.44) | copy-start | bytes 4325380
  79.4 29.9 %all-to-all-start.1 = ((f32[6,64,4,128]{3,2,0,1:T(4,128)}), f32[6,64,4,128]{3,2,0,1:T(4,128)S(1)}, u32[]{:S(2)}, u32[]{:S(2)}) async-start(f32[6,64,4,128]{3,2,0,1:T(4,128)} %copy.111), calls=%async_computation.1 | async-start | bytes 1572864 | tf_op jit(solution)/shard_map/all_to_all | solution.py:340
  87.0 23.7 %collective-permute-start.3 = (f32[3,2,3,128]{3,1,2,0:T(2,128)S(1)}, f32[3,2,3,128]{3,1,2,0:T(2,128)S(1)}, u32[]{:S(2)}, u32[]{:S(2)}) collective-permute-start(f32[3,2,3,128]{3,1,2,0:T(2,128)S(1)} %bitcast.90), channel_id=1, source_target_pairs={{0,1},{1,2},{2,3},{4,5},{5,6},{6,7},{8,9},{9,10},{10,11},{12,13},{... | collective-permute-start | bytes 27656 | tf_op jit(solution)/shard_map/ppermute | solution.py:21
  90.5 10.6 %collective-permute-start.2 = (f32[3,2,3,16]{3,1,2,0:T(2,128)S(1)}, f32[3,2,3,16]{3,1,2,0:T(2,128)S(1)}, u32[]{:S(2)}, u32[]{:S(2)}) collective-permute-start(f32[3,2,3,16]{3,1,2,0:T(2,128)S(1)} %bitcast.87), channel_id=1, source_target_pairs={{0,4},{4,8},{8,12},{12,16},{16,20},{20,24},{24,28},{1,5},{5,9},{9,... | collective-permute-start | bytes 3464 | tf_op jit(solution)/shard_map/ppermute | solution.py:21
  109.5 0.9 copy-start.4
  110.5 0.7 copy-start.5
  111.2 0.7 copy-start.3
